TPU v7x, 256 devices: a whole 4x4x8 slice. The times are simulated.
256 devices in a mesh: blk: 64 (over y, x_lo, z), team: 4 (over x_hi, core).
Axes of the slice: x: 4 (x_hi: 2, x_lo: 2; x = x_hi * 2 + x_lo), y: 4, z: 8, core: 2. Of those that a mesh axis runs over, the one named last changes fastest.
Arguments:
- loadings: bfloat16 [64, 98304], P(None, ('blk', 'team')), may hold values from -6 to 6
- scales: bfloat16 [64, 768], P(None, ('blk', 'team')), may hold values from 0.25 to 4
- cov: bfloat16 [16384, 16, 4, 1536], P('blk', None, 'team'), may hold values from -0.01953125 to 0.01953125
Outputs:
- product: float32 [64, 16384], P(None, 'blk')
All inputs are finite; a program needn't handle non-finite values.
Results may differ from a plain program's by a relative error of at most 0.0028.
Values may be sent and summed in bfloat16 or wider, within the bound.
No kernel may reach another device: no remote copies, remote signals or barrier semaphores. Data moves between devices by JAX's collectives and lax.ppermute only.
A program may use at most 128 MiB of HBM per device.

v0:
```python
import jax
import jax.numpy as jnp
import numpy as np
from jax import lax
from jax.sharding import Mesh
from jax.sharding import PartitionSpec as P

SUB = (("y", 4), ("xl", 2), ("z", 8), ("xh", 2), ("core", 2))
BLK = ("y", "xl", "z")
TEAM = ("xh", "core")


def shifted(x, axis, by):
    n = lax.axis_size(axis)
    return lax.ppermute(x, axis, [(i, (i + by) % n) for i in range(n)])


def ring_gather(x, axis):
    n = lax.axis_size(axis)
    fwd, bwd = x, x
    got = {0: x}
    for s in range(1, n // 2 + 1):
        fwd = shifted(fwd, axis, 1)
        got[-s] = fwd
        if s <= (n - 1) // 2:
            bwd = shifted(bwd, axis, -1)
            got[s] = bwd
    rel = [got[k] if k in got else got[k - n] for k in range(n)]
    rel = jnp.stack(rel + rel)
    me = lax.axis_index(axis)
    return lax.dynamic_slice_in_dim(rel, (n - me) % n, n, 0)


def team_sum(x):
    x = x + shifted(x, "core", 1)
    return x + shifted(x, "xh", 1)


def per_device(loadings, scales, cov):
    n_loads, width = loadings.shape
    groups = scales.shape[1]
    scaled = (
        loadings.astype(jnp.float32).reshape(n_loads, groups, width // groups)
        * scales.astype(jnp.float32)[:, :, None]
    ).reshape(n_loads, width).astype(jnp.bfloat16)
    nz = lax.axis_size("z")
    nt = lax.axis_size("xh") * lax.axis_size("core")
    pairs = []
    for z in range(nz):
        for t in range(nt):
            zh, d = divmod(z, nt)
            pairs.append((z * nt + t, (zh * nt + t) * nt + d))
    moved = lax.ppermute(scaled, ("z", "xh", "core"), pairs)
    s1 = ring_gather(moved, "xl")
    s2 = ring_gather(s1, "z")
    nx = s1.shape[0]
    s2 = s2.reshape(nz // nt, nt, nx, n_loads, width)
    own = jnp.transpose(s2, (3, 2, 0, 1, 4)).reshape(n_loads, nx * nz // nt, nt * width)
    per_y = own.shape[1]
    cov_local = cov[:, :, 0, :]
    ny = lax.axis_size("y")
    me = lax.axis_index("y")

    def term(block, y_from):
        def stop_range(j):
            def run(block, cov_local):
                return lax.dot_general(
                    block,
                    cov_local[:, j * per_y : (j + 1) * per_y, :],
                    (((1, 2), (1, 2)), ((), ())),
                    preferred_element_type=jnp.float32,
                )

            return run

        return lax.switch(y_from % ny, [stop_range(j) for j in range(ny)], block, cov_local)

    part = term(own, me)
    fwd, bwd = own, own
    for s in range(1, ny // 2 + 1):
        fwd = shifted(fwd, "y", 1)
        part = part + term(fwd, me - s)
        if s <= (ny - 1) // 2:
            bwd = shifted(bwd, "y", -1)
            part = part + term(bwd, me + s)
    return team_sum(part)


def solution(mesh):
    sizes = tuple(s for _, s in SUB)
    assert mesh.devices.size == int(np.prod(sizes))
    fine = Mesh(mesh.devices.reshape(sizes), tuple(n for n, _ in SUB))
    placed = (P(None, BLK + TEAM), P(None, BLK + TEAM), P(BLK, None, TEAM, None))
    return jax.shard_map(
        per_device, mesh=fine, in_specs=placed, out_specs=P(None, BLK), check_vma=False
    )
```

profile of v0, /device:TPU:1, one launch (start us, length us, event | category | flops | bytes accessed | tf_op | source)
XLA Modules:
  0.0 101.1 jit_solution(7460392847601814985)
XLA Ops:
  1.7 4.9 %collective-permute-start = (bf16[64,384]{1,0:T(8,128)(2,1)S(1)}, bf16[64,384]{1,0:T(8,128)(2,1)S(1)}, u32[]{:S(2)}, u32[]{:S(2)}) collective-permute-start(bf16[64,384]{1,0:T(8,128)(2,1)S(1)} %fusion.83), channel_id=1, source_target_pairs={{0,0},{1,4},{2,8},{3,12},{4,1},{5,5},{6,9},{7,13},{8,2},{9,6},{10,... | collective-permute-start | bytes 147464 | tf_op jit(solution)/shard_map/ppermute | solution.py:53
  6.7 1.8 %collective-permute-done = bf16[64,384]{1,0:T(8,128)(2,1)S(1)} collective-permute-done((bf16[64,384]{1,0:T(8,128)(2,1)S(1)}, bf16[64,384]{1,0:T(8,128)(2,1)S(1)}, u32[]{:S(2)}, u32[]{:S(2)}) %collective-permute-start) | collective-permute-done | bytes 49184 | tf_op jit(solution)/shard_map/ppermute | solution.py:53
  9.6 1.7 %collective-permute-done.1 = bf16[64,384]{1,0:T(8,128)(2,1)S(1)} collective-permute-done((bf16[64,384]{1,0:T(8,128)(2,1)S(1)}, bf16[64,384]{1,0:T(8,128)(2,1)S(1)}, u32[]{:S(2)}, u32[]{:S(2)}) %collective-permute-start.1) | collective-permute-done | bytes 49184 | tf_op jit(solution)/shard_map/ppermute | solution.py:15
  11.4 8.3 %collective-permute-start.2 = (bf16[2,64,384]{2,1,0:T(8,128)(2,1)S(1)}, bf16[2,64,384]{2,1,0:T(8,128)(2,1)S(1)}, u32[]{:S(2)}, u32[]{:S(2)}) collective-permute-start(bf16[2,64,384]{2,1,0:T(8,128)(2,1)S(1)} %get-tuple-element.122), channel_id=1, source_target_pairs={{0,28},{4,0},{8,4},{12,8},{16,12},{20,16},{24,20},{28,24},{1,29},{... | collective-permute-start | bytes 294920 | tf_op jit(solution)/shard_map/ppermute | solution.py:15
  19.8 1.6 %collective-permute-done.2 = bf16[2,64,384]{2,1,0:T(8,128)(2,1)S(1)} collective-permute-done((bf16[2,64,384]{2,1,0:T(8,128)(2,1)S(1)}, bf16[2,64,384]{2,1,0:T(8,128)(2,1)S(1)}, u32[]{:S(2)}, u32[]{:S(2)}) %collective-permute-start.2) | collective-permute-done | bytes 98336 | tf_op jit(solution)/shard_map/ppermute | solution.py:15
  21.4 3.0 %collective-permute-start.3 = (bf16[2,64,384]{2,1,0:T(8,128)(2,1)S(1)}, bf16[2,64,384]{2,1,0:T(8,128)(2,1)S(1)}, u32[]{:S(2)}, u32[]{:S(2)}) collective-permute-start(bf16[2,64,384]{2,1,0:T(8,128)(2,1)S(1)} %collective-permute-done.2), channel_id=1, source_target_pairs={{0,28},{4,0},{8,4},{12,8},{16,12},{20,16},{24,20},{28,24},{1,29},{... | collective-permute-start | bytes 294920 | tf_op jit(solution)/shard_map/ppermute | solution.py:15
  24.5 1.7 %collective-permute-done.3 = bf16[2,64,384]{2,1,0:T(8,128)(2,1)S(1)} collective-permute-done((bf16[2,64,384]{2,1,0:T(8,128)(2,1)S(1)}, bf16[2,64,384]{2,1,0:T(8,128)(2,1)S(1)}, u32[]{:S(2)}, u32[]{:S(2)}) %collective-permute-start.3) | collective-permute-done | bytes 98336 | tf_op jit(solution)/shard_map/ppermute | solution.py:15
  26.1 3.1 %collective-permute-start.4 = (bf16[2,64,384]{2,1,0:T(8,128)(2,1)S(1)}, bf16[2,64,384]{2,1,0:T(8,128)(2,1)S(1)}, u32[]{:S(2)}, u32[]{:S(2)}) collective-permute-start(bf16[2,64,384]{2,1,0:T(8,128)(2,1)S(1)} %collective-permute-done.3), channel_id=1, source_target_pairs={{0,28},{4,0},{8,4},{12,8},{16,12},{20,16},{24,20},{28,24},{1,29},{... | collective-permute-start | bytes 294920 | tf_op jit(solution)/shard_map/ppermute | solution.py:15
  29.6 5.5 %collective-permute-done.7 = bf16[2,64,384]{2,1,0:T(8,128)(2,1)S(1)} collective-permute-done((bf16[2,64,384]{2,1,0:T(8,128)(2,1)S(1)}, bf16[2,64,384]{2,1,0:T(8,128)(2,1)S(1)}, u32[]{:S(2)}, u32[]{:S(2)}) %collective-permute-start.7) | collective-permute-done | bytes 98336 | tf_op jit(solution)/shard_map/ppermute | solution.py:15
  35.1 4.7 %collective-permute-done.8 = bf16[2,64,384]{2,1,0:T(8,128)(2,1)S(1)} collective-permute-done((bf16[2,64,384]{2,1,0:T(8,128)(2,1)S(1)}, bf16[2,64,384]{2,1,0:T(8,128)(2,1)S(1)}, u32[]{:S(2)}, u32[]{:S(2)}) %collective-permute-start.8) | collective-permute-done | bytes 98336 | tf_op jit(solution)/shard_map/ppermute | solution.py:15
  42.0 1.3 %collective-permute-start.9 = (bf16[64,4,1536]{2,0,1:T(8,128)(2,1)}, bf16[64,4,1536]{2,0,1:T(8,128)(2,1)}, u32[]{:S(2)}, u32[]{:S(2)}) collective-permute-start(bf16[64,4,1536]{2,0,1:T(8,128)(2,1)} %reshape.11), channel_id=1, source_target_pairs={{0,64},{64,128},{128,192},{192,0},{1,65},{65,129},{129,193},{193,1... | collective-permute-start | bytes 2359304 | tf_op jit(solution)/shard_map/ppermute | solution.py:15
  43.3 1.4 %collective-permute-start.10 = (bf16[64,4,1536]{2,0,1:T(8,128)(2,1)}, bf16[64,4,1536]{2,0,1:T(8,128)(2,1)S(1)}, u32[]{:S(2)}, u32[]{:S(2)}) collective-permute-start(bf16[64,4,1536]{2,0,1:T(8,128)(2,1)} %reshape.11), channel_id=1, source_target_pairs={{0,192},{64,0},{128,64},{192,128},{1,193},{65,1},{129,65},{193,129... | collective-permute-start | bytes 2359304 | tf_op jit(solution)/shard_map/ppermute | solution.py:15
  44.7 10.1 %collective-permute-done.9 = bf16[64,4,1536]{2,0,1:T(8,128)(2,1)} collective-permute-done((bf16[64,4,1536]{2,0,1:T(8,128)(2,1)}, bf16[64,4,1536]{2,0,1:T(8,128)(2,1)}, u32[]{:S(2)}, u32[]{:S(2)}) %collective-permute-start.9) | collective-permute-done | bytes 786464 | tf_op jit(solution)/shard_map/ppermute | solution.py:15
  54.8 13.0 %copy.14 = bf16[256,16,1,1536]{3,0,1,2:T(8,128)(2,1)} copy(bf16[256,16,1,1536]{3,1,2,0:T(8,128)(2,1)} %param.21) | data formatting | bytes 25165824 | tf_op args[2]
  67.8 3.4 %conditional.4 = (f32[64,256]{1,0:T(8,128)S(1)}) conditional(s32[]{:T(128)} %clamp.12, (bf16[256,16,1536]{2,0,1:T(8,128)(2,1)}, bf16[64,4,1536]{2,0,1:T(8,128)(2,1)}) %tuple.74, (bf16[256,16,1536]{2,0,1:T(8,128)(2,1)}, bf16[64,4,1536]{2,0,1:T(8,128)(2,1)}) %tuple.75, (bf16[256,16,1536]{2,0,1:T(8,128)(2,1)}, ...), branch_computations={%region_0.1_spmd, %region_1.2_spmd, %region_2.3_spmd, %region_3.4_... | conditional | flops 201326592 | bytes 3997704 | solution.py:76
  67.8 3.2 %fusion.2 = f32[64,256]{1,0:T(8,128)S(1)} fusion(bf16[64,4,1536]{2,0,1:T(8,128)(2,1)} %get-tuple-element.78, bf16[256,16,1536]{2,0,1:T(8,128)(2,1)} %get-tuple-element.79), kind=kOutput, calls=%fused_computation.2 | convolution fusion | flops 201326592 | bytes 3997696 | tf_op jit(solution)/shard_map/cond/branch_0_fun/dot_general | solution.py:67
  71.2 3.2 %conditional.5 = (f32[64,256]{1,0:T(8,128)S(1)}) conditional(s32[]{:T(128)} %clamp.13, (bf16[256,16,1536]{2,0,1:T(8,128)(2,1)}, bf16[64,4,1536]{2,0,1:T(8,128)(2,1)}) %tuple.78, (bf16[256,16,1536]{2,0,1:T(8,128)(2,1)}, bf16[64,4,1536]{2,0,1:T(8,128)(2,1)}) %tuple.79, (bf16[256,16,1536]{2,0,1:T(8,128)(2,1)}, ...), branch_computations={%region_4.5_spmd, %region_5.6_spmd, %region_6.7_spmd, %region_7.8_... | conditional | flops 201326592 | bytes 3997704 | solution.py:76
  71.2 3.2 %fusion.37 = f32[64,256]{1,0:T(8,128)S(1)} fusion(bf16[64,4,1536]{2,0,1:T(8,128)(2,1)} %get-tuple-element.103, bf16[256,16,1536]{2,0,1:T(8,128)(2,1)} %get-tuple-element.104), kind=kOutput, calls=%fused_computation.23 | convolution fusion | flops 201326592 | bytes 3997696 | tf_op jit(solution)/shard_map/cond/branch_3_fun/dot_general | solution.py:67
  74.4 3.0 %conditional.6 = (f32[64,256]{1,0:T(8,128)S(1)}) conditional(s32[]{:T(128)} %clamp.14, (bf16[256,16,1536]{2,0,1:T(8,128)(2,1)}, bf16[64,4,1536]{2,0,1:T(8,128)(2,1)S(1)}) %tuple.82, (bf16[256,16,1536]{2,0,1:T(8,128)(2,1)}, bf16[64,4,1536]{2,0,1:T(8,128)(2,1)S(1)}) %tuple.83, (bf16[256,16,1536]{2,0,1:T(8,128)(2,1)}, ...), branch_computations={%region_8.9_spmd, %region_9.10_spmd, %region_10.11_spmd, %region_1... | conditional | flops 201326592 | bytes 3997704 | solution.py:76
  74.5 3.0 %fusion.47 = f32[64,256]{1,0:T(8,128)S(1)} fusion(bf16[64,4,1536]{2,0,1:T(8,128)(2,1)S(1)} %get-tuple-element.107, bf16[256,16,1536]{2,0,1:T(8,128)(2,1)} %get-tuple-element.108), kind=kOutput, calls=%fused_computation.29 | convolution fusion | flops 201326592 | bytes 3997696 | tf_op jit(solution)/shard_map/cond/branch_1_fun/dot_general | solution.py:67
  77.4 3.0 %conditional.7 = (f32[64,256]{1,0:T(8,128)S(1)}) conditional(s32[]{:T(128)} %clamp.15, (bf16[256,16,1536]{2,0,1:T(8,128)(2,1)}, bf16[64,4,1536]{2,0,1:T(8,128)(2,1)S(1)}) %tuple.86, (bf16[256,16,1536]{2,0,1:T(8,128)(2,1)}, bf16[64,4,1536]{2,0,1:T(8,128)(2,1)S(1)}) %tuple.87, (bf16[256,16,1536]{2,0,1:T(8,128)(2,1)}, ...), branch_computations={%region_12.13_spmd, %region_13.14_spmd, %region_14.15_spmd, %regio... | conditional | flops 201326592 | bytes 3997704 | solution.py:76
  77.5 3.0 %fusion.72 = f32[64,256]{1,0:T(8,128)S(1)} fusion(bf16[64,4,1536]{2,0,1:T(8,128)(2,1)S(1)} %get-tuple-element.117, bf16[256,16,1536]{2,0,1:T(8,128)(2,1)} %get-tuple-element.118), kind=kOutput, calls=%fused_computation.44 | convolution fusion | flops 201326592 | bytes 3997696 | tf_op jit(solution)/shard_map/cond/branch_2_fun/dot_general | solution.py:67
  80.5 14.3 %collective-permute-start.12 = (f32[64,256]{1,0:T(8,128)S(1)}, f32[64,256]{1,0:T(8,128)S(1)}, u32[]{:S(2)}, u32[]{:S(2)}) collective-permute-start(f32[64,256]{1,0:T(8,128)S(1)} %add_add_fusion), channel_id=1, source_target_pairs={{0,1},{1,0},{2,3},{3,2},{4,5},{5,4},{6,7},{7,6},{8,9},{9,8},{10,11... | collective-permute-start | bytes 196616 | tf_op jit(solution)/shard_map/ppermute | solution.py:15
  95.8 4.6 %collective-permute-done.13 = f32[64,256]{1,0:T(8,128)S(1)} collective-permute-done((f32[64,256]{1,0:T(8,128)S(1)}, f32[64,256]{1,0:T(8,128)S(1)}, u32[]{:S(2)}, u32[]{:S(2)}) %collective-permute-start.13) | collective-permute-done | bytes 65568 | tf_op jit(solution)/shard_map/ppermute | solution.py:15
  (38 shorter events, 7.1 us)
Async XLA Ops:
  1.7 6.7 %collective-permute-start = (bf16[64,384]{1,0:T(8,128)(2,1)S(1)}, bf16[64,384]{1,0:T(8,128)(2,1)S(1)}, u32[]{:S(2)}, u32[]{:S(2)}) collective-permute-start(bf16[64,384]{1,0:T(8,128)(2,1)S(1)} %fusion.83), channel_id=1, source_target_pairs={{0,0},{1,4},{2,8},{3,12},{4,1},{5,5},{6,9},{7,13},{8,2},{9,6},{10,... | collective-permute-start | bytes 147464 | tf_op jit(solution)/shard_map/ppermute | solution.py:53
  8.4 2.9 %collective-permute-start.1 = (bf16[64,384]{1,0:T(8,128)(2,1)S(1)}, bf16[64,384]{1,0:T(8,128)(2,1)S(1)}, u32[]{:S(2)}, u32[]{:S(2)}) collective-permute-start(bf16[64,384]{1,0:T(8,128)(2,1)S(1)} %collective-permute-done), channel_id=1, source_target_pairs={{0,32},{32,0},{1,33},{33,1},{2,34},{34,2},{3,35},{35,3},{4,36},{36... | collective-permute-start | bytes 147464 | tf_op jit(solution)/shard_map/ppermute | solution.py:15
  11.4 10.0 %collective-permute-start.2 = (bf16[2,64,384]{2,1,0:T(8,128)(2,1)S(1)}, bf16[2,64,384]{2,1,0:T(8,128)(2,1)S(1)}, u32[]{:S(2)}, u32[]{:S(2)}) collective-permute-start(bf16[2,64,384]{2,1,0:T(8,128)(2,1)S(1)} %get-tuple-element.122), channel_id=1, source_target_pairs={{0,28},{4,0},{8,4},{12,8},{16,12},{20,16},{24,20},{28,24},{1,29},{... | collective-permute-start | bytes 294920 | tf_op jit(solution)/shard_map/ppermute | solution.py:15
  19.8 4.7 %collective-permute-start.5 = (bf16[2,64,384]{2,1,0:T(8,128)(2,1)S(1)}, bf16[2,64,384]{2,1,0:T(8,128)(2,1)S(1)}, u32[]{:S(2)}, u32[]{:S(2)}) collective-permute-start(bf16[2,64,384]{2,1,0:T(8,128)(2,1)S(1)} %get-tuple-element.122), channel_id=1, source_target_pairs={{0,4},{4,8},{8,12},{12,16},{16,20},{20,24},{24,28},{28,0},{1,5},{5... | collective-permute-start | bytes 294920 | tf_op jit(solution)/shard_map/ppermute | solution.py:15
  21.4 4.7 %collective-permute-start.3 = (bf16[2,64,384]{2,1,0:T(8,128)(2,1)S(1)}, bf16[2,64,384]{2,1,0:T(8,128)(2,1)S(1)}, u32[]{:S(2)}, u32[]{:S(2)}) collective-permute-start(bf16[2,64,384]{2,1,0:T(8,128)(2,1)S(1)} %collective-permute-done.2), channel_id=1, source_target_pairs={{0,28},{4,0},{8,4},{12,8},{16,12},{20,16},{24,20},{28,24},{1,29},{... | collective-permute-start | bytes 294920 | tf_op jit(solution)/shard_map/ppermute | solution.py:15
  24.4 5.1 %collective-permute-start.6 = (bf16[2,64,384]{2,1,0:T(8,128)(2,1)S(1)}, bf16[2,64,384]{2,1,0:T(8,128)(2,1)S(1)}, u32[]{:S(2)}, u32[]{:S(2)}) collective-permute-start(bf16[2,64,384]{2,1,0:T(8,128)(2,1)S(1)} %collective-permute-done.5), channel_id=1, source_target_pairs={{0,4},{4,8},{8,12},{12,16},{16,20},{20,24},{24,28},{28,0},{1,5},{5... | collective-permute-start | bytes 294920 | tf_op jit(solution)/shard_map/ppermute | solution.py:15
  26.1 9.0 %collective-permute-start.4 = (bf16[2,64,384]{2,1,0:T(8,128)(2,1)S(1)}, bf16[2,64,384]{2,1,0:T(8,128)(2,1)S(1)}, u32[]{:S(2)}, u32[]{:S(2)}) collective-permute-start(bf16[2,64,384]{2,1,0:T(8,128)(2,1)S(1)} %collective-permute-done.3), channel_id=1, source_target_pairs={{0,28},{4,0},{8,4},{12,8},{16,12},{20,16},{24,20},{28,24},{1,29},{... | collective-permute-start | bytes 294920 | tf_op jit(solution)/shard_map/ppermute | solution.py:15
  29.5 5.6 %collective-permute-start.7 = (bf16[2,64,384]{2,1,0:T(8,128)(2,1)S(1)}, bf16[2,64,384]{2,1,0:T(8,128)(2,1)S(1)}, u32[]{:S(2)}, u32[]{:S(2)}) collective-permute-start(bf16[2,64,384]{2,1,0:T(8,128)(2,1)S(1)} %collective-permute-done.6), channel_id=1, source_target_pairs={{0,4},{4,8},{8,12},{12,16},{16,20},{20,24},{24,28},{28,0},{1,5},{5... | collective-permute-start | bytes 294920 | tf_op jit(solution)/shard_map/ppermute | solution.py:15
  35.1 4.7 %collective-permute-start.8 = (bf16[2,64,384]{2,1,0:T(8,128)(2,1)S(1)}, bf16[2,64,384]{2,1,0:T(8,128)(2,1)S(1)}, u32[]{:S(2)}, u32[]{:S(2)}) collective-permute-start(bf16[2,64,384]{2,1,0:T(8,128)(2,1)S(1)} %collective-permute-done.7), channel_id=1, source_target_pairs={{0,4},{4,8},{8,12},{12,16},{16,20},{20,24},{24,28},{28,0},{1,5},{5... | collective-permute-start | bytes 294920 | tf_op jit(solution)/shard_map/ppermute | solution.py:15
  42.0 12.8 %collective-permute-start.9 = (bf16[64,4,1536]{2,0,1:T(8,128)(2,1)}, bf16[64,4,1536]{2,0,1:T(8,128)(2,1)}, u32[]{:S(2)}, u32[]{:S(2)}) collective-permute-start(bf16[64,4,1536]{2,0,1:T(8,128)(2,1)} %reshape.11), channel_id=1, source_target_pairs={{0,64},{64,128},{128,192},{192,0},{1,65},{65,129},{129,193},{193,1... | collective-permute-start | bytes 2359304 | tf_op jit(solution)/shard_map/ppermute | solution.py:15
  43.3 31.2 %collective-permute-start.10 = (bf16[64,4,1536]{2,0,1:T(8,128)(2,1)}, bf16[64,4,1536]{2,0,1:T(8,128)(2,1)S(1)}, u32[]{:S(2)}, u32[]{:S(2)}) collective-permute-start(bf16[64,4,1536]{2,0,1:T(8,128)(2,1)} %reshape.11), channel_id=1, source_target_pairs={{0,192},{64,0},{128,64},{192,128},{1,193},{65,1},{129,65},{193,129... | collective-permute-start | bytes 2359304 | tf_op jit(solution)/shard_map/ppermute | solution.py:15
  54.8 22.6 %collective-permute-start.11 = (bf16[64,4,1536]{2,0,1:T(8,128)(2,1)}, bf16[64,4,1536]{2,0,1:T(8,128)(2,1)S(1)}, u32[]{:S(2)}, u32[]{:S(2)}) collective-permute-start(bf16[64,4,1536]{2,0,1:T(8,128)(2,1)} %collective-permute-done.9), channel_id=1, source_target_pairs={{0,64},{64,128},{128,192},{192,0},{1,65},{65,129},{129,193},{193,1... | collective-permute-start | bytes 2359304 | tf_op jit(solution)/shard_map/ppermute | solution.py:15
  80.5 15.2 %collective-permute-start.12 = (f32[64,256]{1,0:T(8,128)S(1)}, f32[64,256]{1,0:T(8,128)S(1)}, u32[]{:S(2)}, u32[]{:S(2)}) collective-permute-start(f32[64,256]{1,0:T(8,128)S(1)} %add_add_fusion), channel_id=1, source_target_pairs={{0,1},{1,0},{2,3},{3,2},{4,5},{5,4},{6,7},{7,6},{8,9},{9,8},{10,11... | collective-permute-start | bytes 196616 | tf_op jit(solution)/shard_map/ppermute | solution.py:15
  95.7 4.7 %collective-permute-start.13 = (f32[64,256]{1,0:T(8,128)S(1)}, f32[64,256]{1,0:T(8,128)S(1)}, u32[]{:S(2)}, u32[]{:S(2)}) collective-permute-start(f32[64,256]{1,0:T(8,128)S(1)} %add.57), channel_id=1, source_target_pairs={{0,2},{2,0},{1,3},{3,1},{4,6},{6,4},{5,7},{7,5},{8,10},{10,8},{9,1... | collective-permute-start | bytes 196616 | tf_op jit(solution)/shard_map/ppermute | solution.py:15
where the time goes:
time: 101 us
  starting transfers between devices  37.8 us (37%)
  waiting for transfers between devices  32.9 us (33%)
  local copies, waits for them, and re-layouts  16.1 us (16%)
  matrix products  12.3 us (12%)
  other arithmetic  1.55 us (2%)
    ppermute x13, starting transfers between devices, shifted(): return lax.ppermute(x, axis, [(i, (i + by) % n) for i in range(n)])  32.9 us
    ppermute x13, waiting for transfers between devices, shifted(): return lax.ppermute(x, axis, [(i, (i + by) % n) for i in range(n)])  31.1 us
    unnamed x15, local copies, waits for them, and re-layouts  13.3 us
    dot_general x4, matrix products, run(): lax.dot_general(block, cov_local[:, j * per_y:(j + 1) * per_y, :], (((1,...  12.3 us
    ppermute x1, starting transfers between devices, per_device(): moved = lax.ppermute(scaled, ('z', 'xh', 'core'), pairs)  4.94 us
  transfers between devices with their start and end apart: 14, of which 10 were waited for; matrix products, arithmetic and copies ran while one was open for 22% of the time, Pallas kernels for 0%

commit v1 on v0

--- a/solution.py
+++ b/solution.py
@@ -51,38 +51,33 @@
             zh, d = divmod(z, nt)
             pairs.append((z * nt + t, (zh * nt + t) * nt + d))
     moved = lax.ppermute(scaled, ("z", "xh", "core"), pairs)
-    s1 = ring_gather(moved, "xl")
-    s2 = ring_gather(s1, "z")
+    s1 = lax.all_gather(moved, "xl")
+    s2 = lax.all_gather(s1, "z")
     nx = s1.shape[0]
     s2 = s2.reshape(nz // nt, nt, nx, n_loads, width)
-    own = jnp.transpose(s2, (3, 2, 0, 1, 4)).reshape(n_loads, nx * nz // nt, nt * width)
-    per_y = own.shape[1]
+    own = jnp.transpose(s2, (2, 0, 3, 1, 4)).reshape(nx * nz // nt, n_loads, nt * width)
+    per_y = own.shape[0]
     cov_local = cov[:, :, 0, :]
     ny = lax.axis_size("y")
     me = lax.axis_index("y")
 
     def term(block, y_from):
-        def stop_range(j):
-            def run(block, cov_local):
-                return lax.dot_general(
-                    block,
-                    cov_local[:, j * per_y : (j + 1) * per_y, :],
-                    (((1, 2), (1, 2)), ((), ())),
-                    preferred_element_type=jnp.float32,
-                )
+        cov_part = lax.dynamic_slice_in_dim(cov_local, (y_from % ny) * per_y, per_y, 1)
+        block, cov_part = lax.optimization_barrier((block, cov_part))
+        return lax.dot_general(
+            block, cov_part, (((0, 2), (1, 2)), ((), ())), preferred_element_type=jnp.float32
+        )
 
-            return run
-
-        return lax.switch(y_from % ny, [stop_range(j) for j in range(ny)], block, cov_local)
-
+    fwd = shifted(own, "y", 1)
+    bwd = shifted(own, "y", -1)
     part = term(own, me)
-    fwd, bwd = own, own
-    for s in range(1, ny // 2 + 1):
-        fwd = shifted(fwd, "y", 1)
-        part = part + term(fwd, me - s)
-        if s <= (ny - 1) // 2:
-            bwd = shifted(bwd, "y", -1)
-            part = part + term(bwd, me + s)
+    part = part + term(fwd, me - 1)
+    part = part + term(bwd, me + 1)
+    half = n_loads // 2
+    far_a = shifted(fwd[:, :half], "y", 1)
+    far_b = shifted(bwd[:, half:], "y", -1)
+    far = jnp.concatenate([far_a, far_b], axis=1)
+    part = part + term(far, me + 2)
     return team_sum(part)
 
 

time: 101 us -> 85.6 us (0.85)
  blocking collectives: 0 us -> 29.9 us
  waiting for transfers between devices: 32.9 us -> 11.1 us
  starting transfers between devices: 37.8 us -> 22.5 us
  matrix products: 12.3 us -> 4.26 us
    all_gather x0 -> x2, blocking collectives: none -> 29.9 us  [the longest x1 25.9 us: per_device(): s2 = lax.all_gather(s1, 'z')]
    ppermute x13 -> x6, waiting for transfers between devices: 31.1 us -> 9.41 us  [shifted(): return lax.ppermute(x, axis, [(i, (i + by) % n) for i in range(n)])]
    ppermute x13 -> x6, starting transfers between devices: 32.9 us -> 17.5 us  [shifted(): return lax.ppermute(x, axis, [(i, (i + by) % n) for i in range(n)])]
    dynamic_slice x1, local copies, waits for them, and re-layouts: 0.09 us -> 11.8 us  [term(): lax.dynamic_slice_in_dim(cov_local, y_from % ny * per_y, per_y, 1)]
    unnamed x15 -> x4, local copies, waits for them, and re-layouts: 13.3 us -> 2.28 us
    dot_general x4, matrix products: 12.3 us -> 4.26 us  [term(): lax.dot_general(block, cov_part, (((0, 2), (1, 2)), ((), ())), preferred_...]
  transfers between devices with their start and end apart: 14 -> 7, of which waited for: 10 -> 5; matrix products, arithmetic and copies ran while one was open for 22% -> 20% of each run, Pallas kernels for 0% -> 0%
where the time goes in v1:
time: 85.6 us; the launch traced here: 85.4 us
  blocking collectives  29.9 us (35%)
  starting transfers between devices  22.5 us (26%)
  local copies, waits for them, and re-layouts  15.9 us (19%)
  waiting for transfers between devices  11.1 us (13%)
  matrix products  4.26 us (5%)
  other arithmetic  1.52 us (2%)
    all_gather x1, blocking collectives, per_device(): s2 = lax.all_gather(s1, 'z')  25.9 us
    ppermute x6, starting transfers between devices, shifted(): return lax.ppermute(x, axis, [(i, (i + by) % n) for i in range(n)])  17.5 us
    dynamic_slice x1, local copies, waits for them, and re-layouts, term(): lax.dynamic_slice_in_dim(cov_local, y_from % ny * per_y, per_y, 1)  11.8 us
    ppermute x6, waiting for transfers between devices, shifted(): return lax.ppermute(x, axis, [(i, (i + by) % n) for i in range(n)])  9.41 us
    ppermute x1, starting transfers between devices, per_device(): moved = lax.ppermute(scaled, ('z', 'xh', 'core'), pairs)  4.94 us
    dot_general x4, matrix products, term(): lax.dot_general(block, cov_part, (((0, 2), (1, 2)), ((), ())), preferred_...  4.26 us
    all_gather x1, blocking collectives, per_device(): s1 = lax.all_gather(moved, 'xl')  4.01 us
    unnamed x4, local copies, waits for them, and re-layouts  2.28 us
  transfers between devices with their start and end apart: 7, of which 5 were waited for; matrix products, arithmetic and copies ran while one was open for 20% of the time, Pallas kernels for 0%

profile of v1, /device:TPU:1, one launch (start us, length us, event | category | flops | bytes accessed | tf_op | source)
XLA Modules:
  0.0 85.4 jit_solution(4871386397211412854)
XLA Ops:
  0.0 0.8 copy.12
  0.9 0.8 fusion.3
  1.7 4.9 %collective-permute-start = (bf16[64,384]{1,0:T(8,128)(2,1)S(1)}, bf16[64,384]{1,0:T(8,128)(2,1)S(1)}, u32[]{:S(2)}, u32[]{:S(2)}) collective-permute-start(bf16[64,384]{1,0:T(8,128)(2,1)S(1)} %fusion.3), channel_id=1, source_target_pairs={{0,0},{1,4},{2,8},{3,12},{4,1},{5,5},{6,9},{7,13},{8,2},{9,6},{10,... | collective-permute-start | bytes 147464 | tf_op jit(solution)/shard_map/ppermute | solution.py:53
  6.7 1.7 %collective-permute-done = bf16[64,384]{1,0:T(8,128)(2,1)S(1)} collective-permute-done((bf16[64,384]{1,0:T(8,128)(2,1)S(1)}, bf16[64,384]{1,0:T(8,128)(2,1)S(1)}, u32[]{:S(2)}, u32[]{:S(2)}) %collective-permute-start) | collective-permute-done | bytes 49184 | tf_op jit(solution)/shard_map/ppermute | solution.py:53
  8.4 4.0 %all-gather = bf16[128,384]{1,0:T(8,128)(2,1)S(1)} all-gather(bf16[64,384]{1,0:T(8,128)(2,1)S(1)} %collective-permute-done), channel_id=2, replica_groups=mesh['y'=4,'xl'=2,'z'=8,'xh'=2,'core'=2] {'xl'}, dimensions={0}, use_global_device_ids=true | all-gather | bytes 147456 | tf_op jit(solution)/shard_map/all_gather | solution.py:54
  12.4 25.9 %all-gather.1 = bf16[16,64,384]{2,1,0:T(8,128)(2,1)S(1)} all-gather(bf16[2,64,384]{2,1,0:T(8,128)(2,1)S(1)} %bitcast.49), channel_id=3, replica_groups=mesh['y'=4,'xl'=2,'z'=8,'xh'=2,'core'=2] {'z'}, dimensions={0}, use_global_device_ids=true | all-gather | bytes 884736 | tf_op jit(solution)/shard_map/all_gather | solution.py:55
  38.4 0.6 copy.13
  39.3 1.4 %collective-permute-start.1 = (bf16[4,64,1536]{2,1,0:T(8,128)(2,1)S(1)}, bf16[4,64,1536]{2,1,0:T(8,128)(2,1)S(1)}, u32[]{:S(2)}, u32[]{:S(2)}) collective-permute-start(bf16[4,64,1536]{2,1,0:T(8,128)(2,1)S(1)} %reshape.15), channel_id=1, source_target_pairs={{0,64},{64,128},{128,192},{192,0},{1,65},{65,129},{129,193},{193,1... | collective-permute-start | bytes 2359304 | tf_op jit(solution)/shard_map/ppermute | solution.py:15
  40.7 1.5 %collective-permute-start.2 = (bf16[4,64,1536]{2,1,0:T(8,128)(2,1)S(1)}, bf16[4,64,1536]{2,1,0:T(8,128)(2,1)S(1)}, u32[]{:S(2)}, u32[]{:S(2)}) collective-permute-start(bf16[4,64,1536]{2,1,0:T(8,128)(2,1)S(1)} %reshape.15), channel_id=1, source_target_pairs={{0,192},{64,0},{128,64},{192,128},{1,193},{65,1},{129,65},{193,129... | collective-permute-start | bytes 2359304 | tf_op jit(solution)/shard_map/ppermute | solution.py:15
  42.2 11.8 %constant_dynamic-slice_fusion = (bf16[256,4,1,1536]{3,1,2,0:T(4,128)(2,1)S(1)}, bf16[256,4,1,1536]{3,1,2,0:T(4,128)(2,1)S(1)}, bf16[256,4,1,1536]{3,1,2,0:T(4,128)(2,1)S(1)}, bf16[256,4,1,1536]{3,1,2,0:T(4,128)(2,1)S(1)}) fusion(bf16[256,16,1,1536]{3,1,2,0:T(8,128)(2,1)} %param.5, s32[]{:T(128)S(6)} %select_n.38, s32[]{:T(128)S(6)} %select_n.36, ...), kind=kLoop, calls=%fused_computation.14 | loop fusion | bytes 25165840 | tf_op jit(solution)/shard_map/dynamic_slice | solution.py:65
  54.0 0.6 copy.31
  54.6 0.6 copy.30
  56.3 1.1 %convolution_bitcast_fusion.3 = f32[64,256]{1,0:T(8,128)S(1)} fusion(bf16[4,64,1536]{2,1,0:T(8,128)(2,1)S(1)} %reshape.15, bf16[256,4,1536]{2,0,1:T(8,128)(2,1)S(1)} %bitcast.43), kind=kOutput, calls=%fused_computation.10 | convolution fusion | flops 201326592 | bytes 3997696 | tf_op jit(solution)/shard_map/dot_general | solution.py:67
  57.4 1.5 %collective-permute-start.4 = (bf16[4,32,1536]{2,1,0:T(8,128)(2,1)S(1)}, bf16[4,32,1536]{2,1,0:T(8,128)(2,1)S(1)}, u32[]{:S(2)}, u32[]{:S(2)}) collective-permute-start(bf16[4,32,1536]{2,1,0:T(8,128)(2,1)S(1)} %slice.9), channel_id=1, source_target_pairs={{0,192},{64,0},{128,64},{192,128},{1,193},{65,1},{129,65},{193,129... | collective-permute-start | bytes 1179656 | tf_op jit(solution)/shard_map/ppermute | solution.py:15
  59.1 1.1 %fusion.2 = f32[64,256]{1,0:T(8,128)S(1)} fusion(f32[64,256]{1,0:T(8,128)S(1)} %convolution_bitcast_fusion.3, bf16[4,64,1536]{2,1,0:T(8,128)(2,1)S(1)} %collective-permute-done.1, bf16[256,4,1536]{2,0,1:T(8,128)(2,1)S(1)} %bitcast.46), kind=kOutput, calls=%fused_computation.9 | convolution fusion | flops 201342976 | bytes 4063232 | tf_op jit(solution)/shard_map/dot_general | solution.py:67
  60.1 1.1 %fusion.1 = f32[64,256]{1,0:T(8,128)S(1)} fusion(f32[64,256]{1,0:T(8,128)S(1)} %fusion.2, bf16[4,64,1536]{2,1,0:T(8,128)(2,1)S(1)} %collective-permute-done.2, bf16[256,4,1536]{2,0,1:T(8,128)(2,1)S(1)} %bitcast.45), kind=kOutput, calls=%fused_computation.7 | convolution fusion | flops 201342976 | bytes 4063232 | tf_op jit(solution)/shard_map/dot_general | solution.py:67
  61.2 4.3 %collective-permute-done.4 = bf16[4,32,1536]{2,1,0:T(8,128)(2,1)S(1)} collective-permute-done((bf16[4,32,1536]{2,1,0:T(8,128)(2,1)S(1)}, bf16[4,32,1536]{2,1,0:T(8,128)(2,1)S(1)}, u32[]{:S(2)}, u32[]{:S(2)}) %collective-permute-start.4) | collective-permute-done | bytes 393248 | tf_op jit(solution)/shard_map/ppermute | solution.py:15
  65.6 1.3 %collective-permute-done.3 = bf16[4,32,1536]{2,1,0:T(8,128)(2,1)S(1)} collective-permute-done((bf16[4,32,1536]{2,1,0:T(8,128)(2,1)S(1)}, bf16[4,32,1536]{2,1,0:T(8,128)(2,1)S(1)}, u32[]{:S(2)}, u32[]{:S(2)}) %collective-permute-start.3) | collective-permute-done | bytes 393248 | tf_op jit(solution)/shard_map/ppermute | solution.py:15
  66.9 1.1 %fusion = f32[64,256]{1,0:T(8,128)S(1)} fusion(f32[64,256]{1,0:T(8,128)S(1)} %fusion.1, bf16[4,64,1536]{2,1,0:T(8,128)(2,1)S(1)} %pad_maximum_fusion, bf16[256,4,1536]{2,0,1:T(8,128)(2,1)S(1)} %bitcast.44), kind=kOutput, calls=%fused_computation.5 | convolution fusion | flops 201342976 | bytes 4063232 | tf_op jit(solution)/shard_map/dot_general | solution.py:67
  68.0 11.2 %collective-permute-start.5 = (f32[64,256]{1,0:T(8,128)S(1)}, f32[64,256]{1,0:T(8,128)S(1)}, u32[]{:S(2)}, u32[]{:S(2)}) collective-permute-start(f32[64,256]{1,0:T(8,128)S(1)} %fusion), channel_id=1, source_target_pairs={{0,1},{1,0},{2,3},{3,2},{4,5},{5,4},{6,7},{7,6},{8,9},{9,8},{10,11... | collective-permute-start | bytes 196616 | tf_op jit(solution)/shard_map/ppermute | solution.py:15
  79.1 0.9 %collective-permute-done.5 = f32[64,256]{1,0:T(8,128)S(1)} collective-permute-done((f32[64,256]{1,0:T(8,128)S(1)}, f32[64,256]{1,0:T(8,128)S(1)}, u32[]{:S(2)}, u32[]{:S(2)}) %collective-permute-start.5) | collective-permute-done | bytes 65568 | tf_op jit(solution)/shard_map/ppermute | solution.py:15
  80.1 1.8 %collective-permute-start.6 = (f32[64,256]{1,0:T(8,128)S(1)}, f32[64,256]{1,0:T(8,128)S(1)}, u32[]{:S(2)}, u32[]{:S(2)}) collective-permute-start(f32[64,256]{1,0:T(8,128)S(1)} %add.60), channel_id=1, source_target_pairs={{0,2},{2,0},{1,3},{3,1},{4,6},{6,4},{5,7},{7,5},{8,10},{10,8},{9,1... | collective-permute-start | bytes 196616 | tf_op jit(solution)/shard_map/ppermute | solution.py:15
  81.9 2.9 %collective-permute-done.6 = f32[64,256]{1,0:T(8,128)S(1)} collective-permute-done((f32[64,256]{1,0:T(8,128)S(1)}, f32[64,256]{1,0:T(8,128)S(1)}, u32[]{:S(2)}, u32[]{:S(2)}) %collective-permute-start.6) | collective-permute-done | bytes 65568 | tf_op jit(solution)/shard_map/ppermute | solution.py:15
  84.8 0.6 add.61
  (11 shorter events, 1.8 us)
Async XLA Ops:
  1.7 6.7 %collective-permute-start = (bf16[64,384]{1,0:T(8,128)(2,1)S(1)}, bf16[64,384]{1,0:T(8,128)(2,1)S(1)}, u32[]{:S(2)}, u32[]{:S(2)}) collective-permute-start(bf16[64,384]{1,0:T(8,128)(2,1)S(1)} %fusion.3), channel_id=1, source_target_pairs={{0,0},{1,4},{2,8},{3,12},{4,1},{5,5},{6,9},{7,13},{8,2},{9,6},{10,... | collective-permute-start | bytes 147464 | tf_op jit(solution)/shard_map/ppermute | solution.py:53
  39.3 18.1 %collective-permute-start.1 = (bf16[4,64,1536]{2,1,0:T(8,128)(2,1)S(1)}, bf16[4,64,1536]{2,1,0:T(8,128)(2,1)S(1)}, u32[]{:S(2)}, u32[]{:S(2)}) collective-permute-start(bf16[4,64,1536]{2,1,0:T(8,128)(2,1)S(1)} %reshape.15), channel_id=1, source_target_pairs={{0,64},{64,128},{128,192},{192,0},{1,65},{65,129},{129,193},{193,1... | collective-permute-start | bytes 2359304 | tf_op jit(solution)/shard_map/ppermute | solution.py:15
  40.7 16.7 %collective-permute-start.2 = (bf16[4,64,1536]{2,1,0:T(8,128)(2,1)S(1)}, bf16[4,64,1536]{2,1,0:T(8,128)(2,1)S(1)}, u32[]{:S(2)}, u32[]{:S(2)}) collective-permute-start(bf16[4,64,1536]{2,1,0:T(8,128)(2,1)S(1)} %reshape.15), channel_id=1, source_target_pairs={{0,192},{64,0},{128,64},{192,128},{1,193},{65,1},{129,65},{193,129... | collective-permute-start | bytes 2359304 | tf_op jit(solution)/shard_map/ppermute | solution.py:15
  57.4 8.1 %collective-permute-start.4 = (bf16[4,32,1536]{2,1,0:T(8,128)(2,1)S(1)}, bf16[4,32,1536]{2,1,0:T(8,128)(2,1)S(1)}, u32[]{:S(2)}, u32[]{:S(2)}) collective-permute-start(bf16[4,32,1536]{2,1,0:T(8,128)(2,1)S(1)} %slice.9), channel_id=1, source_target_pairs={{0,192},{64,0},{128,64},{192,128},{1,193},{65,1},{129,65},{193,129... | collective-permute-start | bytes 1179656 | tf_op jit(solution)/shard_map/ppermute | solution.py:15
  58.9 7.9 %collective-permute-start.3 = (bf16[4,32,1536]{2,1,0:T(8,128)(2,1)S(1)}, bf16[4,32,1536]{2,1,0:T(8,128)(2,1)S(1)}, u32[]{:S(2)}, u32[]{:S(2)}) collective-permute-start(bf16[4,32,1536]{2,1,0:T(8,128)(2,1)S(1)} %slice.8), channel_id=1, source_target_pairs={{0,64},{64,128},{128,192},{192,0},{1,65},{65,129},{129,193},{193,1... | collective-permute-start | bytes 1179656 | tf_op jit(solution)/shard_map/ppermute | solution.py:15
  68.0 12.1 %collective-permute-start.5 = (f32[64,256]{1,0:T(8,128)S(1)}, f32[64,256]{1,0:T(8,128)S(1)}, u32[]{:S(2)}, u32[]{:S(2)}) collective-permute-start(f32[64,256]{1,0:T(8,128)S(1)} %fusion), channel_id=1, source_target_pairs={{0,1},{1,0},{2,3},{3,2},{4,5},{5,4},{6,7},{7,6},{8,9},{9,8},{10,11... | collective-permute-start | bytes 196616 | tf_op jit(solution)/shard_map/ppermute | solution.py:15
  80.1 4.7 %collective-permute-start.6 = (f32[64,256]{1,0:T(8,128)S(1)}, f32[64,256]{1,0:T(8,128)S(1)}, u32[]{:S(2)}, u32[]{:S(2)}) collective-permute-start(f32[64,256]{1,0:T(8,128)S(1)} %add.60), channel_id=1, source_target_pairs={{0,2},{2,0},{1,3},{3,1},{4,6},{6,4},{5,7},{7,5},{8,10},{10,8},{9,1... | collective-permute-start | bytes 196616 | tf_op jit(solution)/shard_map/ppermute | solution.py:15

commit v2 on v1

--- a/solution.py
+++ b/solution.py
@@ -32,8 +32,9 @@
 
 
 def team_sum(x):
-    x = x + shifted(x, "core", 1)
-    return x + shifted(x, "xh", 1)
+    on_chip = x + shifted(x, "core", 1)
+    across = shifted(x, "xh", 1) + lax.ppermute(x, ("xh", "core"), [(0, 3), (3, 0), (1, 2), (2, 1)])
+    return on_chip + across
 
 
 def per_device(loadings, scales, cov):
@@ -43,17 +44,31 @@
         loadings.astype(jnp.float32).reshape(n_loads, groups, width // groups)
         * scales.astype(jnp.float32)[:, :, None]
     ).reshape(n_loads, width).astype(jnp.bfloat16)
+    nx = lax.axis_size("xl")
     nz = lax.axis_size("z")
     nt = lax.axis_size("xh") * lax.axis_size("core")
-    pairs = []
-    for z in range(nz):
-        for t in range(nt):
-            zh, d = divmod(z, nt)
-            pairs.append((z * nt + t, (zh * nt + t) * nt + d))
-    moved = lax.ppermute(scaled, ("z", "xh", "core"), pairs)
-    s1 = lax.all_gather(moved, "xl")
-    s2 = lax.all_gather(s1, "z")
-    nx = s1.shape[0]
+    same, other = [], []
+    for x in range(nx):
+        for z in range(nz):
+            for t in range(nt):
+                zh, d = divmod(z, nt)
+                src = (x * nz + z) * nt + t
+                same.append((src, (x * nz + zh * nt + t) * nt + d))
+                other.append((src, (((x + 1) % nx) * nz + zh * nt + t) * nt + d))
+    axes = ("xl", "z", "xh", "core")
+    mine = lax.ppermute(scaled, axes, same)
+    theirs = lax.ppermute(scaled, axes, other)
+    first = lax.axis_index("xl") == 0
+    s1 = jnp.where(first, jnp.stack([mine, theirs]), jnp.stack([theirs, mine]))
+    got = {0: s1}
+    for s in range(1, nz // 2):
+        got[-s] = shifted(s1, "z", s)
+        got[s] = shifted(s1, "z", -s)
+    got[-(nz // 2)] = shifted(got[-(nz // 2 - 1)], "z", 1)
+    rel = [got[k] if k in got else got[k - nz] for k in range(nz)]
+    rel = jnp.stack(rel + rel)
+    zme = lax.axis_index("z")
+    s2 = lax.dynamic_slice_in_dim(rel, (nz - zme) % nz, nz, 0)
     s2 = s2.reshape(nz // nt, nt, nx, n_loads, width)
     own = jnp.transpose(s2, (2, 0, 3, 1, 4)).reshape(nx * nz // nt, n_loads, nt * width)
     per_y = own.shape[0]

time: 85.6 us -> 86.9 us (1.015)
  the two profiles are of different devices: /device:TPU:1 before, /device:TPU:2 now
where the time goes in v2:
time: 86.9 us; the launch traced here: 86.7 us
  starting transfers between devices  40.1 us (46%)
  waiting for transfers between devices  24.2 us (28%)
  local copies, waits for them, and re-layouts  16.3 us (19%)
  matrix products  4.26 us (5%)
  other arithmetic  1.59 us (2%)
    ppermute x13, starting transfers between devices, shifted(): return lax.ppermute(x, axis, [(i, (i + by) % n) for i in range(n)])  37.1 us
    ppermute x13, waiting for transfers between devices, shifted(): return lax.ppermute(x, axis, [(i, (i + by) % n) for i in range(n)])  19.2 us
    dynamic_slice x1, local copies, waits for them, and re-layouts, term(): lax.dynamic_slice_in_dim(cov_local, y_from % ny * per_y, per_y, 1)  11.8 us
    dot_general x4, matrix products, term(): lax.dot_general(block, cov_part, (((0, 2), (1, 2)), ((), ())), preferred_...  4.26 us
    ppermute x1, waiting for transfers between devices, team_sum(): lax.ppermute(x, ('xh', 'core'), [(0, 3), (3, 0), (1, 2), (2, 1)])  2.95 us
    unnamed x17, local copies, waits for them, and re-layouts  2.53 us
    ppermute x1, starting transfers between devices, per_device(): theirs = lax.ppermute(scaled, axes, other)  2.36 us
    ppermute x1, waiting for transfers between devices, per_device(): theirs = lax.ppermute(scaled, axes, other)  2.07 us
  transfers between devices with their start and end apart: 16, of which 8 were waited for; matrix products, arithmetic and copies ran while one was open for 20% of the time, Pallas kernels for 0%

profile of v2, /device:TPU:2, one launch (start us, length us, event | category | flops | bytes accessed | tf_op | source)
XLA Modules:
  0.0 86.7 jit_solution(2976703515196061283)
XLA Ops:
  0.0 0.8 copy.10
  0.9 0.8 fusion.3
  2.4 2.4 %collective-permute-start.1 = (bf16[64,384]{1,0:T(8,128)(2,1)S(1)}, bf16[64,384]{1,0:T(8,128)(2,1)S(1)}, u32[]{:S(2)}, u32[]{:S(2)}) collective-permute-start(bf16[64,384]{1,0:T(8,128)(2,1)S(1)} %fusion.3), channel_id=1, source_target_pairs={{0,32},{1,36},{2,40},{3,44},{4,33},{5,37},{6,41},{7,45},{8,34},{9,... | collective-permute-start | bytes 147464 | tf_op jit(solution)/shard_map/ppermute | solution.py:60
  4.8 2.1 %collective-permute-done.1 = bf16[64,384]{1,0:T(8,128)(2,1)S(1)} collective-permute-done((bf16[64,384]{1,0:T(8,128)(2,1)S(1)}, bf16[64,384]{1,0:T(8,128)(2,1)S(1)}, u32[]{:S(2)}, u32[]{:S(2)}) %collective-permute-start.1) | collective-permute-done | bytes 49184 | tf_op jit(solution)/shard_map/ppermute | solution.py:60
  6.8 12.2 %collective-permute-start.2 = (bf16[2,64,384]{2,1,0:T(8,128)(2,1)S(1)}, bf16[2,64,384]{2,1,0:T(8,128)(2,1)S(1)}, u32[]{:S(2)}, u32[]{:S(2)}) collective-permute-start(bf16[2,64,384]{2,1,0:T(8,128)(2,1)S(1)} %maximum_select_fusion.1), channel_id=1, source_target_pairs={{0,28},{4,0},{8,4},{12,8},{16,12},{20,16},{24,20},{28,24},{1,29},{... | collective-permute-start | bytes 294920 | tf_op jit(solution)/shard_map/ppermute | solution.py:15
  19.4 3.8 %collective-permute-start.5 = (bf16[2,64,384]{2,1,0:T(8,128)(2,1)S(1)}, bf16[2,64,384]{2,1,0:T(8,128)(2,1)S(1)}, u32[]{:S(2)}, u32[]{:S(2)}) collective-permute-start(bf16[2,64,384]{2,1,0:T(8,128)(2,1)S(1)} %maximum_select_fusion.1), channel_id=1, source_target_pairs={{0,12},{4,16},{8,20},{12,24},{16,28},{20,0},{24,4},{28,8},{1,13},{... | collective-permute-start | bytes 294920 | tf_op jit(solution)/shard_map/ppermute | solution.py:15
  23.2 3.8 %collective-permute-start.7 = (bf16[2,64,384]{2,1,0:T(8,128)(2,1)S(1)}, bf16[2,64,384]{2,1,0:T(8,128)(2,1)S(1)}, u32[]{:S(2)}, u32[]{:S(2)}) collective-permute-start(bf16[2,64,384]{2,1,0:T(8,128)(2,1)S(1)} %maximum_select_fusion.1), channel_id=1, source_target_pairs={{0,8},{4,12},{8,16},{12,20},{16,24},{20,28},{24,0},{28,4},{1,9},{5... | collective-permute-start | bytes 294920 | tf_op jit(solution)/shard_map/ppermute | solution.py:15
  27.2 4.0 %collective-permute-done.5 = bf16[2,64,384]{2,1,0:T(8,128)(2,1)S(1)} collective-permute-done((bf16[2,64,384]{2,1,0:T(8,128)(2,1)S(1)}, bf16[2,64,384]{2,1,0:T(8,128)(2,1)S(1)}, u32[]{:S(2)}, u32[]{:S(2)}) %collective-permute-start.5) | collective-permute-done | bytes 98336 | tf_op jit(solution)/shard_map/ppermute | solution.py:15
  31.2 3.9 %collective-permute-start.6 = (bf16[2,64,384]{2,1,0:T(8,128)(2,1)S(1)}, bf16[2,64,384]{2,1,0:T(8,128)(2,1)S(1)}, u32[]{:S(2)}, u32[]{:S(2)}) collective-permute-start(bf16[2,64,384]{2,1,0:T(8,128)(2,1)S(1)} %collective-permute-done.5), channel_id=1, source_target_pairs={{0,4},{4,8},{8,12},{12,16},{16,20},{20,24},{24,28},{28,0},{1,5},{5... | collective-permute-start | bytes 294920 | tf_op jit(solution)/shard_map/ppermute | solution.py:15
  35.1 3.9 %collective-permute-done.6 = bf16[2,64,384]{2,1,0:T(8,128)(2,1)S(1)} collective-permute-done((bf16[2,64,384]{2,1,0:T(8,128)(2,1)S(1)}, bf16[2,64,384]{2,1,0:T(8,128)(2,1)S(1)}, u32[]{:S(2)}, u32[]{:S(2)}) %collective-permute-start.6) | collective-permute-done | bytes 98336 | tf_op jit(solution)/shard_map/ppermute | solution.py:15
  40.4 1.7 %collective-permute-start.9 = (bf16[4,64,1536]{2,1,0:T(8,128)(2,1)S(1)}, bf16[4,64,1536]{2,1,0:T(8,128)(2,1)S(1)}, u32[]{:S(2)}, u32[]{:S(2)}) collective-permute-start(bf16[4,64,1536]{2,1,0:T(8,128)(2,1)S(1)} %reshape.74), channel_id=1, source_target_pairs={{0,64},{64,128},{128,192},{192,0},{1,65},{65,129},{129,193},{193,1... | collective-permute-start | bytes 2359304 | tf_op jit(solution)/shard_map/ppermute | solution.py:15
  42.0 1.7 %collective-permute-start.10 = (bf16[4,64,1536]{2,1,0:T(8,128)(2,1)S(1)}, bf16[4,64,1536]{2,1,0:T(8,128)(2,1)S(1)}, u32[]{:S(2)}, u32[]{:S(2)}) collective-permute-start(bf16[4,64,1536]{2,1,0:T(8,128)(2,1)S(1)} %reshape.74), channel_id=1, source_target_pairs={{0,192},{64,0},{128,64},{192,128},{1,193},{65,1},{129,65},{193,129... | collective-permute-start | bytes 2359304 | tf_op jit(solution)/shard_map/ppermute | solution.py:15
  43.7 11.8 %constant_dynamic-slice_fusion = (bf16[256,4,1,1536]{3,1,2,0:T(4,128)(2,1)S(1)}, bf16[256,4,1,1536]{3,1,2,0:T(4,128)(2,1)S(1)}, bf16[256,4,1,1536]{3,1,2,0:T(4,128)(2,1)S(1)}, bf16[256,4,1,1536]{3,1,2,0:T(4,128)(2,1)S(1)}) fusion(bf16[256,16,1,1536]{3,1,2,0:T(8,128)(2,1)} %param.5, s32[]{:T(128)S(6)} %select_n.70, s32[]{:T(128)S(6)} %select_n.68, ...), kind=kLoop, calls=%fused_computation.33 | loop fusion | bytes 25165840 | tf_op jit(solution)/shard_map/dynamic_slice | solution.py:80
  57.9 1.1 %convolution_bitcast_fusion.3 = f32[64,256]{1,0:T(8,128)S(1)} fusion(bf16[4,64,1536]{2,1,0:T(8,128)(2,1)S(1)} %reshape.74, bf16[256,4,1536]{2,0,1:T(8,128)(2,1)S(1)} %bitcast.67), kind=kOutput, calls=%fused_computation.10 | convolution fusion | flops 201326592 | bytes 3997696 | tf_op jit(solution)/shard_map/dot_general | solution.py:82
  58.9 1.3 %collective-permute-done.9 = bf16[4,64,1536]{2,1,0:T(8,128)(2,1)S(1)} collective-permute-done((bf16[4,64,1536]{2,1,0:T(8,128)(2,1)S(1)}, bf16[4,64,1536]{2,1,0:T(8,128)(2,1)S(1)}, u32[]{:S(2)}, u32[]{:S(2)}) %collective-permute-start.9) | collective-permute-done | bytes 786464 | tf_op jit(solution)/shard_map/ppermute | solution.py:15
  60.3 3.3 %collective-permute-start.12 = (bf16[4,32,1536]{2,1,0:T(8,128)(2,1)S(1)}, bf16[4,32,1536]{2,1,0:T(8,128)(2,1)S(1)}, u32[]{:S(2)}, u32[]{:S(2)}) collective-permute-start(bf16[4,32,1536]{2,1,0:T(8,128)(2,1)S(1)} %slice.9), channel_id=1, source_target_pairs={{0,192},{64,0},{128,64},{192,128},{1,193},{65,1},{129,65},{193,129... | collective-permute-start | bytes 1179656 | tf_op jit(solution)/shard_map/ppermute | solution.py:15
  63.7 1.1 %fusion.2 = f32[64,256]{1,0:T(8,128)S(1)} fusion(f32[64,256]{1,0:T(8,128)S(1)} %convolution_bitcast_fusion.3, bf16[4,64,1536]{2,1,0:T(8,128)(2,1)S(1)} %collective-permute-done.9, bf16[256,4,1536]{2,0,1:T(8,128)(2,1)S(1)} %bitcast.70), kind=kOutput, calls=%fused_computation.9 | convolution fusion | flops 201342976 | bytes 4063232 | tf_op jit(solution)/shard_map/dot_general | solution.py:82
  64.8 1.1 %fusion.1 = f32[64,256]{1,0:T(8,128)S(1)} fusion(f32[64,256]{1,0:T(8,128)S(1)} %fusion.2, bf16[4,64,1536]{2,1,0:T(8,128)(2,1)S(1)} %collective-permute-done.10, bf16[256,4,1536]{2,0,1:T(8,128)(2,1)S(1)} %bitcast.69), kind=kOutput, calls=%fused_computation.7 | convolution fusion | flops 201342976 | bytes 4063232 | tf_op jit(solution)/shard_map/dot_general | solution.py:82
  65.8 4.4 %collective-permute-done.12 = bf16[4,32,1536]{2,1,0:T(8,128)(2,1)S(1)} collective-permute-done((bf16[4,32,1536]{2,1,0:T(8,128)(2,1)S(1)}, bf16[4,32,1536]{2,1,0:T(8,128)(2,1)S(1)}, u32[]{:S(2)}, u32[]{:S(2)}) %collective-permute-start.12) | collective-permute-done | bytes 393248 | tf_op jit(solution)/shard_map/ppermute | solution.py:15
  70.2 3.5 %collective-permute-done.11 = bf16[4,32,1536]{2,1,0:T(8,128)(2,1)S(1)} collective-permute-done((bf16[4,32,1536]{2,1,0:T(8,128)(2,1)S(1)}, bf16[4,32,1536]{2,1,0:T(8,128)(2,1)S(1)}, u32[]{:S(2)}, u32[]{:S(2)}) %collective-permute-start.11) | collective-permute-done | bytes 393248 | tf_op jit(solution)/shard_map/ppermute | solution.py:15
  73.8 1.1 %fusion = f32[64,256]{1,0:T(8,128)S(1)} fusion(f32[64,256]{1,0:T(8,128)S(1)} %fusion.1, bf16[4,64,1536]{2,1,0:T(8,128)(2,1)S(1)} %pad_maximum_fusion, bf16[256,4,1536]{2,0,1:T(8,128)(2,1)S(1)} %bitcast.68), kind=kOutput, calls=%fused_computation.5 | convolution fusion | flops 201342976 | bytes 4063232 | tf_op jit(solution)/shard_map/dot_general | solution.py:82
  74.9 6.0 %collective-permute-start.14 = (f32[64,256]{1,0:T(8,128)S(1)}, f32[64,256]{1,0:T(8,128)S(1)}, u32[]{:S(2)}, u32[]{:S(2)}) collective-permute-start(f32[64,256]{1,0:T(8,128)S(1)} %fusion), channel_id=1, source_target_pairs={{0,2},{2,0},{1,3},{3,1},{4,6},{6,4},{5,7},{7,5},{8,10},{10,8},{9,1... | collective-permute-start | bytes 196616 | tf_op jit(solution)/shard_map/ppermute | solution.py:15
  81.1 2.0 %collective-permute-done.14 = f32[64,256]{1,0:T(8,128)S(1)} collective-permute-done((f32[64,256]{1,0:T(8,128)S(1)}, f32[64,256]{1,0:T(8,128)S(1)}, u32[]{:S(2)}, u32[]{:S(2)}) %collective-permute-start.14) | collective-permute-done | bytes 65568 | tf_op jit(solution)/shard_map/ppermute | solution.py:15
  83.1 2.9 %collective-permute-done.15 = f32[64,256]{1,0:T(8,128)S(1)} collective-permute-done((f32[64,256]{1,0:T(8,128)S(1)}, f32[64,256]{1,0:T(8,128)S(1)}, u32[]{:S(2)}, u32[]{:S(2)}) %collective-permute-start.15) | collective-permute-done | bytes 65568 | tf_op jit(solution)/shard_map/ppermute | solution.py:36
  (44 shorter events, 5.9 us)
Async XLA Ops:
  1.7 3.0 %collective-permute-start = (bf16[64,384]{1,0:T(8,128)(2,1)S(1)}, bf16[64,384]{1,0:T(8,128)(2,1)S(1)}, u32[]{:S(2)}, u32[]{:S(2)}) collective-permute-start(bf16[64,384]{1,0:T(8,128)(2,1)S(1)} %fusion.3), channel_id=1, source_target_pairs={{0,0},{1,4},{2,8},{3,12},{4,1},{5,5},{6,9},{7,13},{8,2},{9,6},{10,... | collective-permute-start | bytes 147464 | tf_op jit(solution)/shard_map/ppermute | solution.py:59
  2.4 4.4 %collective-permute-start.1 = (bf16[64,384]{1,0:T(8,128)(2,1)S(1)}, bf16[64,384]{1,0:T(8,128)(2,1)S(1)}, u32[]{:S(2)}, u32[]{:S(2)}) collective-permute-start(bf16[64,384]{1,0:T(8,128)(2,1)S(1)} %fusion.3), channel_id=1, source_target_pairs={{0,32},{1,36},{2,40},{3,44},{4,33},{5,37},{6,41},{7,45},{8,34},{9,... | collective-permute-start | bytes 147464 | tf_op jit(solution)/shard_map/ppermute | solution.py:60
  6.8 20.2 %collective-permute-start.2 = (bf16[2,64,384]{2,1,0:T(8,128)(2,1)S(1)}, bf16[2,64,384]{2,1,0:T(8,128)(2,1)S(1)}, u32[]{:S(2)}, u32[]{:S(2)}) collective-permute-start(bf16[2,64,384]{2,1,0:T(8,128)(2,1)S(1)} %maximum_select_fusion.1), channel_id=1, source_target_pairs={{0,28},{4,0},{8,4},{12,8},{16,12},{20,16},{24,20},{28,24},{1,29},{... | collective-permute-start | bytes 294920 | tf_op jit(solution)/shard_map/ppermute | solution.py:15
  19.1 16.0 %collective-permute-start.3 = (bf16[2,64,384]{2,1,0:T(8,128)(2,1)S(1)}, bf16[2,64,384]{2,1,0:T(8,128)(2,1)S(1)}, u32[]{:S(2)}, u32[]{:S(2)}) collective-permute-start(bf16[2,64,384]{2,1,0:T(8,128)(2,1)S(1)} %maximum_select_fusion.1), channel_id=1, source_target_pairs={{0,24},{4,28},{8,0},{12,4},{16,8},{20,12},{24,16},{28,20},{1,25},{... | collective-permute-start | bytes 294920 | tf_op jit(solution)/shard_map/ppermute | solution.py:15
  19.4 15.7 %collective-permute-start.4 = (bf16[2,64,384]{2,1,0:T(8,128)(2,1)S(1)}, bf16[2,64,384]{2,1,0:T(8,128)(2,1)S(1)}, u32[]{:S(2)}, u32[]{:S(2)}) collective-permute-start(bf16[2,64,384]{2,1,0:T(8,128)(2,1)S(1)} %maximum_select_fusion.1), channel_id=1, source_target_pairs={{0,20},{4,24},{8,28},{12,0},{16,4},{20,8},{24,12},{28,16},{1,21},{... | collective-permute-start | bytes 294920 | tf_op jit(solution)/shard_map/ppermute | solution.py:15
  19.4 11.8 %collective-permute-start.5 = (bf16[2,64,384]{2,1,0:T(8,128)(2,1)S(1)}, bf16[2,64,384]{2,1,0:T(8,128)(2,1)S(1)}, u32[]{:S(2)}, u32[]{:S(2)}) collective-permute-start(bf16[2,64,384]{2,1,0:T(8,128)(2,1)S(1)} %maximum_select_fusion.1), channel_id=1, source_target_pairs={{0,12},{4,16},{8,20},{12,24},{16,28},{20,0},{24,4},{28,8},{1,13},{... | collective-permute-start | bytes 294920 | tf_op jit(solution)/shard_map/ppermute | solution.py:15
  23.2 15.8 %collective-permute-start.7 = (bf16[2,64,384]{2,1,0:T(8,128)(2,1)S(1)}, bf16[2,64,384]{2,1,0:T(8,128)(2,1)S(1)}, u32[]{:S(2)}, u32[]{:S(2)}) collective-permute-start(bf16[2,64,384]{2,1,0:T(8,128)(2,1)S(1)} %maximum_select_fusion.1), channel_id=1, source_target_pairs={{0,8},{4,12},{8,16},{12,20},{16,24},{20,28},{24,0},{28,4},{1,9},{5... | collective-permute-start | bytes 294920 | tf_op jit(solution)/shard_map/ppermute | solution.py:15
  27.1 12.0 %collective-permute-start.8 = (bf16[2,64,384]{2,1,0:T(8,128)(2,1)S(1)}, bf16[2,64,384]{2,1,0:T(8,128)(2,1)S(1)}, u32[]{:S(2)}, u32[]{:S(2)}) collective-permute-start(bf16[2,64,384]{2,1,0:T(8,128)(2,1)S(1)} %maximum_select_fusion.1), channel_id=1, source_target_pairs={{0,4},{4,8},{8,12},{12,16},{16,20},{20,24},{24,28},{28,0},{1,5},{5... | collective-permute-start | bytes 294920 | tf_op jit(solution)/shard_map/ppermute | solution.py:15
  31.2 7.8 %collective-permute-start.6 = (bf16[2,64,384]{2,1,0:T(8,128)(2,1)S(1)}, bf16[2,64,384]{2,1,0:T(8,128)(2,1)S(1)}, u32[]{:S(2)}, u32[]{:S(2)}) collective-permute-start(bf16[2,64,384]{2,1,0:T(8,128)(2,1)S(1)} %collective-permute-done.5), channel_id=1, source_target_pairs={{0,4},{4,8},{8,12},{12,16},{16,20},{20,24},{24,28},{28,0},{1,5},{5... | collective-permute-start | bytes 294920 | tf_op jit(solution)/shard_map/ppermute | solution.py:15
  40.4 19.9 %collective-permute-start.9 = (bf16[4,64,1536]{2,1,0:T(8,128)(2,1)S(1)}, bf16[4,64,1536]{2,1,0:T(8,128)(2,1)S(1)}, u32[]{:S(2)}, u32[]{:S(2)}) collective-permute-start(bf16[4,64,1536]{2,1,0:T(8,128)(2,1)S(1)} %reshape.74), channel_id=1, source_target_pairs={{0,64},{64,128},{128,192},{192,0},{1,65},{65,129},{129,193},{193,1... | collective-permute-start | bytes 2359304 | tf_op jit(solution)/shard_map/ppermute | solution.py:15
  42.0 18.2 %collective-permute-start.10 = (bf16[4,64,1536]{2,1,0:T(8,128)(2,1)S(1)}, bf16[4,64,1536]{2,1,0:T(8,128)(2,1)S(1)}, u32[]{:S(2)}, u32[]{:S(2)}) collective-permute-start(bf16[4,64,1536]{2,1,0:T(8,128)(2,1)S(1)} %reshape.74), channel_id=1, source_target_pairs={{0,192},{64,0},{128,64},{192,128},{1,193},{65,1},{129,65},{193,129... | collective-permute-start | bytes 2359304 | tf_op jit(solution)/shard_map/ppermute | solution.py:15
  60.3 9.9 %collective-permute-start.12 = (bf16[4,32,1536]{2,1,0:T(8,128)(2,1)S(1)}, bf16[4,32,1536]{2,1,0:T(8,128)(2,1)S(1)}, u32[]{:S(2)}, u32[]{:S(2)}) collective-permute-start(bf16[4,32,1536]{2,1,0:T(8,128)(2,1)S(1)} %slice.9), channel_id=1, source_target_pairs={{0,192},{64,0},{128,64},{192,128},{1,193},{65,1},{129,65},{193,129... | collective-permute-start | bytes 1179656 | tf_op jit(solution)/shard_map/ppermute | solution.py:15
  63.6 10.2 %collective-permute-start.11 = (bf16[4,32,1536]{2,1,0:T(8,128)(2,1)S(1)}, bf16[4,32,1536]{2,1,0:T(8,128)(2,1)S(1)}, u32[]{:S(2)}, u32[]{:S(2)}) collective-permute-start(bf16[4,32,1536]{2,1,0:T(8,128)(2,1)S(1)} %slice.8), channel_id=1, source_target_pairs={{0,64},{64,128},{128,192},{192,0},{1,65},{65,129},{129,193},{193,1... | collective-permute-start | bytes 1179656 | tf_op jit(solution)/shard_map/ppermute | solution.py:15
  74.9 8.2 %collective-permute-start.14 = (f32[64,256]{1,0:T(8,128)S(1)}, f32[64,256]{1,0:T(8,128)S(1)}, u32[]{:S(2)}, u32[]{:S(2)}) collective-permute-start(f32[64,256]{1,0:T(8,128)S(1)} %fusion), channel_id=1, source_target_pairs={{0,2},{2,0},{1,3},{3,1},{4,6},{6,4},{5,7},{7,5},{8,10},{10,8},{9,1... | collective-permute-start | bytes 196616 | tf_op jit(solution)/shard_map/ppermute | solution.py:15
  80.9 5.2 %collective-permute-start.15 = (f32[64,256]{1,0:T(8,128)S(1)}, f32[64,256]{1,0:T(8,128)S(1)}, u32[]{:S(2)}, u32[]{:S(2)}) collective-permute-start(f32[64,256]{1,0:T(8,128)S(1)} %fusion), channel_id=1, source_target_pairs={{0,3},{3,0},{1,2},{2,1},{4,7},{7,4},{5,6},{6,5},{8,11},{11,8},{9,1... | collective-permute-start | bytes 196616 | tf_op jit(solution)/shard_map/ppermute | solution.py:36
  80.9 5.2 %collective-permute-start.13 = (f32[64,256]{1,0:T(8,128)S(1)}, f32[64,256]{1,0:T(8,128)S(1)}, u32[]{:S(2)}, u32[]{:S(2)}) collective-permute-start(f32[64,256]{1,0:T(8,128)S(1)} %fusion), channel_id=1, source_target_pairs={{0,1},{1,0},{2,3},{3,2},{4,5},{5,4},{6,7},{7,6},{8,9},{9,8},{10,11... | collective-permute-start | bytes 196616 | tf_op jit(solution)/shard_map/ppermute | solution.py:15

commit v3 on v1

--- a/solution.py
+++ b/solution.py
@@ -43,6 +43,7 @@
         loadings.astype(jnp.float32).reshape(n_loads, groups, width // groups)
         * scales.astype(jnp.float32)[:, :, None]
     ).reshape(n_loads, width).astype(jnp.bfloat16)
+    nx = lax.axis_size("xl")
     nz = lax.axis_size("z")
     nt = lax.axis_size("xh") * lax.axis_size("core")
     pairs = []
@@ -51,11 +52,10 @@
             zh, d = divmod(z, nt)
             pairs.append((z * nt + t, (zh * nt + t) * nt + d))
     moved = lax.ppermute(scaled, ("z", "xh", "core"), pairs)
-    s1 = lax.all_gather(moved, "xl")
-    s2 = lax.all_gather(s1, "z")
-    nx = s1.shape[0]
-    s2 = s2.reshape(nz // nt, nt, nx, n_loads, width)
-    own = jnp.transpose(s2, (2, 0, 3, 1, 4)).reshape(nx * nz // nt, n_loads, nt * width)
+    copies = jnp.broadcast_to(moved[None], (nx * nz,) + moved.shape)
+    s2 = lax.all_to_all(copies, ("xl", "z"), 0, 0)
+    s2 = s2.reshape(nx, nz // nt, nt, n_loads, width)
+    own = jnp.transpose(s2, (0, 1, 3, 2, 4)).reshape(nx * nz // nt, n_loads, nt * width)
     per_y = own.shape[0]
     cov_local = cov[:, :, 0, :]
     ny = lax.axis_size("y")

time: 85.6 us -> 84 us (0.981)
  blocking collectives: 29.9 us -> 0 us
  waiting for transfers between devices: 11.1 us -> 27.8 us
  starting transfers between devices: 22.5 us -> 33 us
  local copies, waits for them, and re-layouts: 15.9 us -> 16.9 us
    all_gather x2 -> x0, blocking collectives: 29.9 us -> none  [the longest x1 25.9 us: per_device(): s2 = lax.all_gather(s1, 'z')]
    all_to_all x0 -> x1, waiting for transfers between devices: none -> 17.3 us  [per_device(): s2 = lax.all_to_all(copies, ('xl', 'z'), 0, 0)]
    all_to_all x0 -> x1, starting transfers between devices: none -> 10.7 us  [per_device(): s2 = lax.all_to_all(copies, ('xl', 'z'), 0, 0)]
    broadcast_in_dim x0 -> x1, local copies, waits for them, and re-layouts: none -> 0.98 us  [per_device(): copies = jnp.broadcast_to(moved[None], (nx * nz,) + moved.shape)]
  transfers between devices with their start and end apart: 7 -> 8, of which waited for: 5 -> 6; matrix products, arithmetic and copies ran while one was open for 20% -> 21% of each run, Pallas kernels for 0% -> 0%
where the time goes in v3:
time: 84 us; the launch traced here: 83.7 us
  starting transfers between devices  33 us (39%)
  waiting for transfers between devices  27.8 us (33%)
  local copies, waits for them, and re-layouts  16.9 us (20%)
  matrix products  4.26 us (5%)
  other arithmetic  1.52 us (2%)
    ppermute x6, starting transfers between devices, shifted(): return lax.ppermute(x, axis, [(i, (i + by) % n) for i in range(n)])  17.4 us
    all_to_all x1, waiting for transfers between devices, per_device(): s2 = lax.all_to_all(copies, ('xl', 'z'), 0, 0)  17.3 us
    dynamic_slice x1, local copies, waits for them, and re-layouts, term(): lax.dynamic_slice_in_dim(cov_local, y_from % ny * per_y, per_y, 1)  11.8 us
    all_to_all x1, starting transfers between devices, per_device(): s2 = lax.all_to_all(copies, ('xl', 'z'), 0, 0)  10.7 us
    ppermute x6, waiting for transfers between devices, shifted(): return lax.ppermute(x, axis, [(i, (i + by) % n) for i in range(n)])  8.7 us
    ppermute x1, starting transfers between devices, per_device(): moved = lax.ppermute(scaled, ('z', 'xh', 'core'), pairs)  4.94 us
    dot_general x4, matrix products, term(): lax.dot_general(block, cov_part, (((0, 2), (1, 2)), ((), ())), preferred_...  4.26 us
    unnamed x4, local copies, waits for them, and re-layouts  2.28 us
  transfers between devices with their start and end apart: 8, of which 6 were waited for; matrix products, arithmetic and copies ran while one was open for 21% of the time, Pallas kernels for 0%

profile of v3, /device:TPU:1, one launch (start us, length us, event | category | flops | bytes accessed | tf_op | source)
XLA Modules:
  0.0 83.7 jit_solution(8756875784884512232)
XLA Ops:
  0.0 0.8 copy.10
  0.9 0.8 fusion.3
  1.7 4.9 %collective-permute-start = (bf16[64,384]{1,0:T(8,128)(2,1)S(1)}, bf16[64,384]{1,0:T(8,128)(2,1)S(1)}, u32[]{:S(2)}, u32[]{:S(2)}) collective-permute-start(bf16[64,384]{1,0:T(8,128)(2,1)S(1)} %fusion.3), channel_id=1, source_target_pairs={{0,0},{1,4},{2,8},{3,12},{4,1},{5,5},{6,9},{7,13},{8,2},{9,6},{10,... | collective-permute-start | bytes 147464 | tf_op jit(solution)/shard_map/ppermute | solution.py:54
  6.7 1.8 %collective-permute-done = bf16[64,384]{1,0:T(8,128)(2,1)S(1)} collective-permute-done((bf16[64,384]{1,0:T(8,128)(2,1)S(1)}, bf16[64,384]{1,0:T(8,128)(2,1)S(1)}, u32[]{:S(2)}, u32[]{:S(2)}) %collective-permute-start) | collective-permute-done | bytes 49184 | tf_op jit(solution)/shard_map/ppermute | solution.py:54
  8.4 1.0 %broadcast_in_dim.2 = bf16[16,64,384]{2,1,0:T(8,128)(2,1)} broadcast(bf16[64,384]{1,0:T(8,128)(2,1)S(1)} %collective-permute-done), dimensions={1,2} | broadcast | bytes 835584 | tf_op jit(solution)/shard_map/broadcast_in_dim | solution.py:55
  9.4 10.7 %all-to-all-start = ((bf16[16,64,384]{2,1,0:T(8,128)(2,1)}), bf16[16,64,384]{2,1,0:T(8,128)(2,1)S(1)}, u32[]{:S(2)}, u32[]{:S(2)}) async-start(bf16[16,64,384]{2,1,0:T(8,128)(2,1)} %broadcast_in_dim.2), calls=%async_computation | async-start | bytes 1572864 | tf_op jit(solution)/shard_map/all_to_all | solution.py:56
  20.2 17.3 %all-to-all-done = bf16[16,64,384]{2,1,0:T(8,128)(2,1)S(1)} async-done(((bf16[16,64,384]{2,1,0:T(8,128)(2,1)}), bf16[16,64,384]{2,1,0:T(8,128)(2,1)S(1)}, u32[]{:S(2)}, u32[]{:S(2)}) %all-to-all-start) | async-done | bytes 786464 | tf_op jit(solution)/shard_map/all_to_all | solution.py:56
  37.5 0.6 copy.11
  38.4 1.4 %collective-permute-start.1 = (bf16[4,64,1536]{2,1,0:T(8,128)(2,1)S(1)}, bf16[4,64,1536]{2,1,0:T(8,128)(2,1)S(1)}, u32[]{:S(2)}, u32[]{:S(2)}) collective-permute-start(bf16[4,64,1536]{2,1,0:T(8,128)(2,1)S(1)} %reshape.16), channel_id=1, source_target_pairs={{0,64},{64,128},{128,192},{192,0},{1,65},{65,129},{129,193},{193,1... | collective-permute-start | bytes 2359304 | tf_op jit(solution)/shard_map/ppermute | solution.py:15
  39.8 1.5 %collective-permute-start.2 = (bf16[4,64,1536]{2,1,0:T(8,128)(2,1)S(1)}, bf16[4,64,1536]{2,1,0:T(8,128)(2,1)S(1)}, u32[]{:S(2)}, u32[]{:S(2)}) collective-permute-start(bf16[4,64,1536]{2,1,0:T(8,128)(2,1)S(1)} %reshape.16), channel_id=1, source_target_pairs={{0,192},{64,0},{128,64},{192,128},{1,193},{65,1},{129,65},{193,129... | collective-permute-start | bytes 2359304 | tf_op jit(solution)/shard_map/ppermute | solution.py:15
  41.3 11.8 %constant_dynamic-slice_fusion = (bf16[256,4,1,1536]{3,1,2,0:T(4,128)(2,1)S(1)}, bf16[256,4,1,1536]{3,1,2,0:T(4,128)(2,1)S(1)}, bf16[256,4,1,1536]{3,1,2,0:T(4,128)(2,1)S(1)}, bf16[256,4,1,1536]{3,1,2,0:T(4,128)(2,1)S(1)}) fusion(bf16[256,16,1,1536]{3,1,2,0:T(8,128)(2,1)} %param.5, s32[]{:T(128)S(6)} %select_n.38, s32[]{:T(128)S(6)} %select_n.36, ...), kind=kLoop, calls=%fused_computation.14 | loop fusion | bytes 25165840 | tf_op jit(solution)/shard_map/dynamic_slice | solution.py:65
  53.1 0.6 copy.29
  55.5 1.1 %convolution_bitcast_fusion.3 = f32[64,256]{1,0:T(8,128)S(1)} fusion(bf16[4,64,1536]{2,1,0:T(8,128)(2,1)S(1)} %reshape.16, bf16[256,4,1536]{2,0,1:T(8,128)(2,1)S(1)} %bitcast.42), kind=kOutput, calls=%fused_computation.10 | convolution fusion | flops 201326592 | bytes 3997696 | tf_op jit(solution)/shard_map/dot_general | solution.py:67
  56.6 1.5 %collective-permute-start.4 = (bf16[4,32,1536]{2,1,0:T(8,128)(2,1)S(1)}, bf16[4,32,1536]{2,1,0:T(8,128)(2,1)S(1)}, u32[]{:S(2)}, u32[]{:S(2)}) collective-permute-start(bf16[4,32,1536]{2,1,0:T(8,128)(2,1)S(1)} %slice.9), channel_id=1, source_target_pairs={{0,192},{64,0},{128,64},{192,128},{1,193},{65,1},{129,65},{193,129... | collective-permute-start | bytes 1179656 | tf_op jit(solution)/shard_map/ppermute | solution.py:15
  58.2 1.1 %fusion.2 = f32[64,256]{1,0:T(8,128)S(1)} fusion(f32[64,256]{1,0:T(8,128)S(1)} %convolution_bitcast_fusion.3, bf16[4,64,1536]{2,1,0:T(8,128)(2,1)S(1)} %collective-permute-done.1, bf16[256,4,1536]{2,0,1:T(8,128)(2,1)S(1)} %bitcast.45), kind=kOutput, calls=%fused_computation.9 | convolution fusion | flops 201342976 | bytes 4063232 | tf_op jit(solution)/shard_map/dot_general | solution.py:67
  59.3 1.1 %fusion.1 = f32[64,256]{1,0:T(8,128)S(1)} fusion(f32[64,256]{1,0:T(8,128)S(1)} %fusion.2, bf16[4,64,1536]{2,1,0:T(8,128)(2,1)S(1)} %collective-permute-done.2, bf16[256,4,1536]{2,0,1:T(8,128)(2,1)S(1)} %bitcast.44), kind=kOutput, calls=%fused_computation.7 | convolution fusion | flops 201342976 | bytes 4063232 | tf_op jit(solution)/shard_map/dot_general | solution.py:67
  60.4 2.9 %collective-permute-done.4 = bf16[4,32,1536]{2,1,0:T(8,128)(2,1)S(1)} collective-permute-done((bf16[4,32,1536]{2,1,0:T(8,128)(2,1)S(1)}, bf16[4,32,1536]{2,1,0:T(8,128)(2,1)S(1)}, u32[]{:S(2)}, u32[]{:S(2)}) %collective-permute-start.4) | collective-permute-done | bytes 393248 | tf_op jit(solution)/shard_map/ppermute | solution.py:15
  63.3 2.7 %collective-permute-done.3 = bf16[4,32,1536]{2,1,0:T(8,128)(2,1)S(1)} collective-permute-done((bf16[4,32,1536]{2,1,0:T(8,128)(2,1)S(1)}, bf16[4,32,1536]{2,1,0:T(8,128)(2,1)S(1)}, u32[]{:S(2)}, u32[]{:S(2)}) %collective-permute-start.3) | collective-permute-done | bytes 393248 | tf_op jit(solution)/shard_map/ppermute | solution.py:15
  66.0 1.1 %fusion = f32[64,256]{1,0:T(8,128)S(1)} fusion(f32[64,256]{1,0:T(8,128)S(1)} %fusion.1, bf16[4,64,1536]{2,1,0:T(8,128)(2,1)S(1)} %pad_maximum_fusion, bf16[256,4,1536]{2,0,1:T(8,128)(2,1)S(1)} %bitcast.43), kind=kOutput, calls=%fused_computation.5 | convolution fusion | flops 201342976 | bytes 4063232 | tf_op jit(solution)/shard_map/dot_general | solution.py:67
  67.1 6.7 %collective-permute-start.5 = (f32[64,256]{1,0:T(8,128)S(1)}, f32[64,256]{1,0:T(8,128)S(1)}, u32[]{:S(2)}, u32[]{:S(2)}) collective-permute-start(f32[64,256]{1,0:T(8,128)S(1)} %fusion), channel_id=1, source_target_pairs={{0,1},{1,0},{2,3},{3,2},{4,5},{5,4},{6,7},{7,6},{8,9},{9,8},{10,11... | collective-permute-start | bytes 196616 | tf_op jit(solution)/shard_map/ppermute | solution.py:15
  73.8 0.9 %collective-permute-done.5 = f32[64,256]{1,0:T(8,128)S(1)} collective-permute-done((f32[64,256]{1,0:T(8,128)S(1)}, f32[64,256]{1,0:T(8,128)S(1)}, u32[]{:S(2)}, u32[]{:S(2)}) %collective-permute-start.5) | collective-permute-done | bytes 65568 | tf_op jit(solution)/shard_map/ppermute | solution.py:15
  74.8 6.2 %collective-permute-start.6 = (f32[64,256]{1,0:T(8,128)S(1)}, f32[64,256]{1,0:T(8,128)S(1)}, u32[]{:S(2)}, u32[]{:S(2)}) collective-permute-start(f32[64,256]{1,0:T(8,128)S(1)} %add.60), channel_id=1, source_target_pairs={{0,2},{2,0},{1,3},{3,1},{4,6},{6,4},{5,7},{7,5},{8,10},{10,8},{9,1... | collective-permute-start | bytes 196616 | tf_op jit(solution)/shard_map/ppermute | solution.py:15
  80.9 2.2 %collective-permute-done.6 = f32[64,256]{1,0:T(8,128)S(1)} collective-permute-done((f32[64,256]{1,0:T(8,128)S(1)}, f32[64,256]{1,0:T(8,128)S(1)}, u32[]{:S(2)}, u32[]{:S(2)}) %collective-permute-start.6) | collective-permute-done | bytes 65568 | tf_op jit(solution)/shard_map/ppermute | solution.py:15
  83.1 0.6 add.61
  (12 shorter events, 2.4 us)
Async XLA Ops:
  1.7 6.7 %collective-permute-start = (bf16[64,384]{1,0:T(8,128)(2,1)S(1)}, bf16[64,384]{1,0:T(8,128)(2,1)S(1)}, u32[]{:S(2)}, u32[]{:S(2)}) collective-permute-start(bf16[64,384]{1,0:T(8,128)(2,1)S(1)} %fusion.3), channel_id=1, source_target_pairs={{0,0},{1,4},{2,8},{3,12},{4,1},{5,5},{6,9},{7,13},{8,2},{9,6},{10,... | collective-permute-start | bytes 147464 | tf_op jit(solution)/shard_map/ppermute | solution.py:54
  9.4 28.1 %all-to-all-start = ((bf16[16,64,384]{2,1,0:T(8,128)(2,1)}), bf16[16,64,384]{2,1,0:T(8,128)(2,1)S(1)}, u32[]{:S(2)}, u32[]{:S(2)}) async-start(bf16[16,64,384]{2,1,0:T(8,128)(2,1)} %broadcast_in_dim.2), calls=%async_computation | async-start | bytes 1572864 | tf_op jit(solution)/shard_map/all_to_all | solution.py:56
  38.4 18.1 %collective-permute-start.1 = (bf16[4,64,1536]{2,1,0:T(8,128)(2,1)S(1)}, bf16[4,64,1536]{2,1,0:T(8,128)(2,1)S(1)}, u32[]{:S(2)}, u32[]{:S(2)}) collective-permute-start(bf16[4,64,1536]{2,1,0:T(8,128)(2,1)S(1)} %reshape.16), channel_id=1, source_target_pairs={{0,64},{64,128},{128,192},{192,0},{1,65},{65,129},{129,193},{193,1... | collective-permute-start | bytes 2359304 | tf_op jit(solution)/shard_map/ppermute | solution.py:15
  39.8 16.7 %collective-permute-start.2 = (bf16[4,64,1536]{2,1,0:T(8,128)(2,1)S(1)}, bf16[4,64,1536]{2,1,0:T(8,128)(2,1)S(1)}, u32[]{:S(2)}, u32[]{:S(2)}) collective-permute-start(bf16[4,64,1536]{2,1,0:T(8,128)(2,1)S(1)} %reshape.16), channel_id=1, source_target_pairs={{0,192},{64,0},{128,64},{192,128},{1,193},{65,1},{129,65},{193,129... | collective-permute-start | bytes 2359304 | tf_op jit(solution)/shard_map/ppermute | solution.py:15
  56.6 6.7 %collective-permute-start.4 = (bf16[4,32,1536]{2,1,0:T(8,128)(2,1)S(1)}, bf16[4,32,1536]{2,1,0:T(8,128)(2,1)S(1)}, u32[]{:S(2)}, u32[]{:S(2)}) collective-permute-start(bf16[4,32,1536]{2,1,0:T(8,128)(2,1)S(1)} %slice.9), channel_id=1, source_target_pairs={{0,192},{64,0},{128,64},{192,128},{1,193},{65,1},{129,65},{193,129... | collective-permute-start | bytes 1179656 | tf_op jit(solution)/shard_map/ppermute | solution.py:15
  58.1 7.9 %collective-permute-start.3 = (bf16[4,32,1536]{2,1,0:T(8,128)(2,1)S(1)}, bf16[4,32,1536]{2,1,0:T(8,128)(2,1)S(1)}, u32[]{:S(2)}, u32[]{:S(2)}) collective-permute-start(bf16[4,32,1536]{2,1,0:T(8,128)(2,1)S(1)} %slice.8), channel_id=1, source_target_pairs={{0,64},{64,128},{128,192},{192,0},{1,65},{65,129},{129,193},{193,1... | collective-permute-start | bytes 1179656 | tf_op jit(solution)/shard_map/ppermute | solution.py:15
  67.1 7.6 %collective-permute-start.5 = (f32[64,256]{1,0:T(8,128)S(1)}, f32[64,256]{1,0:T(8,128)S(1)}, u32[]{:S(2)}, u32[]{:S(2)}) collective-permute-start(f32[64,256]{1,0:T(8,128)S(1)} %fusion), channel_id=1, source_target_pairs={{0,1},{1,0},{2,3},{3,2},{4,5},{5,4},{6,7},{7,6},{8,9},{9,8},{10,11... | collective-permute-start | bytes 196616 | tf_op jit(solution)/shard_map/ppermute | solution.py:15
  74.8 8.3 %collective-permute-start.6 = (f32[64,256]{1,0:T(8,128)S(1)}, f32[64,256]{1,0:T(8,128)S(1)}, u32[]{:S(2)}, u32[]{:S(2)}) collective-permute-start(f32[64,256]{1,0:T(8,128)S(1)} %add.60), channel_id=1, source_target_pairs={{0,2},{2,0},{1,3},{3,1},{4,6},{6,4},{5,7},{7,5},{8,10},{10,8},{9,1... | collective-permute-start | bytes 196616 | tf_op jit(solution)/shard_map/ppermute | solution.py:15

commit v4 on v3

--- a/solution.py
+++ b/solution.py
@@ -52,14 +52,10 @@
             zh, d = divmod(z, nt)
             pairs.append((z * nt + t, (zh * nt + t) * nt + d))
     moved = lax.ppermute(scaled, ("z", "xh", "core"), pairs)
-    copies = jnp.broadcast_to(moved[None], (nx * nz,) + moved.shape)
-    s2 = lax.all_to_all(copies, ("xl", "z"), 0, 0)
-    s2 = s2.reshape(nx, nz // nt, nt, n_loads, width)
-    own = jnp.transpose(s2, (0, 1, 3, 2, 4)).reshape(nx * nz // nt, n_loads, nt * width)
-    per_y = own.shape[0]
     cov_local = cov[:, :, 0, :]
     ny = lax.axis_size("y")
     me = lax.axis_index("y")
+    per_y = nx * nz // nt
 
     def term(block, y_from):
         cov_part = lax.dynamic_slice_in_dim(cov_local, (y_from % ny) * per_y, per_y, 1)
@@ -68,17 +64,33 @@
             block, cov_part, (((0, 2), (1, 2)), ((), ())), preferred_element_type=jnp.float32
         )
 
-    fwd = shifted(own, "y", 1)
-    bwd = shifted(own, "y", -1)
-    part = term(own, me)
-    part = part + term(fwd, me - 1)
-    part = part + term(bwd, me + 1)
-    half = n_loads // 2
-    far_a = shifted(fwd[:, :half], "y", 1)
-    far_b = shifted(bwd[:, half:], "y", -1)
-    far = jnp.concatenate([far_a, far_b], axis=1)
-    part = part + term(far, me + 2)
-    return team_sum(part)
+    def gather_z(piece):
+        rows = piece.shape[0]
+        copies = jnp.broadcast_to(piece[None], (nx * nz,) + piece.shape)
+        s2 = lax.all_to_all(copies, ("xl", "z"), 0, 0)
+        s2 = s2.reshape(nx, nz // nt, nt, rows, width)
+        return jnp.transpose(s2, (0, 1, 3, 2, 4)).reshape(per_y, rows, nt * width)
+
+    def ring_y(own):
+        rows = own.shape[1]
+        fwd = shifted(own, "y", 1)
+        bwd = shifted(own, "y", -1)
+        part = term(own, me)
+        part = part + term(fwd, me - 1)
+        part = part + term(bwd, me + 1)
+        half = rows // 2
+        far_a = shifted(fwd[:, :half], "y", 1)
+        far_b = shifted(bwd[:, half:], "y", -1)
+        far = jnp.concatenate([far_a, far_b], axis=1)
+        return team_sum(part + term(far, me + 2))
+
+    split = n_loads // 2
+    own_a = gather_z(moved[:split])
+    own_a, rest = lax.optimization_barrier((own_a, moved[split:]))
+    out_a = ring_y(own_a)
+    own_b = gather_z(rest)
+    out_b = ring_y(own_b)
+    return jnp.concatenate([out_a, out_b], axis=0)
 
 
 def solution(mesh):

time: 84 us -> 111 us (1.32)
  starting transfers between devices: 33 us -> 47.8 us
  matrix products: 4.26 us -> 16.7 us
  waiting for transfers between devices: 27.8 us -> 16.7 us
  local copies, waits for them, and re-layouts: 16.9 us -> 26.9 us
    dot_general x4 -> x8, matrix products: 4.26 us -> 16.7 us  [term(): lax.dot_general(block, cov_part, (((0, 2), (1, 2)), ((), ())), preferred_...]
    all_to_all x1 -> x2, waiting for transfers between devices: 17.3 us -> 9.1 us  [gather_z(): s2 = lax.all_to_all(copies, ('xl', 'z'), 0, 0)]
    ppermute x6 -> x12, starting transfers between devices: 17.4 us -> 25.2 us  [shifted(): return lax.ppermute(x, axis, [(i, (i + by) % n) for i in range(n)])]
    all_to_all x1 -> x2, starting transfers between devices: 10.7 us -> 17.6 us  [gather_z(): s2 = lax.all_to_all(copies, ('xl', 'z'), 0, 0)]
    unnamed x4 -> x10, local copies, waits for them, and re-layouts: 2.28 us -> 7.34 us
    ppermute x6 -> x12, waiting for transfers between devices: 8.7 us -> 5.88 us  [shifted(): return lax.ppermute(x, axis, [(i, (i + by) % n) for i in range(n)])]
    slice x2 -> x5, local copies, waits for them, and re-layouts: 0.05 us -> 1.92 us  [the longest x2 0.96 us: ring_y(): far_a = shifted(fwd[:, :half], 'y', 1)]
    reshape x1 -> x2, local copies, waits for them, and re-layouts: 0.3 us -> 2.06 us  [gather_z(): return jnp.transpose(s2, (0, 1, 3, 2, 4)).reshape(per_y, rows, nt * width)]
  transfers between devices with their start and end apart: 8 -> 15, of which waited for: 6 -> 6; matrix products, arithmetic and copies ran while one was open for 21% -> 36% of each run, Pallas kernels for 0% -> 0%
where the time goes in v4:
time: 111 us
  starting transfers between devices  47.8 us (43%)
  local copies, waits for them, and re-layouts  26.9 us (24%)
  waiting for transfers between devices  16.7 us (15%)
  matrix products  16.7 us (15%)
  other arithmetic  2.29 us (2%)
    ppermute x12, starting transfers between devices, shifted(): return lax.ppermute(x, axis, [(i, (i + by) % n) for i in range(n)])  25.2 us
    all_to_all x2, starting transfers between devices, gather_z(): s2 = lax.all_to_all(copies, ('xl', 'z'), 0, 0)  17.6 us
    dot_general x8, matrix products, term(): lax.dot_general(block, cov_part, (((0, 2), (1, 2)), ((), ())), preferred_...  16.7 us
    dynamic_slice x1, local copies, waits for them, and re-layouts, term(): lax.dynamic_slice_in_dim(cov_local, y_from % ny * per_y, per_y, 1)  11.9 us
    all_to_all x2, waiting for transfers between devices, gather_z(): s2 = lax.all_to_all(copies, ('xl', 'z'), 0, 0)  9.1 us
    unnamed x10, local copies, waits for them, and re-layouts  7.34 us
    ppermute x12, waiting for transfers between devices, shifted(): return lax.ppermute(x, axis, [(i, (i + by) % n) for i in range(n)])  5.88 us
    ppermute x1, starting transfers between devices, per_device(): moved = lax.ppermute(scaled, ('z', 'xh', 'core'), pairs)  4.94 us
  transfers between devices with their start and end apart: 15, of which 6 were waited for; matrix products, arithmetic and copies ran while one was open for 36% of the time, Pallas kernels for 0%

profile of v4, /device:TPU:1, one launch (start us, length us, event | category | flops | bytes accessed | tf_op | source)
XLA Modules:
  0.0 110.8 jit_solution(4894479197761907218)
XLA Ops:
  1.7 4.9 %collective-permute-start = (bf16[64,384]{1,0:T(8,128)(2,1)S(1)}, bf16[64,384]{1,0:T(8,128)(2,1)S(1)}, u32[]{:S(2)}, u32[]{:S(2)}) collective-permute-start(bf16[64,384]{1,0:T(8,128)(2,1)S(1)} %fusion.6), channel_id=1, source_target_pairs={{0,0},{1,4},{2,8},{3,12},{4,1},{5,5},{6,9},{7,13},{8,2},{9,6},{10,... | collective-permute-start | bytes 147464 | tf_op jit(solution)/shard_map/ppermute | solution.py:54
  6.7 1.8 %collective-permute-done = bf16[64,384]{1,0:T(8,128)(2,1)S(1)} collective-permute-done((bf16[64,384]{1,0:T(8,128)(2,1)S(1)}, bf16[64,384]{1,0:T(8,128)(2,1)S(1)}, u32[]{:S(2)}, u32[]{:S(2)}) %collective-permute-start) | collective-permute-done | bytes 49184 | tf_op jit(solution)/shard_map/ppermute | solution.py:54
  9.2 10.7 %all-to-all-start = ((bf16[16,32,384]{2,1,0:T(8,128)(2,1)}), bf16[16,32,384]{2,1,0:T(8,128)(2,1)S(1)}, u32[]{:S(2)}, u32[]{:S(2)}) async-start(bf16[16,32,384]{2,1,0:T(8,128)(2,1)} %broadcast_in_dim.4), calls=%async_computation | async-start | bytes 786432 | tf_op jit(solution)/shard_map/all_to_all | solution.py:70
  20.0 9.1 %all-to-all-done = bf16[16,32,384]{2,1,0:T(8,128)(2,1)S(1)} async-done(((bf16[16,32,384]{2,1,0:T(8,128)(2,1)}), bf16[16,32,384]{2,1,0:T(8,128)(2,1)S(1)}, u32[]{:S(2)}, u32[]{:S(2)}) %all-to-all-start) | async-done | bytes 393248 | tf_op jit(solution)/shard_map/all_to_all | solution.py:70
  30.2 1.3 %collective-permute-start.1 = (bf16[4,32,1536]{2,1,0:T(8,128)(2,1)}, bf16[4,32,1536]{2,1,0:T(8,128)(2,1)}, u32[]{:S(2)}, u32[]{:S(2)}) collective-permute-start(bf16[4,32,1536]{2,1,0:T(8,128)(2,1)} %reshape.23), channel_id=1, source_target_pairs={{0,64},{64,128},{128,192},{192,0},{1,65},{65,129},{129,193},{193,1... | collective-permute-start | bytes 1179656 | tf_op jit(solution)/shard_map/ppermute | solution.py:15
  31.5 1.4 %collective-permute-start.2 = (bf16[4,32,1536]{2,1,0:T(8,128)(2,1)}, bf16[4,32,1536]{2,1,0:T(8,128)(2,1)}, u32[]{:S(2)}, u32[]{:S(2)}) collective-permute-start(bf16[4,32,1536]{2,1,0:T(8,128)(2,1)} %reshape.23), channel_id=1, source_target_pairs={{0,192},{64,0},{128,64},{192,128},{1,193},{65,1},{129,65},{193,129... | collective-permute-start | bytes 1179656 | tf_op jit(solution)/shard_map/ppermute | solution.py:15
  32.9 11.9 %constant_dynamic-slice_fusion = (bf16[256,4,1,1536]{3,1,2,0:T(4,128)(2,1)S(1)}, bf16[256,4,1,1536]{3,1,2,0:T(4,128)(2,1)S(1)}, bf16[256,4,1,1536]{3,1,2,0:T(4,128)(2,1)S(1)}, bf16[256,4,1,1536]{3,1,2,0:T(4,128)(2,1)S(1)}) fusion(bf16[256,16,1,1536]{3,1,2,0:T(8,128)(2,1)} %param.5, s32[]{:T(128)S(6)} %select_n.50, s32[]{:T(128)S(6)} %select_n.48, ...), kind=kLoop, calls=%fused_computation.23 | loop fusion | bytes 25165840 | tf_op jit(solution)/shard_map/dynamic_slice | solution.py:61
  44.9 2.2 %copy.30 = bf16[256,4,1,1536]{3,0,2,1:T(8,128)(2,1)} copy(bf16[256,4,1,1536]{3,1,2,0:T(4,128)(2,1)S(1)} %get-tuple-element.44) | data formatting | bytes 6291456
  47.1 2.3 %copy.29 = bf16[256,4,1,1536]{3,0,2,1:T(8,128)(2,1)} copy(bf16[256,4,1,1536]{3,1,2,0:T(4,128)(2,1)S(1)} %get-tuple-element.43) | data formatting | bytes 6291456
  49.3 2.3 %copy.28 = bf16[256,4,1,1536]{3,0,2,1:T(8,128)(2,1)} copy(bf16[256,4,1,1536]{3,1,2,0:T(4,128)(2,1)S(1)} %get-tuple-element.42) | data formatting | bytes 6291456
  53.0 7.0 %all-to-all-start.1 = ((bf16[16,32,384]{2,1,0:T(8,128)(2,1)}), bf16[16,32,384]{2,1,0:T(8,128)(2,1)S(1)}, u32[]{:S(2)}, u32[]{:S(2)}) async-start(bf16[16,32,384]{2,1,0:T(8,128)(2,1)} %broadcast_in_dim.5), calls=%async_computation.1 | async-start | bytes 786432 | tf_op jit(solution)/shard_map/all_to_all | solution.py:70
  60.0 3.2 %convolution_bitcast_fusion.7 = f32[32,256]{1,0:T(8,128)S(1)} fusion(bf16[4,32,1536]{2,1,0:T(8,128)(2,1)} %reshape.23, bf16[256,4,1536]{2,0,1:T(8,128)(2,1)} %bitcast.73), kind=kOutput, calls=%fused_computation.17 | convolution fusion | flops 100663296 | bytes 3571712 | tf_op jit(solution)/shard_map/dot_general | solution.py:63
  65.2 2.7 %collective-permute-start.4 = (bf16[4,16,1536]{2,1,0:T(8,128)(2,1)S(1)}, bf16[4,16,1536]{2,1,0:T(8,128)(2,1)S(1)}, u32[]{:S(2)}, u32[]{:S(2)}) collective-permute-start(bf16[4,16,1536]{2,1,0:T(8,128)(2,1)S(1)} %slice.27), channel_id=1, source_target_pairs={{0,192},{64,0},{128,64},{192,128},{1,193},{65,1},{129,65},{193,129... | collective-permute-start | bytes 589832 | tf_op jit(solution)/shard_map/ppermute | solution.py:15
  67.9 3.0 %fusion.5 = f32[32,256]{1,0:T(8,128)S(1)} fusion(f32[32,256]{1,0:T(8,128)S(1)} %convolution_bitcast_fusion.7, bf16[4,32,1536]{2,1,0:T(8,128)(2,1)} %collective-permute-done.1, bf16[256,4,1536]{2,0,1:T(8,128)(2,1)} %bitcast.71), kind=kOutput, calls=%fused_computation.16 | convolution fusion | flops 100671488 | bytes 3604480 | tf_op jit(solution)/shard_map/dot_general | solution.py:63
  70.9 2.6 %fusion.4 = f32[32,256]{1,0:T(8,128)} fusion(f32[32,256]{1,0:T(8,128)S(1)} %fusion.5, bf16[4,32,1536]{2,1,0:T(8,128)(2,1)} %collective-permute-done.2, bf16[256,4,1536]{2,0,1:T(8,128)(2,1)S(1)} %bitcast.69), kind=kOutput, calls=%fused_computation.14 | convolution fusion | flops 100671488 | bytes 3604480 | tf_op jit(solution)/shard_map/dot_general | solution.py:63
  76.6 2.7 %collective-permute-start.8 = (bf16[4,32,1536]{2,1,0:T(8,128)(2,1)S(1)}, bf16[4,32,1536]{2,1,0:T(8,128)(2,1)S(1)}, u32[]{:S(2)}, u32[]{:S(2)}) collective-permute-start(bf16[4,32,1536]{2,1,0:T(8,128)(2,1)S(1)} %reshape.25), channel_id=1, source_target_pairs={{0,192},{64,0},{128,64},{192,128},{1,193},{65,1},{129,65},{193,129... | collective-permute-start | bytes 1179656 | tf_op jit(solution)/shard_map/ppermute | solution.py:15
  79.2 2.0 %fusion.3 = f32[32,256]{1,0:T(8,128)S(1)} fusion(f32[32,256]{1,0:T(8,128)} %fusion.4, bf16[4,32,1536]{2,1,0:T(8,128)(2,1)} %pad_maximum_fusion, bf16[256,4,1536]{2,0,1:T(8,128)(2,1)S(1)} %bitcast.67), kind=kOutput, calls=%fused_computation.12 | convolution fusion | flops 100671488 | bytes 3604480 | tf_op jit(solution)/shard_map/dot_general | solution.py:63
  81.3 4.0 %collective-permute-start.5 = (f32[32,256]{1,0:T(8,128)S(1)}, f32[32,256]{1,0:T(8,128)S(1)}, u32[]{:S(2)}, u32[]{:S(2)}) collective-permute-start(f32[32,256]{1,0:T(8,128)S(1)} %fusion.3), channel_id=1, source_target_pairs={{0,1},{1,0},{2,3},{3,2},{4,5},{5,4},{6,7},{7,6},{8,9},{9,8},{10,11... | collective-permute-start | bytes 98312 | tf_op jit(solution)/shard_map/ppermute | solution.py:15
  85.2 2.9 %convolution_bitcast_fusion.3 = f32[32,256]{1,0:T(8,128)S(1)} fusion(bf16[4,32,1536]{2,1,0:T(8,128)(2,1)S(1)} %reshape.25, bf16[256,4,1536]{2,0,1:T(8,128)(2,1)} %bitcast.74), kind=kOutput, calls=%fused_computation.10 | convolution fusion | flops 100663296 | bytes 3571712 | tf_op jit(solution)/shard_map/dot_general | solution.py:63
  88.3 1.5 %collective-permute-start.9 = (bf16[4,16,1536]{2,1,0:T(8,128)(2,1)S(1)}, bf16[4,16,1536]{2,1,0:T(8,128)(2,1)S(1)}, u32[]{:S(2)}, u32[]{:S(2)}) collective-permute-start(bf16[4,16,1536]{2,1,0:T(8,128)(2,1)S(1)} %slice.28), channel_id=1, source_target_pairs={{0,64},{64,128},{128,192},{192,0},{1,65},{65,129},{129,193},{193,1... | collective-permute-start | bytes 589832 | tf_op jit(solution)/shard_map/ppermute | solution.py:15
  91.9 1.7 %collective-permute-done.10 = bf16[4,16,1536]{2,1,0:T(8,128)(2,1)S(1)} collective-permute-done((bf16[4,16,1536]{2,1,0:T(8,128)(2,1)S(1)}, bf16[4,16,1536]{2,1,0:T(8,128)(2,1)S(1)}, u32[]{:S(2)}, u32[]{:S(2)}) %collective-permute-start.10) | collective-permute-done | bytes 196640 | tf_op jit(solution)/shard_map/ppermute | solution.py:15
  95.1 5.3 %collective-permute-start.11 = (f32[32,256]{1,0:T(8,128)S(1)}, f32[32,256]{1,0:T(8,128)S(1)}, u32[]{:S(2)}, u32[]{:S(2)}) collective-permute-start(f32[32,256]{1,0:T(8,128)S(1)} %fusion), channel_id=1, source_target_pairs={{0,1},{1,0},{2,3},{3,2},{4,5},{5,4},{6,7},{7,6},{8,9},{9,8},{10,11... | collective-permute-start | bytes 98312 | tf_op jit(solution)/shard_map/ppermute | solution.py:15
  100.5 5.3 %collective-permute-start.6 = (f32[32,256]{1,0:T(8,128)S(1)}, f32[32,256]{1,0:T(8,128)S(1)}, u32[]{:S(2)}, u32[]{:S(2)}) collective-permute-start(f32[32,256]{1,0:T(8,128)S(1)} %add.85), channel_id=1, source_target_pairs={{0,2},{2,0},{1,3},{3,1},{4,6},{6,4},{5,7},{7,5},{8,10},{10,8},{9,1... | collective-permute-start | bytes 98312 | tf_op jit(solution)/shard_map/ppermute | solution.py:15
  107.5 2.6 %collective-permute-done.12 = f32[32,256]{1,0:T(8,128)S(1)} collective-permute-done((f32[32,256]{1,0:T(8,128)S(1)}, f32[32,256]{1,0:T(8,128)S(1)}, u32[]{:S(2)}, u32[]{:S(2)}) %collective-permute-start.12) | collective-permute-done | bytes 32800 | tf_op jit(solution)/shard_map/ppermute | solution.py:15
  (46 shorter events, 16.1 us)
Async XLA Ops:
  1.7 6.7 %collective-permute-start = (bf16[64,384]{1,0:T(8,128)(2,1)S(1)}, bf16[64,384]{1,0:T(8,128)(2,1)S(1)}, u32[]{:S(2)}, u32[]{:S(2)}) collective-permute-start(bf16[64,384]{1,0:T(8,128)(2,1)S(1)} %fusion.6), channel_id=1, source_target_pairs={{0,0},{1,4},{2,8},{3,12},{4,1},{5,5},{6,9},{7,13},{8,2},{9,6},{10,... | collective-permute-start | bytes 147464 | tf_op jit(solution)/shard_map/ppermute | solution.py:54
  9.2 19.8 %all-to-all-start = ((bf16[16,32,384]{2,1,0:T(8,128)(2,1)}), bf16[16,32,384]{2,1,0:T(8,128)(2,1)S(1)}, u32[]{:S(2)}, u32[]{:S(2)}) async-start(bf16[16,32,384]{2,1,0:T(8,128)(2,1)} %broadcast_in_dim.4), calls=%async_computation | async-start | bytes 786432 | tf_op jit(solution)/shard_map/all_to_all | solution.py:70
  30.2 32.9 %collective-permute-start.1 = (bf16[4,32,1536]{2,1,0:T(8,128)(2,1)}, bf16[4,32,1536]{2,1,0:T(8,128)(2,1)}, u32[]{:S(2)}, u32[]{:S(2)}) collective-permute-start(bf16[4,32,1536]{2,1,0:T(8,128)(2,1)} %reshape.23), channel_id=1, source_target_pairs={{0,64},{64,128},{128,192},{192,0},{1,65},{65,129},{129,193},{193,1... | collective-permute-start | bytes 1179656 | tf_op jit(solution)/shard_map/ppermute | solution.py:15
  31.5 31.7 %collective-permute-start.2 = (bf16[4,32,1536]{2,1,0:T(8,128)(2,1)}, bf16[4,32,1536]{2,1,0:T(8,128)(2,1)}, u32[]{:S(2)}, u32[]{:S(2)}) collective-permute-start(bf16[4,32,1536]{2,1,0:T(8,128)(2,1)} %reshape.23), channel_id=1, source_target_pairs={{0,192},{64,0},{128,64},{192,128},{1,193},{65,1},{129,65},{193,129... | collective-permute-start | bytes 1179656 | tf_op jit(solution)/shard_map/ppermute | solution.py:15
  53.0 21.4 %all-to-all-start.1 = ((bf16[16,32,384]{2,1,0:T(8,128)(2,1)}), bf16[16,32,384]{2,1,0:T(8,128)(2,1)S(1)}, u32[]{:S(2)}, u32[]{:S(2)}) async-start(bf16[16,32,384]{2,1,0:T(8,128)(2,1)} %broadcast_in_dim.5), calls=%async_computation.1 | async-start | bytes 786432 | tf_op jit(solution)/shard_map/all_to_all | solution.py:70
  60.0 11.0 %copy-start = (bf16[256,4,1,1536]{3,0,2,1:T(8,128)(2,1)S(1)}, bf16[256,4,1,1536]{3,0,2,1:T(8,128)(2,1)}, u32[]{:S(2)}) copy-start(bf16[256,4,1,1536]{3,0,2,1:T(8,128)(2,1)} %copy.28) | copy-start | bytes 9437188
  64.1 9.5 %collective-permute-start.3 = (bf16[4,16,1536]{2,1,0:T(8,128)(2,1)S(1)}, bf16[4,16,1536]{2,1,0:T(8,128)(2,1)S(1)}, u32[]{:S(2)}, u32[]{:S(2)}) collective-permute-start(bf16[4,16,1536]{2,1,0:T(8,128)(2,1)S(1)} %slice.26), channel_id=1, source_target_pairs={{0,64},{64,128},{128,192},{192,0},{1,65},{65,129},{129,193},{193,1... | collective-permute-start | bytes 589832 | tf_op jit(solution)/shard_map/ppermute | solution.py:15
  65.2 8.4 %collective-permute-start.4 = (bf16[4,16,1536]{2,1,0:T(8,128)(2,1)S(1)}, bf16[4,16,1536]{2,1,0:T(8,128)(2,1)S(1)}, u32[]{:S(2)}, u32[]{:S(2)}) collective-permute-start(bf16[4,16,1536]{2,1,0:T(8,128)(2,1)S(1)} %slice.27), channel_id=1, source_target_pairs={{0,192},{64,0},{128,64},{192,128},{1,193},{65,1},{129,65},{193,129... | collective-permute-start | bytes 589832 | tf_op jit(solution)/shard_map/ppermute | solution.py:15
  76.5 13.4 %copy-start.2 = (bf16[256,4,1,1536]{3,0,2,1:T(8,128)(2,1)S(1)}, bf16[256,4,1,1536]{3,0,2,1:T(8,128)(2,1)}, u32[]{:S(2)}) copy-start(bf16[256,4,1,1536]{3,0,2,1:T(8,128)(2,1)} %copy.29) | copy-start | bytes 9437188
  76.5 11.7 %collective-permute-start.7 = (bf16[4,32,1536]{2,1,0:T(8,128)(2,1)S(1)}, bf16[4,32,1536]{2,1,0:T(8,128)(2,1)S(1)}, u32[]{:S(2)}, u32[]{:S(2)}) collective-permute-start(bf16[4,32,1536]{2,1,0:T(8,128)(2,1)S(1)} %reshape.25), channel_id=1, source_target_pairs={{0,64},{64,128},{128,192},{192,0},{1,65},{65,129},{129,193},{193,1... | collective-permute-start | bytes 1179656 | tf_op jit(solution)/shard_map/ppermute | solution.py:15
  76.6 11.6 %collective-permute-start.8 = (bf16[4,32,1536]{2,1,0:T(8,128)(2,1)S(1)}, bf16[4,32,1536]{2,1,0:T(8,128)(2,1)S(1)}, u32[]{:S(2)}, u32[]{:S(2)}) collective-permute-start(bf16[4,32,1536]{2,1,0:T(8,128)(2,1)S(1)} %reshape.25), channel_id=1, source_target_pairs={{0,192},{64,0},{128,64},{192,128},{1,193},{65,1},{129,65},{193,129... | collective-permute-start | bytes 1179656 | tf_op jit(solution)/shard_map/ppermute | solution.py:15
  81.2 9.6 %copy-start.1 = (bf16[256,4,1,1536]{3,0,2,1:T(8,128)(2,1)S(1)}, bf16[256,4,1,1536]{3,0,2,1:T(8,128)(2,1)}, u32[]{:S(2)}) copy-start(bf16[256,4,1,1536]{3,0,2,1:T(8,128)(2,1)} %copy.28) | copy-start | bytes 9437188
  81.3 19.2 %collective-permute-start.5 = (f32[32,256]{1,0:T(8,128)S(1)}, f32[32,256]{1,0:T(8,128)S(1)}, u32[]{:S(2)}, u32[]{:S(2)}) collective-permute-start(f32[32,256]{1,0:T(8,128)S(1)} %fusion.3), channel_id=1, source_target_pairs={{0,1},{1,0},{2,3},{3,2},{4,5},{5,4},{6,7},{7,6},{8,9},{9,8},{10,11... | collective-permute-start | bytes 98312 | tf_op jit(solution)/shard_map/ppermute | solution.py:15
  88.2 5.3 %collective-permute-start.10 = (bf16[4,16,1536]{2,1,0:T(8,128)(2,1)S(1)}, bf16[4,16,1536]{2,1,0:T(8,128)(2,1)S(1)}, u32[]{:S(2)}, u32[]{:S(2)}) collective-permute-start(bf16[4,16,1536]{2,1,0:T(8,128)(2,1)S(1)} %slice.29), channel_id=1, source_target_pairs={{0,192},{64,0},{128,64},{192,128},{1,193},{65,1},{129,65},{193,129... | collective-permute-start | bytes 589832 | tf_op jit(solution)/shard_map/ppermute | solution.py:15
  88.3 5.8 %collective-permute-start.9 = (bf16[4,16,1536]{2,1,0:T(8,128)(2,1)S(1)}, bf16[4,16,1536]{2,1,0:T(8,128)(2,1)S(1)}, u32[]{:S(2)}, u32[]{:S(2)}) collective-permute-start(bf16[4,16,1536]{2,1,0:T(8,128)(2,1)S(1)} %slice.28), channel_id=1, source_target_pairs={{0,64},{64,128},{128,192},{192,0},{1,65},{65,129},{129,193},{193,1... | collective-permute-start | bytes 589832 | tf_op jit(solution)/shard_map/ppermute | solution.py:15
  95.1 10.6 %collective-permute-start.11 = (f32[32,256]{1,0:T(8,128)S(1)}, f32[32,256]{1,0:T(8,128)S(1)}, u32[]{:S(2)}, u32[]{:S(2)}) collective-permute-start(f32[32,256]{1,0:T(8,128)S(1)} %fusion), channel_id=1, source_target_pairs={{0,1},{1,0},{2,3},{3,2},{4,5},{5,4},{6,7},{7,6},{8,9},{9,8},{10,11... | collective-permute-start | bytes 98312 | tf_op jit(solution)/shard_map/ppermute | solution.py:15
  100.5 7.0 %collective-permute-start.6 = (f32[32,256]{1,0:T(8,128)S(1)}, f32[32,256]{1,0:T(8,128)S(1)}, u32[]{:S(2)}, u32[]{:S(2)}) collective-permute-start(f32[32,256]{1,0:T(8,128)S(1)} %add.85), channel_id=1, source_target_pairs={{0,2},{2,0},{1,3},{3,1},{4,6},{6,4},{5,7},{7,5},{8,10},{10,8},{9,1... | collective-permute-start | bytes 98312 | tf_op jit(solution)/shard_map/ppermute | solution.py:15
  105.8 4.4 %collective-permute-start.12 = (f32[32,256]{1,0:T(8,128)S(1)}, f32[32,256]{1,0:T(8,128)S(1)}, u32[]{:S(2)}, u32[]{:S(2)}) collective-permute-start(f32[32,256]{1,0:T(8,128)S(1)} %add.90), channel_id=1, source_target_pairs={{0,2},{2,0},{1,3},{3,1},{4,6},{6,4},{5,7},{7,5},{8,10},{10,8},{9,1... | collective-permute-start | bytes 98312 | tf_op jit(solution)/shard_map/ppermute | solution.py:15

commit v5 on v3

--- a/solution.py
+++ b/solution.py
@@ -52,32 +52,21 @@
             zh, d = divmod(z, nt)
             pairs.append((z * nt + t, (zh * nt + t) * nt + d))
     moved = lax.ppermute(scaled, ("z", "xh", "core"), pairs)
-    copies = jnp.broadcast_to(moved[None], (nx * nz,) + moved.shape)
-    s2 = lax.all_to_all(copies, ("xl", "z"), 0, 0)
-    s2 = s2.reshape(nx, nz // nt, nt, n_loads, width)
-    own = jnp.transpose(s2, (0, 1, 3, 2, 4)).reshape(nx * nz // nt, n_loads, nt * width)
-    per_y = own.shape[0]
+    ny = lax.axis_size("y")
+    copies = jnp.broadcast_to(moved[None], (ny * nx * nz,) + moved.shape)
+    s3 = lax.all_to_all(copies, ("y", "xl", "z"), 0, 0)
+    s3 = s3.reshape(ny, nx, nz // nt, nt, n_loads, width)
+    blocks = jnp.transpose(s3, (0, 1, 2, 4, 3, 5)).reshape(ny, nx * nz // nt, n_loads, nt * width)
+    per_y = blocks.shape[1]
     cov_local = cov[:, :, 0, :]
-    ny = lax.axis_size("y")
-    me = lax.axis_index("y")
-
-    def term(block, y_from):
-        cov_part = lax.dynamic_slice_in_dim(cov_local, (y_from % ny) * per_y, per_y, 1)
-        block, cov_part = lax.optimization_barrier((block, cov_part))
-        return lax.dot_general(
+    part = None
+    for j in range(ny):
+        cov_part = cov_local[:, j * per_y : (j + 1) * per_y, :]
+        block, cov_part = lax.optimization_barrier((blocks[j], cov_part))
+        term = lax.dot_general(
             block, cov_part, (((0, 2), (1, 2)), ((), ())), preferred_element_type=jnp.float32
         )
-
-    fwd = shifted(own, "y", 1)
-    bwd = shifted(own, "y", -1)
-    part = term(own, me)
-    part = part + term(fwd, me - 1)
-    part = part + term(bwd, me + 1)
-    half = n_loads // 2
-    far_a = shifted(fwd[:, :half], "y", 1)
-    far_b = shifted(bwd[:, half:], "y", -1)
-    far = jnp.concatenate([far_a, far_b], axis=1)
-    part = part + term(far, me + 2)
+        part = term if part is None else part + term
     return team_sum(part)
 
 

time: 84 us -> 128 us (1.52)
  waiting for transfers between devices: 27.8 us -> 58.8 us
  local copies, waits for them, and re-layouts: 16.9 us -> 31.3 us
  starting transfers between devices: 33 us -> 29.8 us
  matrix products: 4.26 us -> 6.62 us
    all_to_all x1, waiting for transfers between devices: 17.3 us -> 54 us  [per_device(): s3 = lax.all_to_all(copies, ('y', 'xl', 'z'), 0, 0)]
    slice x2 -> x6, local copies, waits for them, and re-layouts: 0.05 us -> 20.2 us  [the longest x1 15.2 us: per_device(): cov_part = cov_local[:, j * per_y:(j + 1) * per_y, :]]
    dynamic_slice x1 -> x0, local copies, waits for them, and re-layouts: 11.8 us -> none  [term(): lax.dynamic_slice_in_dim(cov_local, y_from % ny * per_y, per_y, 1)]
    ppermute x6 -> x2, starting transfers between devices: 17.4 us -> 10.7 us  [shifted(): return lax.ppermute(x, axis, [(i, (i + by) % n) for i in range(n)])]
    squeeze x0 -> x4, local copies, waits for them, and re-layouts: none -> 6.14 us  [per_device(): block, cov_part = lax.optimization_barrier((blocks[j], cov_part))]
    ppermute x6 -> x2, waiting for transfers between devices: 8.7 us -> 3.08 us  [shifted(): return lax.ppermute(x, axis, [(i, (i + by) % n) for i in range(n)])]
    all_to_all x1, starting transfers between devices: 10.7 us -> 14.2 us  [per_device(): s3 = lax.all_to_all(copies, ('y', 'xl', 'z'), 0, 0)]
    dot_general x4, matrix products: 4.26 us -> 6.62 us  [per_device(): lax.dot_general(block, cov_part, (((0, 2), (1, 2)), ((), ())), preferred_...]
  transfers between devices with their start and end apart: 8 -> 4, of which waited for: 6 -> 4; matrix products, arithmetic and copies ran while one was open for 21% -> 12% of each run, Pallas kernels for 0% -> 0%
where the time goes in v5:
time: 128 us
  waiting for transfers between devices  58.8 us (46%)
  local copies, waits for them, and re-layouts  31.3 us (24%)
  starting transfers between devices  29.8 us (23%)
  matrix products  6.62 us (5%)
  other arithmetic  1.47 us (1%)
    all_to_all x1, waiting for transfers between devices, per_device(): s3 = lax.all_to_all(copies, ('y', 'xl', 'z'), 0, 0)  54 us
    slice x1, local copies, waits for them, and re-layouts, per_device(): cov_part = cov_local[:, j * per_y:(j + 1) * per_y, :]  15.2 us
    all_to_all x1, starting transfers between devices, per_device(): s3 = lax.all_to_all(copies, ('y', 'xl', 'z'), 0, 0)  14.2 us
    ppermute x2, starting transfers between devices, shifted(): return lax.ppermute(x, axis, [(i, (i + by) % n) for i in range(n)])  10.7 us
    dot_general x4, matrix products, per_device(): lax.dot_general(block, cov_part, (((0, 2), (1, 2)), ((), ())), preferred_...  6.62 us
    squeeze x4, local copies, waits for them, and re-layouts, per_device(): block, cov_part = lax.optimization_barrier((blocks[j], cov_part))  6.14 us
    ppermute x1, starting transfers between devices, per_device(): moved = lax.ppermute(scaled, ('z', 'xh', 'core'), pairs)  4.94 us
    slice x5, local copies, waits for them, and re-layouts, per_device(): block, cov_part = lax.optimization_barrier((blocks[j], cov_part))  4.94 us
  transfers between devices with their start and end apart: 4, of which 4 were waited for; matrix products, arithmetic and copies ran while one was open for 12% of the time, Pallas kernels for 0%

profile of v5, /device:TPU:1, one launch (start us, length us, event | category | flops | bytes accessed | tf_op | source)
XLA Modules:
  0.0 128.1 jit_solution(13609994318674728648)
XLA Ops:
  0.0 0.8 copy.14
  0.9 0.8 fusion.29
  1.7 4.9 %collective-permute-start = (bf16[64,384]{1,0:T(8,128)(2,1)S(1)}, bf16[64,384]{1,0:T(8,128)(2,1)S(1)}, u32[]{:S(2)}, u32[]{:S(2)}) collective-permute-start(bf16[64,384]{1,0:T(8,128)(2,1)S(1)} %fusion.29), channel_id=1, source_target_pairs={{0,0},{1,4},{2,8},{3,12},{4,1},{5,5},{6,9},{7,13},{8,2},{9,6},{10,... | collective-permute-start | bytes 147464 | tf_op jit(solution)/shard_map/ppermute | solution.py:54
  6.7 1.8 %collective-permute-done = bf16[64,384]{1,0:T(8,128)(2,1)S(1)} collective-permute-done((bf16[64,384]{1,0:T(8,128)(2,1)S(1)}, bf16[64,384]{1,0:T(8,128)(2,1)S(1)}, u32[]{:S(2)}, u32[]{:S(2)}) %collective-permute-start) | collective-permute-done | bytes 49184 | tf_op jit(solution)/shard_map/ppermute | solution.py:54
  8.4 2.2 %broadcast_in_dim.2 = bf16[64,64,384]{2,1,0:T(8,128)(2,1)} broadcast(bf16[64,384]{1,0:T(8,128)(2,1)S(1)} %collective-permute-done), dimensions={1,2} | broadcast | bytes 3194880 | tf_op jit(solution)/shard_map/broadcast_in_dim | solution.py:56
  10.6 14.2 %all-to-all-start = ((bf16[64,64,384]{2,1,0:T(8,128)(2,1)}), bf16[64,64,384]{2,1,0:T(8,128)(2,1)S(1)}, u32[]{:S(2)}, u32[]{:S(2)}) async-start(bf16[64,64,384]{2,1,0:T(8,128)(2,1)} %broadcast_in_dim.2), calls=%async_computation | async-start | bytes 6291456 | tf_op jit(solution)/shard_map/all_to_all | solution.py:57
  24.8 15.2 %fusion.30 = (bf16[256,4,1536]{2,1,0:T(4,128)(2,1)}, bf16[256,4,1536]{2,1,0:T(4,128)(2,1)}, bf16[256,4,1536]{2,1,0:T(4,128)(2,1)}, bf16[256,4,1536]{2,1,0:T(4,128)(2,1)}) fusion(bf16[256,16,1536]{2,1,0:T(8,128)(2,1)} %bitcast.27), kind=kLoop, calls=%fused_computation.17 | loop fusion | bytes 25165824 | tf_op jit(solution)/shard_map/slice | solution.py:64
  40.0 54.0 %all-to-all-done = bf16[64,64,384]{2,1,0:T(8,128)(2,1)S(1)} async-done(((bf16[64,64,384]{2,1,0:T(8,128)(2,1)}), bf16[64,64,384]{2,1,0:T(8,128)(2,1)S(1)}, u32[]{:S(2)}, u32[]{:S(2)}) %all-to-all-start) | async-done | bytes 3145760 | tf_op jit(solution)/shard_map/all_to_all | solution.py:57
  94.0 1.6 %fusion.31 = (bf16[1,2,2,64,4,384]{5,3,4,2,1,0:T(8,128)(2,1)S(1)}, bf16[1,2,2,64,4,384]{5,3,4,2,1,0:T(8,128)(2,1)}, bf16[1,2,2,64,4,384]{5,3,4,2,1,0:T(8,128)(2,1)}, bf16[1,2,2,64,4,384]{5,3,4,2,1,0:T(8,128)(2,1)}) fusion(bf16[4,2,2,64,4,384]{5,3,4,2,1,0:T(8,128)(2,1)S(1)} %bitcast.28), kind=kLoop, calls=%fused_computation.18 | loop fusion | bytes 6291456 | tf_op jit(solution)/shard_map/slice | solution.py:65
  96.2 1.3 squeeze.19
  98.1 1.2 squeeze.18
  99.9 1.2 squeeze.17
  101.1 1.5 %copy.15 = bf16[1,2,2,64,4,384]{5,4,3,2,1,0:T(4,128)(2,1)} copy(bf16[1,2,2,64,4,384]{5,3,4,2,1,0:T(8,128)(2,1)S(1)} %copy-done.3) | data formatting | bytes 1572864 | tf_op jit(solution)/shard_map/slice | solution.py:65
  102.6 2.5 %squeeze.15 = bf16[4,64,1536]{2,1,0:T(8,128)(2,1)} reshape(bf16[1,2,2,64,4,384]{5,4,3,2,1,0:T(4,128)(2,1)} %copy.15) | data formatting | bytes 1572864 | tf_op jit(solution)/shard_map/squeeze | solution.py:65
  105.1 3.3 %fusion.8 = f32[64,256]{1,0:T(8,128)S(1)} fusion(bf16[4,64,1536]{2,1,0:T(8,128)(2,1)} %squeeze.15, bf16[256,4,1536]{2,1,0:T(4,128)(2,1)} %get-tuple-element.14), kind=kOutput, calls=%fused_computation.8 | convolution fusion | flops 201326592 | bytes 3997696 | tf_op jit(solution)/shard_map/dot_general | solution.py:66
  108.5 1.1 fusion.26
  109.6 0.8 copy-done.1
  110.5 1.1 fusion.23
  111.6 0.8 copy-done
  112.6 1.1 fusion.20
  113.7 5.1 %collective-permute-start.1 = (f32[64,256]{1,0:T(8,128)S(1)}, f32[64,256]{1,0:T(8,128)S(1)}, u32[]{:S(2)}, u32[]{:S(2)}) collective-permute-start(f32[64,256]{1,0:T(8,128)S(1)} %fusion.20), channel_id=1, source_target_pairs={{0,1},{1,0},{2,3},{3,2},{4,5},{5,4},{6,7},{7,6},{8,9},{9,8},{10,11... | collective-permute-start | bytes 196616 | tf_op jit(solution)/shard_map/ppermute | solution.py:15
  118.8 0.9 collective-permute-done.1
  119.7 5.6 %collective-permute-start.2 = (f32[64,256]{1,0:T(8,128)S(1)}, f32[64,256]{1,0:T(8,128)S(1)}, u32[]{:S(2)}, u32[]{:S(2)}) collective-permute-start(f32[64,256]{1,0:T(8,128)S(1)} %add.18), channel_id=1, source_target_pairs={{0,2},{2,0},{1,3},{3,1},{4,6},{6,4},{5,7},{7,5},{8,10},{10,8},{9,1... | collective-permute-start | bytes 196616 | tf_op jit(solution)/shard_map/ppermute | solution.py:15
  125.3 2.2 %collective-permute-done.2 = f32[64,256]{1,0:T(8,128)S(1)} collective-permute-done((f32[64,256]{1,0:T(8,128)S(1)}, f32[64,256]{1,0:T(8,128)S(1)}, u32[]{:S(2)}, u32[]{:S(2)}) %collective-permute-start.2) | collective-permute-done | bytes 65568 | tf_op jit(solution)/shard_map/ppermute | solution.py:15
  (22 shorter events, 3.0 us)
Async XLA Ops:
  1.7 6.7 %collective-permute-start = (bf16[64,384]{1,0:T(8,128)(2,1)S(1)}, bf16[64,384]{1,0:T(8,128)(2,1)S(1)}, u32[]{:S(2)}, u32[]{:S(2)}) collective-permute-start(bf16[64,384]{1,0:T(8,128)(2,1)S(1)} %fusion.29), channel_id=1, source_target_pairs={{0,0},{1,4},{2,8},{3,12},{4,1},{5,5},{6,9},{7,13},{8,2},{9,6},{10,... | collective-permute-start | bytes 147464 | tf_op jit(solution)/shard_map/ppermute | solution.py:54
  10.6 83.4 %all-to-all-start = ((bf16[64,64,384]{2,1,0:T(8,128)(2,1)}), bf16[64,64,384]{2,1,0:T(8,128)(2,1)S(1)}, u32[]{:S(2)}, u32[]{:S(2)}) async-start(bf16[64,64,384]{2,1,0:T(8,128)(2,1)} %broadcast_in_dim.2), calls=%async_computation | async-start | bytes 6291456 | tf_op jit(solution)/shard_map/all_to_all | solution.py:57
  95.6 1.9 %copy-start.5 = (bf16[1,2,2,64,4,384]{5,3,4,2,1,0:T(8,128)(2,1)S(1)}, bf16[1,2,2,64,4,384]{5,3,4,2,1,0:T(8,128)(2,1)}, u32[]{:S(2)}) copy-start(bf16[1,2,2,64,4,384]{5,3,4,2,1,0:T(8,128)(2,1)} %get-tuple-element.26) | copy-start | bytes 2359300
  95.6 3.7 %copy-start.4 = (bf16[1,2,2,64,4,384]{5,3,4,2,1,0:T(8,128)(2,1)S(1)}, bf16[1,2,2,64,4,384]{5,3,4,2,1,0:T(8,128)(2,1)}, u32[]{:S(2)}) copy-start(bf16[1,2,2,64,4,384]{5,3,4,2,1,0:T(8,128)(2,1)} %get-tuple-element.27) | copy-start | bytes 2359300
  97.5 3.6 %copy-start.3 = (bf16[1,2,2,64,4,384]{5,3,4,2,1,0:T(8,128)(2,1)S(1)}, bf16[1,2,2,64,4,384]{5,3,4,2,1,0:T(8,128)(2,1)}, u32[]{:S(2)}) copy-start(bf16[1,2,2,64,4,384]{5,3,4,2,1,0:T(8,128)(2,1)} %get-tuple-element.28) | copy-start | bytes 2359300
  102.6 5.8 %copy-start.2 = (bf16[256,4,1536]{2,1,0:T(4,128)(2,1)S(1)}, bf16[256,4,1536]{2,1,0:T(4,128)(2,1)}, u32[]{:S(2)}) copy-start(bf16[256,4,1536]{2,1,0:T(4,128)(2,1)} %get-tuple-element.16) | copy-start | bytes 9437188
  105.1 3.3 %copy-start.8 = (bf16[4,64,1536]{2,1,0:T(8,128)(2,1)S(1)}, bf16[4,64,1536]{2,1,0:T(8,128)(2,1)}, u32[]{:S(2)}) copy-start(bf16[4,64,1536]{2,1,0:T(8,128)(2,1)} %squeeze.17) | copy-start | bytes 2359300
  108.4 1.9 %copy-start.1 = (bf16[256,4,1536]{2,1,0:T(4,128)(2,1)S(1)}, bf16[256,4,1536]{2,1,0:T(4,128)(2,1)}, u32[]{:S(2)}) copy-start(bf16[256,4,1536]{2,1,0:T(4,128)(2,1)} %get-tuple-element.18) | copy-start | bytes 9437188
  108.4 2.1 %copy-start.7 = (bf16[4,64,1536]{2,1,0:T(8,128)(2,1)S(1)}, bf16[4,64,1536]{2,1,0:T(8,128)(2,1)}, u32[]{:S(2)}) copy-start(bf16[4,64,1536]{2,1,0:T(8,128)(2,1)} %squeeze.18) | copy-start | bytes 2359300
  110.5 1.9 %copy-start = (bf16[256,4,1536]{2,1,0:T(4,128)(2,1)S(1)}, bf16[256,4,1536]{2,1,0:T(4,128)(2,1)}, u32[]{:S(2)}) copy-start(bf16[256,4,1536]{2,1,0:T(4,128)(2,1)} %get-tuple-element.20) | copy-start | bytes 9437188
  110.5 2.1 %copy-start.6 = (bf16[4,64,1536]{2,1,0:T(8,128)(2,1)S(1)}, bf16[4,64,1536]{2,1,0:T(8,128)(2,1)}, u32[]{:S(2)}) copy-start(bf16[4,64,1536]{2,1,0:T(8,128)(2,1)} %squeeze.19) | copy-start | bytes 2359300
  113.7 6.0 %collective-permute-start.1 = (f32[64,256]{1,0:T(8,128)S(1)}, f32[64,256]{1,0:T(8,128)S(1)}, u32[]{:S(2)}, u32[]{:S(2)}) collective-permute-start(f32[64,256]{1,0:T(8,128)S(1)} %fusion.20), channel_id=1, source_target_pairs={{0,1},{1,0},{2,3},{3,2},{4,5},{5,4},{6,7},{7,6},{8,9},{9,8},{10,11... | collective-permute-start | bytes 196616 | tf_op jit(solution)/shard_map/ppermute | solution.py:15
  119.7 7.8 %collective-permute-start.2 = (f32[64,256]{1,0:T(8,128)S(1)}, f32[64,256]{1,0:T(8,128)S(1)}, u32[]{:S(2)}, u32[]{:S(2)}) collective-permute-start(f32[64,256]{1,0:T(8,128)S(1)} %add.18), channel_id=1, source_target_pairs={{0,2},{2,0},{1,3},{3,1},{4,6},{6,4},{5,7},{7,5},{8,10},{10,8},{9,1... | collective-permute-start | bytes 196616 | tf_op jit(solution)/shard_map/ppermute | solution.py:15

commit v6 on v3

--- a/solution.py
+++ b/solution.py
@@ -68,16 +68,17 @@
             block, cov_part, (((0, 2), (1, 2)), ((), ())), preferred_element_type=jnp.float32
         )
 
-    fwd = shifted(own, "y", 1)
-    bwd = shifted(own, "y", -1)
-    part = term(own, me)
-    part = part + term(fwd, me - 1)
-    part = part + term(bwd, me + 1)
     half = n_loads // 2
-    far_a = shifted(fwd[:, :half], "y", 1)
-    far_b = shifted(bwd[:, half:], "y", -1)
-    far = jnp.concatenate([far_a, far_b], axis=1)
-    part = part + term(far, me + 2)
+    top, bot = own[:, :half], own[:, half:]
+    fwd_top = shifted(top, "y", 1)
+    bwd_bot = shifted(bot, "y", -1)
+    fwd_bot = shifted(bot, "y", 1)
+    bwd_top = shifted(top, "y", -1)
+    far_top = shifted(fwd_top, "y", 1)
+    far_bot = shifted(bwd_bot, "y", -1)
+    part_top = term(top, me) + term(fwd_top, me - 1) + term(bwd_top, me + 1) + term(far_top, me - 2)
+    part_bot = term(bot, me) + term(bwd_bot, me + 1) + term(fwd_bot, me - 1) + term(far_bot, me + 2)
+    part = jnp.concatenate([part_top, part_bot], axis=0)
     return team_sum(part)
 
 

time: 84 us -> 93.9 us (1.12)
  local copies, waits for them, and re-layouts: 16.9 us -> 32.2 us
  waiting for transfers between devices: 27.8 us -> 16.3 us
  matrix products: 4.26 us -> 9.86 us
    all_to_all x1, waiting for transfers between devices: 17.3 us -> 0.01 us  [per_device(): s2 = lax.all_to_all(copies, ('xl', 'z'), 0, 0)]
    unnamed x4 -> x13, local copies, waits for them, and re-layouts: 2.28 us -> 9.6 us
    ppermute x6 -> x8, waiting for transfers between devices: 8.7 us -> 14.5 us  [shifted(): return lax.ppermute(x, axis, [(i, (i + by) % n) for i in range(n)])]
    dot_general x4 -> x8, matrix products: 4.26 us -> 9.86 us  [term(): lax.dot_general(block, cov_part, (((0, 2), (1, 2)), ((), ())), preferred_...]
    dynamic_slice x1, local copies, waits for them, and re-layouts: 11.8 us -> 14.4 us  [term(): lax.dynamic_slice_in_dim(cov_local, y_from % ny * per_y, per_y, 1)]
    reshape x1, local copies, waits for them, and re-layouts: 0.3 us -> 2.39 us  [per_device(): jnp.transpose(s2, (0, 1, 3, 2, 4))]
    transpose x1, local copies, waits for them, and re-layouts: 0.61 us -> 2.62 us  [per_device(): jnp.transpose(s2, (0, 1, 3, 2, 4))]
    slice x2 -> x1, local copies, waits for them, and re-layouts: 0.05 us -> 1.33 us  [per_device(): top, bot = (own[:, :half], own[:, half:])]
  transfers between devices with their start and end apart: 8 -> 10, of which waited for: 6 -> 6; matrix products, arithmetic and copies ran while one was open for 21% -> 34% of each run, Pallas kernels for 0% -> 0%
where the time goes in v6:
time: 93.9 us; the launch traced here: 93.6 us
  starting transfers between devices  33.4 us (36%)
  local copies, waits for them, and re-layouts  32.2 us (34%)
  waiting for transfers between devices  16.3 us (17%)
  matrix products  9.86 us (11%)
  other arithmetic  1.48 us (2%)
    ppermute x8, starting transfers between devices, shifted(): return lax.ppermute(x, axis, [(i, (i + by) % n) for i in range(n)])  17.7 us
    ppermute x8, waiting for transfers between devices, shifted(): return lax.ppermute(x, axis, [(i, (i + by) % n) for i in range(n)])  14.5 us
    dynamic_slice x1, local copies, waits for them, and re-layouts, term(): lax.dynamic_slice_in_dim(cov_local, y_from % ny * per_y, per_y, 1)  14.4 us
    all_to_all x1, starting transfers between devices, per_device(): s2 = lax.all_to_all(copies, ('xl', 'z'), 0, 0)  10.7 us
    dot_general x8, matrix products, term(): lax.dot_general(block, cov_part, (((0, 2), (1, 2)), ((), ())), preferred_...  9.86 us
    unnamed x13, local copies, waits for them, and re-layouts  9.6 us
    ppermute x1, starting transfers between devices, per_device(): moved = lax.ppermute(scaled, ('z', 'xh', 'core'), pairs)  4.94 us
    transpose x1, local copies, waits for them, and re-layouts, per_device(): jnp.transpose(s2, (0, 1, 3, 2, 4))  2.62 us
  transfers between devices with their start and end apart: 10, of which 6 were waited for; matrix products, arithmetic and copies ran while one was open for 34% of the time, Pallas kernels for 0%

profile of v6, /device:TPU:1, one launch (start us, length us, event | category | flops | bytes accessed | tf_op | source)
XLA Modules:
  0.0 93.6 jit_solution(16334391149526643383)
XLA Ops:
  1.7 4.9 %collective-permute-start = (bf16[64,384]{1,0:T(8,128)(2,1)S(1)}, bf16[64,384]{1,0:T(8,128)(2,1)S(1)}, u32[]{:S(2)}, u32[]{:S(2)}) collective-permute-start(bf16[64,384]{1,0:T(8,128)(2,1)S(1)} %fusion.6), channel_id=1, source_target_pairs={{0,0},{1,4},{2,8},{3,12},{4,1},{5,5},{6,9},{7,13},{8,2},{9,6},{10,... | collective-permute-start | bytes 147464 | tf_op jit(solution)/shard_map/ppermute | solution.py:54
  6.7 1.8 %collective-permute-done = bf16[64,384]{1,0:T(8,128)(2,1)S(1)} collective-permute-done((bf16[64,384]{1,0:T(8,128)(2,1)S(1)}, bf16[64,384]{1,0:T(8,128)(2,1)S(1)}, u32[]{:S(2)}, u32[]{:S(2)}) %collective-permute-start) | collective-permute-done | bytes 49184 | tf_op jit(solution)/shard_map/ppermute | solution.py:54
  9.4 10.7 %all-to-all-start = ((bf16[16,64,384]{2,1,0:T(8,128)(2,1)}), bf16[16,64,384]{2,1,0:T(8,128)(2,1)}, u32[]{:S(2)}, u32[]{:S(2)}) async-start(bf16[16,64,384]{2,1,0:T(8,128)(2,1)} %broadcast_in_dim.2), calls=%async_computation | async-start | bytes 1572864 | tf_op jit(solution)/shard_map/all_to_all | solution.py:56
  20.2 14.4 %constant_dynamic-slice_fusion.1 = (bf16[256,4,1,1536]{3,1,2,0:T(4,128)(2,1)S(1)}, bf16[256,4,1,1536]{3,1,2,0:T(4,128)(2,1)S(1)}, bf16[256,4,1,1536]{3,1,2,0:T(4...) fusion(bf16[256,16,1,1536]{3,1,2,0:T(8,128)(2,1)} %param.5, s32[]{:T(128)S(6)} %select_n.54, ...), kind=kLoop, calls=%fused_computation.23 | loop fusion | bytes 31457300 | tf_op jit(solution)/shard_map/dynamic_slice | solution.py:65
  34.6 2.2 %copy.34 = bf16[256,4,1,1536]{3,0,2,1:T(8,128)(2,1)} copy(bf16[256,4,1,1536]{3,1,2,0:T(4,128)(2,1)S(1)} %get-tuple-element.40) | data formatting | bytes 6291456
  37.4 2.3 %copy.32 = bf16[256,4,1,1536]{3,0,2,1:T(8,128)(2,1)} copy(bf16[256,4,1,1536]{3,1,2,0:T(4,128)(2,1)S(1)} %get-tuple-element.38) | data formatting | bytes 6291456
  39.7 2.2 %copy.31 = bf16[256,4,1,1536]{3,0,2,1:T(8,128)(2,1)} copy(bf16[256,4,1,1536]{3,1,2,0:T(4,128)(2,1)S(1)} %get-tuple-element.37) | data formatting | bytes 6291456
  41.9 2.3 %copy.30 = bf16[256,4,1,1536]{3,0,2,1:T(8,128)(2,1)} copy(bf16[256,4,1,1536]{3,1,2,0:T(4,128)(2,1)S(1)} %get-tuple-element.41) | data formatting | bytes 6291456
  44.2 2.6 %copy.12 = bf16[2,2,64,4,384]{4,3,2,1,0:T(4,128)(2,1)} copy(bf16[2,2,64,4,384]{4,2,3,1,0:T(8,128)(2,1)} %bitcast.1) | data formatting | bytes 1572864 | tf_op jit(solution)/shard_map/transpose | solution.py:58
  46.8 2.4 %reshape.17 = bf16[4,64,1536]{2,1,0:T(8,128)(2,1)} reshape(bf16[2,2,64,4,384]{4,3,2,1,0:T(4,128)(2,1)} %copy.12) | data formatting | bytes 1572864 | tf_op jit(solution)/shard_map/reshape | solution.py:58
  49.2 1.3 %fusion.8 = (bf16[4,32,1536]{2,1,0:T(8,128)(2,1)S(1)}, bf16[4,32,1536]{2,1,0:T(8,128)(2,1)S(1)}) fusion(bf16[4,64,1536]{2,1,0:T(8,128)(2,1)} %reshape.17), kind=kLoop, calls=%fused_computation.28 | loop fusion | bytes 1572864 | tf_op jit(solution)/shard_map/slice | solution.py:72
  50.6 1.2 %collective-permute-start.1 = (bf16[4,32,1536]{2,1,0:T(8,128)(2,1)S(1)}, bf16[4,32,1536]{2,1,0:T(8,128)(2,1)S(1)}, u32[]{:S(2)}, u32[]{:S(2)}) collective-permute-start(bf16[4,32,1536]{2,1,0:T(8,128)(2,1)S(1)} %get-tuple-element.21), channel_id=1, source_target_pairs={{0,64},{64,128},{128,192},{192,0},{1,65},{65,129},{129,193},{193,1... | collective-permute-start | bytes 1179656 | tf_op jit(solution)/shard_map/ppermute | solution.py:15
  51.8 2.0 %collective-permute-start.2 = (bf16[4,32,1536]{2,1,0:T(8,128)(2,1)S(1)}, bf16[4,32,1536]{2,1,0:T(8,128)(2,1)S(1)}, u32[]{:S(2)}, u32[]{:S(2)}) collective-permute-start(bf16[4,32,1536]{2,1,0:T(8,128)(2,1)S(1)} %get-tuple-element.21), channel_id=1, source_target_pairs={{0,192},{64,0},{128,64},{192,128},{1,193},{65,1},{129,65},{193,129... | collective-permute-start | bytes 1179656 | tf_op jit(solution)/shard_map/ppermute | solution.py:15
  53.7 1.4 %collective-permute-start.4 = (bf16[4,32,1536]{2,1,0:T(8,128)(2,1)S(1)}, bf16[4,32,1536]{2,1,0:T(8,128)(2,1)S(1)}, u32[]{:S(2)}, u32[]{:S(2)}) collective-permute-start(bf16[4,32,1536]{2,1,0:T(8,128)(2,1)S(1)} %get-tuple-element.29), channel_id=1, source_target_pairs={{0,192},{64,0},{128,64},{192,128},{1,193},{65,1},{129,65},{193,129... | collective-permute-start | bytes 1179656 | tf_op jit(solution)/shard_map/ppermute | solution.py:15
  55.2 2.9 %convolution_bitcast_fusion.7 = f32[32,256]{1,0:T(8,128)S(1)} fusion(bf16[4,32,1536]{2,1,0:T(8,128)(2,1)S(1)} %get-tuple-element.21, bf16[256,4,1536]{2,0,1:T(8,128)(2,1)} %bitcast.71), kind=kOutput, calls=%fused_computation.18 | convolution fusion | flops 100663296 | bytes 3571712 | tf_op jit(solution)/shard_map/dot_general | solution.py:67
  59.1 1.5 %collective-permute-done.1 = bf16[4,32,1536]{2,1,0:T(8,128)(2,1)S(1)} collective-permute-done((bf16[4,32,1536]{2,1,0:T(8,128)(2,1)S(1)}, bf16[4,32,1536]{2,1,0:T(8,128)(2,1)S(1)}, u32[]{:S(2)}, u32[]{:S(2)}) %collective-permute-start.1) | collective-permute-done | bytes 393248 | tf_op jit(solution)/shard_map/ppermute | solution.py:15
  62.7 6.2 %collective-permute-done.4 = bf16[4,32,1536]{2,1,0:T(8,128)(2,1)S(1)} collective-permute-done((bf16[4,32,1536]{2,1,0:T(8,128)(2,1)S(1)}, bf16[4,32,1536]{2,1,0:T(8,128)(2,1)S(1)}, u32[]{:S(2)}, u32[]{:S(2)}) %collective-permute-start.4) | collective-permute-done | bytes 393248 | tf_op jit(solution)/shard_map/ppermute | solution.py:15
  68.9 1.2 %collective-permute-start.3 = (bf16[4,32,1536]{2,1,0:T(8,128)(2,1)S(1)}, bf16[4,32,1536]{2,1,0:T(8,128)(2,1)S(1)}, u32[]{:S(2)}, u32[]{:S(2)}) collective-permute-start(bf16[4,32,1536]{2,1,0:T(8,128)(2,1)S(1)} %collective-permute-done.1), channel_id=1, source_target_pairs={{0,64},{64,128},{128,192},{192,0},{1,65},{65,129},{129,193},{193,1... | collective-permute-start | bytes 1179656 | tf_op jit(solution)/shard_map/ppermute | solution.py:15
  70.1 1.5 %collective-permute-start.6 = (bf16[4,32,1536]{2,1,0:T(8,128)(2,1)S(1)}, bf16[4,32,1536]{2,1,0:T(8,128)(2,1)S(1)}, u32[]{:S(2)}, u32[]{:S(2)}) collective-permute-start(bf16[4,32,1536]{2,1,0:T(8,128)(2,1)S(1)} %collective-permute-done.4), channel_id=1, source_target_pairs={{0,192},{64,0},{128,64},{192,128},{1,193},{65,1},{129,65},{193,129... | collective-permute-start | bytes 1179656 | tf_op jit(solution)/shard_map/ppermute | solution.py:15
  71.6 1.0 %fusion.2 = f32[32,256]{1,0:T(8,128)S(1)} fusion(f32[32,256]{1,0:T(8,128)S(1)} %convolution_bitcast_fusion.3, bf16[4,32,1536]{2,1,0:T(8,128)(2,1)S(1)} %collective-permute-done.4, bf16[256,4,1536]{2,0,1:T(8,128)(2,1)S(1)} %bitcast.70), kind=kOutput, calls=%fused_computation.10 | convolution fusion | flops 100671488 | bytes 3604480 | tf_op jit(solution)/shard_map/dot_general | solution.py:67
  73.6 3.7 %collective-permute-done.3 = bf16[4,32,1536]{2,1,0:T(8,128)(2,1)S(1)} collective-permute-done((bf16[4,32,1536]{2,1,0:T(8,128)(2,1)S(1)}, bf16[4,32,1536]{2,1,0:T(8,128)(2,1)S(1)}, u32[]{:S(2)}, u32[]{:S(2)}) %collective-permute-start.3) | collective-permute-done | bytes 393248 | tf_op jit(solution)/shard_map/ppermute | solution.py:15
  79.4 4.5 %collective-permute-start.7 = (f32[64,256]{1,0:T(8,128)S(1)}, f32[64,256]{1,0:T(8,128)S(1)}, u32[]{:S(2)}, u32[]{:S(2)}) collective-permute-start(f32[64,256]{1,0:T(8,128)S(1)} %pad_maximum_fusion), channel_id=1, source_target_pairs={{0,1},{1,0},{2,3},{3,2},{4,5},{5,4},{6,7},{7,6},{8,9},{9,8},{10,11... | collective-permute-start | bytes 196616 | tf_op jit(solution)/shard_map/ppermute | solution.py:15
  84.8 5.9 %collective-permute-start.8 = (f32[64,256]{1,0:T(8,128)S(1)}, f32[64,256]{1,0:T(8,128)S(1)}, u32[]{:S(2)}, u32[]{:S(2)}) collective-permute-start(f32[64,256]{1,0:T(8,128)S(1)} %fusion.7), channel_id=1, source_target_pairs={{0,2},{2,0},{1,3},{3,1},{4,6},{6,4},{5,7},{7,5},{8,10},{10,8},{9,1... | collective-permute-start | bytes 196616 | tf_op jit(solution)/shard_map/ppermute | solution.py:15
  90.8 2.2 %collective-permute-done.8 = f32[64,256]{1,0:T(8,128)S(1)} collective-permute-done((f32[64,256]{1,0:T(8,128)S(1)}, f32[64,256]{1,0:T(8,128)S(1)}, u32[]{:S(2)}, u32[]{:S(2)}) %collective-permute-start.8) | collective-permute-done | bytes 65568 | tf_op jit(solution)/shard_map/ppermute | solution.py:15
  (28 shorter events, 11.0 us)
Async XLA Ops:
  1.7 6.7 %collective-permute-start = (bf16[64,384]{1,0:T(8,128)(2,1)S(1)}, bf16[64,384]{1,0:T(8,128)(2,1)S(1)}, u32[]{:S(2)}, u32[]{:S(2)}) collective-permute-start(bf16[64,384]{1,0:T(8,128)(2,1)S(1)} %fusion.6), channel_id=1, source_target_pairs={{0,0},{1,4},{2,8},{3,12},{4,1},{5,5},{6,9},{7,13},{8,2},{9,6},{10,... | collective-permute-start | bytes 147464 | tf_op jit(solution)/shard_map/ppermute | solution.py:54
  9.4 34.8 %all-to-all-start = ((bf16[16,64,384]{2,1,0:T(8,128)(2,1)}), bf16[16,64,384]{2,1,0:T(8,128)(2,1)}, u32[]{:S(2)}, u32[]{:S(2)}) async-start(bf16[16,64,384]{2,1,0:T(8,128)(2,1)} %broadcast_in_dim.2), calls=%async_computation | async-start | bytes 1572864 | tf_op jit(solution)/shard_map/all_to_all | solution.py:56
  49.2 8.9 %copy-start.1 = (bf16[256,4,1,1536]{3,0,2,1:T(8,128)(2,1)S(1)}, bf16[256,4,1,1536]{3,0,2,1:T(8,128)(2,1)}, u32[]{:S(2)}) copy-start(bf16[256,4,1,1536]{3,0,2,1:T(8,128)(2,1)} %copy.34) | copy-start | bytes 9437188
  50.6 10.1 %collective-permute-start.1 = (bf16[4,32,1536]{2,1,0:T(8,128)(2,1)S(1)}, bf16[4,32,1536]{2,1,0:T(8,128)(2,1)S(1)}, u32[]{:S(2)}, u32[]{:S(2)}) collective-permute-start(bf16[4,32,1536]{2,1,0:T(8,128)(2,1)S(1)} %get-tuple-element.21), channel_id=1, source_target_pairs={{0,64},{64,128},{128,192},{192,0},{1,65},{65,129},{129,193},{193,1... | collective-permute-start | bytes 1179656 | tf_op jit(solution)/shard_map/ppermute | solution.py:15
  51.8 9.9 %collective-permute-start.2 = (bf16[4,32,1536]{2,1,0:T(8,128)(2,1)S(1)}, bf16[4,32,1536]{2,1,0:T(8,128)(2,1)S(1)}, u32[]{:S(2)}, u32[]{:S(2)}) collective-permute-start(bf16[4,32,1536]{2,1,0:T(8,128)(2,1)S(1)} %get-tuple-element.21), channel_id=1, source_target_pairs={{0,192},{64,0},{128,64},{192,128},{1,193},{65,1},{129,65},{193,129... | collective-permute-start | bytes 1179656 | tf_op jit(solution)/shard_map/ppermute | solution.py:15
  53.7 15.2 %collective-permute-start.4 = (bf16[4,32,1536]{2,1,0:T(8,128)(2,1)S(1)}, bf16[4,32,1536]{2,1,0:T(8,128)(2,1)S(1)}, u32[]{:S(2)}, u32[]{:S(2)}) collective-permute-start(bf16[4,32,1536]{2,1,0:T(8,128)(2,1)S(1)} %get-tuple-element.29), channel_id=1, source_target_pairs={{0,192},{64,0},{128,64},{192,128},{1,193},{65,1},{129,65},{193,129... | collective-permute-start | bytes 1179656 | tf_op jit(solution)/shard_map/ppermute | solution.py:15
  55.1 17.5 %collective-permute-start.5 = (bf16[4,32,1536]{2,1,0:T(8,128)(2,1)S(1)}, bf16[4,32,1536]{2,1,0:T(8,128)(2,1)S(1)}, u32[]{:S(2)}, u32[]{:S(2)}) collective-permute-start(bf16[4,32,1536]{2,1,0:T(8,128)(2,1)S(1)} %get-tuple-element.29), channel_id=1, source_target_pairs={{0,64},{64,128},{128,192},{192,0},{1,65},{65,129},{129,193},{193,1... | collective-permute-start | bytes 1179656 | tf_op jit(solution)/shard_map/ppermute | solution.py:15
  58.1 3.6 %copy-start = (bf16[256,4,1,1536]{3,0,2,1:T(8,128)(2,1)S(1)}, bf16[256,4,1,1536]{3,0,2,1:T(8,128)(2,1)}, u32[]{:S(2)}) copy-start(bf16[256,4,1,1536]{3,0,2,1:T(8,128)(2,1)} %copy.32) | copy-start | bytes 9437188
  62.7 14.7 %copy-start.3 = (bf16[256,4,1,1536]{3,0,2,1:T(8,128)(2,1)S(1)}, bf16[256,4,1,1536]{3,0,2,1:T(8,128)(2,1)}, u32[]{:S(2)}) copy-start(bf16[256,4,1,1536]{3,0,2,1:T(8,128)(2,1)} %copy.31) | copy-start | bytes 9437188
  68.9 8.5 %collective-permute-start.3 = (bf16[4,32,1536]{2,1,0:T(8,128)(2,1)S(1)}, bf16[4,32,1536]{2,1,0:T(8,128)(2,1)S(1)}, u32[]{:S(2)}, u32[]{:S(2)}) collective-permute-start(bf16[4,32,1536]{2,1,0:T(8,128)(2,1)S(1)} %collective-permute-done.1), channel_id=1, source_target_pairs={{0,64},{64,128},{128,192},{192,0},{1,65},{65,129},{129,193},{193,1... | collective-permute-start | bytes 1179656 | tf_op jit(solution)/shard_map/ppermute | solution.py:15
  70.1 7.3 %collective-permute-start.6 = (bf16[4,32,1536]{2,1,0:T(8,128)(2,1)S(1)}, bf16[4,32,1536]{2,1,0:T(8,128)(2,1)S(1)}, u32[]{:S(2)}, u32[]{:S(2)}) collective-permute-start(bf16[4,32,1536]{2,1,0:T(8,128)(2,1)S(1)} %collective-permute-done.4), channel_id=1, source_target_pairs={{0,192},{64,0},{128,64},{192,128},{1,193},{65,1},{129,65},{193,129... | collective-permute-start | bytes 1179656 | tf_op jit(solution)/shard_map/ppermute | solution.py:15
  72.6 5.8 %copy-start.2 = (bf16[256,4,1,1536]{3,0,2,1:T(8,128)(2,1)S(1)}, bf16[256,4,1,1536]{3,0,2,1:T(8,128)(2,1)}, u32[]{:S(2)}) copy-start(bf16[256,4,1,1536]{3,0,2,1:T(8,128)(2,1)} %copy.30) | copy-start | bytes 9437188
  79.4 5.4 %collective-permute-start.7 = (f32[64,256]{1,0:T(8,128)S(1)}, f32[64,256]{1,0:T(8,128)S(1)}, u32[]{:S(2)}, u32[]{:S(2)}) collective-permute-start(f32[64,256]{1,0:T(8,128)S(1)} %pad_maximum_fusion), channel_id=1, source_target_pairs={{0,1},{1,0},{2,3},{3,2},{4,5},{5,4},{6,7},{7,6},{8,9},{9,8},{10,11... | collective-permute-start | bytes 196616 | tf_op jit(solution)/shard_map/ppermute | solution.py:15
  84.8 8.1 %collective-permute-start.8 = (f32[64,256]{1,0:T(8,128)S(1)}, f32[64,256]{1,0:T(8,128)S(1)}, u32[]{:S(2)}, u32[]{:S(2)}) collective-permute-start(f32[64,256]{1,0:T(8,128)S(1)} %fusion.7), channel_id=1, source_target_pairs={{0,2},{2,0},{1,3},{3,1},{4,6},{6,4},{5,7},{7,5},{8,10},{10,8},{9,1... | collective-permute-start | bytes 196616 | tf_op jit(solution)/shard_map/ppermute | solution.py:15

commit v7 on v2

--- a/solution.py
+++ b/solution.py
@@ -32,9 +32,8 @@
 
 
 def team_sum(x):
-    on_chip = x + shifted(x, "core", 1)
-    across = shifted(x, "xh", 1) + lax.ppermute(x, ("xh", "core"), [(0, 3), (3, 0), (1, 2), (2, 1)])
-    return on_chip + across
+    x = x + shifted(x, "core", 1)
+    return x + shifted(x, "xh", 1)
 
 
 def per_device(loadings, scales, cov):
@@ -60,17 +59,11 @@
     theirs = lax.ppermute(scaled, axes, other)
     first = lax.axis_index("xl") == 0
     s1 = jnp.where(first, jnp.stack([mine, theirs]), jnp.stack([theirs, mine]))
-    got = {0: s1}
-    for s in range(1, nz // 2):
-        got[-s] = shifted(s1, "z", s)
-        got[s] = shifted(s1, "z", -s)
-    got[-(nz // 2)] = shifted(got[-(nz // 2 - 1)], "z", 1)
-    rel = [got[k] if k in got else got[k - nz] for k in range(nz)]
-    rel = jnp.stack(rel + rel)
-    zme = lax.axis_index("z")
-    s2 = lax.dynamic_slice_in_dim(rel, (nz - zme) % nz, nz, 0)
-    s2 = s2.reshape(nz // nt, nt, nx, n_loads, width)
-    own = jnp.transpose(s2, (2, 0, 3, 1, 4)).reshape(nx * nz // nt, n_loads, nt * width)
+    copies = jnp.broadcast_to(s1[None], (nz,) + s1.shape)
+    s2 = lax.all_to_all(copies, "z", 0, 0)
+    s2 = jnp.swapaxes(s2, 0, 1)
+    s2 = s2.reshape(nx, nz // nt, nt, n_loads, width)
+    own = jnp.transpose(s2, (0, 1, 3, 2, 4)).reshape(nx * nz // nt, n_loads, nt * width)
     per_y = own.shape[0]
     cov_local = cov[:, :, 0, :]
     ny = lax.axis_size("y")

time: 86.9 us -> 91.8 us (1.056)
  the two profiles are of different devices: /device:TPU:2 before, /device:TPU:1 now
where the time goes in v7:
time: 91.8 us; the launch traced here: 91.6 us
  starting transfers between devices  34.9 us (38%)
  waiting for transfers between devices  33.8 us (37%)
  local copies, waits for them, and re-layouts  16.9 us (18%)
  matrix products  4.26 us (5%)
  other arithmetic  1.54 us (2%)
    all_to_all x1, waiting for transfers between devices, per_device(): s2 = lax.all_to_all(copies, 'z', 0, 0)  21.1 us
    ppermute x6, starting transfers between devices, shifted(): return lax.ppermute(x, axis, [(i, (i + by) % n) for i in range(n)])  19 us
    dynamic_slice x1, local copies, waits for them, and re-layouts, term(): lax.dynamic_slice_in_dim(cov_local, y_from % ny * per_y, per_y, 1)  11.8 us
    all_to_all x1, starting transfers between devices, per_device(): s2 = lax.all_to_all(copies, 'z', 0, 0)  9.96 us
    ppermute x6, waiting for transfers between devices, shifted(): return lax.ppermute(x, axis, [(i, (i + by) % n) for i in range(n)])  8.78 us
    dot_general x4, matrix products, term(): lax.dot_general(block, cov_part, (((0, 2), (1, 2)), ((), ())), preferred_...  4.26 us
    ppermute x1, starting transfers between devices, per_device(): theirs = lax.ppermute(scaled, axes, other)  4.04 us
    ppermute x1, waiting for transfers between devices, per_device(): mine = lax.ppermute(scaled, axes, same)  3.85 us
  transfers between devices with their start and end apart: 9, of which 6 were waited for; matrix products, arithmetic and copies ran while one was open for 19% of the time, Pallas kernels for 0%

profile of v7, /device:TPU:1, one launch (start us, length us, event | category | flops | bytes accessed | tf_op | source)
XLA Modules:
  0.0 91.6 jit_solution(875783010237450478)
XLA Ops:
  0.0 0.8 copy.16
  0.9 0.8 fusion.3
  1.7 4.0 %collective-permute-start.1 = (bf16[64,384]{1,0:T(8,128)(2,1)S(1)}, bf16[64,384]{1,0:T(8,128)(2,1)S(1)}, u32[]{:S(2)}, u32[]{:S(2)}) collective-permute-start(bf16[64,384]{1,0:T(8,128)(2,1)S(1)} %fusion.3), channel_id=1, source_target_pairs={{0,32},{1,36},{2,40},{3,44},{4,33},{5,37},{6,41},{7,45},{8,34},{9,... | collective-permute-start | bytes 147464 | tf_op jit(solution)/shard_map/ppermute | solution.py:59
  5.8 1.9 %collective-permute-start = (bf16[64,384]{1,0:T(8,128)(2,1)S(1)}, bf16[64,384]{1,0:T(8,128)(2,1)S(1)}, u32[]{:S(2)}, u32[]{:S(2)}) collective-permute-start(bf16[64,384]{1,0:T(8,128)(2,1)S(1)} %fusion.3), channel_id=1, source_target_pairs={{0,0},{1,4},{2,8},{3,12},{4,1},{5,5},{6,9},{7,13},{8,2},{9,6},{10,... | collective-permute-start | bytes 147464 | tf_op jit(solution)/shard_map/ppermute | solution.py:58
  7.7 3.9 %collective-permute-done = bf16[64,384]{1,0:T(8,128)(2,1)S(1)} collective-permute-done((bf16[64,384]{1,0:T(8,128)(2,1)S(1)}, bf16[64,384]{1,0:T(8,128)(2,1)S(1)}, u32[]{:S(2)}, u32[]{:S(2)}) %collective-permute-start) | collective-permute-done | bytes 49184 | tf_op jit(solution)/shard_map/ppermute | solution.py:58
  11.6 1.0 %broadcast_in_dim.2 = bf16[8,2,64,384]{3,2,1,0:T(8,128)(2,1)} broadcast(bf16[2,64,384]{2,1,0:T(8,128)(2,1)S(1)} %maximum_select_fusion), dimensions={1,2,3} | broadcast | bytes 884736 | tf_op jit(solution)/shard_map/broadcast_in_dim | solution.py:62
  12.6 10.0 %all-to-all-start = ((bf16[8,2,64,384]{3,2,1,0:T(8,128)(2,1)}), bf16[8,2,64,384]{3,2,1,0:T(8,128)(2,1)S(1)}, u32[]{:S(2)}, u32[]{:S(2)}) async-start(bf16[8,2,64,384]{3,2,1,0:T(8,128)(2,1)} %broadcast_in_dim.2), calls=%async_computation | async-start | bytes 1572864 | tf_op jit(solution)/shard_map/all_to_all | solution.py:63
  22.5 21.1 %all-to-all-done = bf16[8,2,64,384]{3,2,1,0:T(8,128)(2,1)S(1)} async-done(((bf16[8,2,64,384]{3,2,1,0:T(8,128)(2,1)}), bf16[8,2,64,384]{3,2,1,0:T(8,128)(2,1)S(1)}, u32[]{:S(2)}, u32[]{:S(2)}) %all-to-all-start) | async-done | bytes 786464 | tf_op jit(solution)/shard_map/all_to_all | solution.py:63
  43.6 0.6 copy.18
  44.6 1.4 %collective-permute-start.2 = (bf16[4,64,1536]{2,1,0:T(8,128)(2,1)S(1)}, bf16[4,64,1536]{2,1,0:T(8,128)(2,1)S(1)}, u32[]{:S(2)}, u32[]{:S(2)}) collective-permute-start(bf16[4,64,1536]{2,1,0:T(8,128)(2,1)S(1)} %reshape.48), channel_id=1, source_target_pairs={{0,64},{64,128},{128,192},{192,0},{1,65},{65,129},{129,193},{193,1... | collective-permute-start | bytes 2359304 | tf_op jit(solution)/shard_map/ppermute | solution.py:15
  45.9 1.5 %collective-permute-start.3 = (bf16[4,64,1536]{2,1,0:T(8,128)(2,1)S(1)}, bf16[4,64,1536]{2,1,0:T(8,128)(2,1)S(1)}, u32[]{:S(2)}, u32[]{:S(2)}) collective-permute-start(bf16[4,64,1536]{2,1,0:T(8,128)(2,1)S(1)} %reshape.48), channel_id=1, source_target_pairs={{0,192},{64,0},{128,64},{192,128},{1,193},{65,1},{129,65},{193,129... | collective-permute-start | bytes 2359304 | tf_op jit(solution)/shard_map/ppermute | solution.py:15
  47.5 11.8 %constant_dynamic-slice_fusion = (bf16[256,4,1,1536]{3,1,2,0:T(4,128)(2,1)S(1)}, bf16[256,4,1,1536]{3,1,2,0:T(4,128)(2,1)S(1)}, bf16[256,4,1,1536]{3,1,2,0:T(4,128)(2,1)S(1)}, bf16[256,4,1,1536]{3,1,2,0:T(4,128)(2,1)S(1)}) fusion(bf16[256,16,1,1536]{3,1,2,0:T(8,128)(2,1)} %param.5, s32[]{:T(128)S(6)} %select_n.52, s32[]{:T(128)S(6)} %select_n.50, ...), kind=kLoop, calls=%fused_computation.15 | loop fusion | bytes 25165840 | tf_op jit(solution)/shard_map/dynamic_slice | solution.py:73
  61.6 1.1 %convolution_bitcast_fusion.3 = f32[64,256]{1,0:T(8,128)S(1)} fusion(bf16[4,64,1536]{2,1,0:T(8,128)(2,1)S(1)} %reshape.48, bf16[256,4,1536]{2,0,1:T(8,128)(2,1)S(1)} %bitcast.45), kind=kOutput, calls=%fused_computation.10 | convolution fusion | flops 201326592 | bytes 3997696 | tf_op jit(solution)/shard_map/dot_general | solution.py:75
  62.7 2.0 %collective-permute-start.5 = (bf16[4,32,1536]{2,1,0:T(8,128)(2,1)S(1)}, bf16[4,32,1536]{2,1,0:T(8,128)(2,1)S(1)}, u32[]{:S(2)}, u32[]{:S(2)}) collective-permute-start(bf16[4,32,1536]{2,1,0:T(8,128)(2,1)S(1)} %slice.9), channel_id=1, source_target_pairs={{0,192},{64,0},{128,64},{192,128},{1,193},{65,1},{129,65},{193,129... | collective-permute-start | bytes 1179656 | tf_op jit(solution)/shard_map/ppermute | solution.py:15
  64.8 1.1 %fusion.2 = f32[64,256]{1,0:T(8,128)S(1)} fusion(f32[64,256]{1,0:T(8,128)S(1)} %convolution_bitcast_fusion.3, bf16[4,64,1536]{2,1,0:T(8,128)(2,1)S(1)} %collective-permute-done.2, bf16[256,4,1536]{2,0,1:T(8,128)(2,1)S(1)} %bitcast.48), kind=kOutput, calls=%fused_computation.9 | convolution fusion | flops 201342976 | bytes 4063232 | tf_op jit(solution)/shard_map/dot_general | solution.py:75
  65.9 1.1 %fusion.1 = f32[64,256]{1,0:T(8,128)S(1)} fusion(f32[64,256]{1,0:T(8,128)S(1)} %fusion.2, bf16[4,64,1536]{2,1,0:T(8,128)(2,1)S(1)} %collective-permute-done.3, bf16[256,4,1536]{2,0,1:T(8,128)(2,1)S(1)} %bitcast.47), kind=kOutput, calls=%fused_computation.7 | convolution fusion | flops 201342976 | bytes 4063232 | tf_op jit(solution)/shard_map/dot_general | solution.py:75
  66.9 2.8 %collective-permute-done.5 = bf16[4,32,1536]{2,1,0:T(8,128)(2,1)S(1)} collective-permute-done((bf16[4,32,1536]{2,1,0:T(8,128)(2,1)S(1)}, bf16[4,32,1536]{2,1,0:T(8,128)(2,1)S(1)}, u32[]{:S(2)}, u32[]{:S(2)}) %collective-permute-start.5) | collective-permute-done | bytes 393248 | tf_op jit(solution)/shard_map/ppermute | solution.py:15
  69.7 2.9 %collective-permute-done.4 = bf16[4,32,1536]{2,1,0:T(8,128)(2,1)S(1)} collective-permute-done((bf16[4,32,1536]{2,1,0:T(8,128)(2,1)S(1)}, bf16[4,32,1536]{2,1,0:T(8,128)(2,1)S(1)}, u32[]{:S(2)}, u32[]{:S(2)}) %collective-permute-start.4) | collective-permute-done | bytes 393248 | tf_op jit(solution)/shard_map/ppermute | solution.py:15
  72.7 1.1 %fusion = f32[64,256]{1,0:T(8,128)S(1)} fusion(f32[64,256]{1,0:T(8,128)S(1)} %fusion.1, bf16[4,64,1536]{2,1,0:T(8,128)(2,1)S(1)} %pad_maximum_fusion, bf16[256,4,1536]{2,0,1:T(8,128)(2,1)S(1)} %bitcast.46), kind=kOutput, calls=%fused_computation.5 | convolution fusion | flops 201342976 | bytes 4063232 | tf_op jit(solution)/shard_map/dot_general | solution.py:75
  73.8 5.6 %collective-permute-start.6 = (f32[64,256]{1,0:T(8,128)S(1)}, f32[64,256]{1,0:T(8,128)S(1)}, u32[]{:S(2)}, u32[]{:S(2)}) collective-permute-start(f32[64,256]{1,0:T(8,128)S(1)} %fusion), channel_id=1, source_target_pairs={{0,1},{1,0},{2,3},{3,2},{4,5},{5,4},{6,7},{7,6},{8,9},{9,8},{10,11... | collective-permute-start | bytes 196616 | tf_op jit(solution)/shard_map/ppermute | solution.py:15
  79.3 0.9 collective-permute-done.6
  80.2 8.5 %collective-permute-start.7 = (f32[64,256]{1,0:T(8,128)S(1)}, f32[64,256]{1,0:T(8,128)S(1)}, u32[]{:S(2)}, u32[]{:S(2)}) collective-permute-start(f32[64,256]{1,0:T(8,128)S(1)} %add.60), channel_id=1, source_target_pairs={{0,2},{2,0},{1,3},{3,1},{4,6},{6,4},{5,7},{7,5},{8,10},{10,8},{9,1... | collective-permute-start | bytes 196616 | tf_op jit(solution)/shard_map/ppermute | solution.py:15
  88.7 2.2 %collective-permute-done.7 = f32[64,256]{1,0:T(8,128)S(1)} collective-permute-done((f32[64,256]{1,0:T(8,128)S(1)}, f32[64,256]{1,0:T(8,128)S(1)}, u32[]{:S(2)}, u32[]{:S(2)}) %collective-permute-start.7) | collective-permute-done | bytes 65568 | tf_op jit(solution)/shard_map/ppermute | solution.py:15
  90.9 0.6 add.61
  (15 shorter events, 2.9 us)
Async XLA Ops:
  1.7 6.0 %collective-permute-start.1 = (bf16[64,384]{1,0:T(8,128)(2,1)S(1)}, bf16[64,384]{1,0:T(8,128)(2,1)S(1)}, u32[]{:S(2)}, u32[]{:S(2)}) collective-permute-start(bf16[64,384]{1,0:T(8,128)(2,1)S(1)} %fusion.3), channel_id=1, source_target_pairs={{0,32},{1,36},{2,40},{3,44},{4,33},{5,37},{6,41},{7,45},{8,34},{9,... | collective-permute-start | bytes 147464 | tf_op jit(solution)/shard_map/ppermute | solution.py:59
  5.8 5.8 %collective-permute-start = (bf16[64,384]{1,0:T(8,128)(2,1)S(1)}, bf16[64,384]{1,0:T(8,128)(2,1)S(1)}, u32[]{:S(2)}, u32[]{:S(2)}) collective-permute-start(bf16[64,384]{1,0:T(8,128)(2,1)S(1)} %fusion.3), channel_id=1, source_target_pairs={{0,0},{1,4},{2,8},{3,12},{4,1},{5,5},{6,9},{7,13},{8,2},{9,6},{10,... | collective-permute-start | bytes 147464 | tf_op jit(solution)/shard_map/ppermute | solution.py:58
  12.6 31.1 %all-to-all-start = ((bf16[8,2,64,384]{3,2,1,0:T(8,128)(2,1)}), bf16[8,2,64,384]{3,2,1,0:T(8,128)(2,1)S(1)}, u32[]{:S(2)}, u32[]{:S(2)}) async-start(bf16[8,2,64,384]{3,2,1,0:T(8,128)(2,1)} %broadcast_in_dim.2), calls=%async_computation | async-start | bytes 1572864 | tf_op jit(solution)/shard_map/all_to_all | solution.py:63
  44.6 18.1 %collective-permute-start.2 = (bf16[4,64,1536]{2,1,0:T(8,128)(2,1)S(1)}, bf16[4,64,1536]{2,1,0:T(8,128)(2,1)S(1)}, u32[]{:S(2)}, u32[]{:S(2)}) collective-permute-start(bf16[4,64,1536]{2,1,0:T(8,128)(2,1)S(1)} %reshape.48), channel_id=1, source_target_pairs={{0,64},{64,128},{128,192},{192,0},{1,65},{65,129},{129,193},{193,1... | collective-permute-start | bytes 2359304 | tf_op jit(solution)/shard_map/ppermute | solution.py:15
  45.9 16.7 %collective-permute-start.3 = (bf16[4,64,1536]{2,1,0:T(8,128)(2,1)S(1)}, bf16[4,64,1536]{2,1,0:T(8,128)(2,1)S(1)}, u32[]{:S(2)}, u32[]{:S(2)}) collective-permute-start(bf16[4,64,1536]{2,1,0:T(8,128)(2,1)S(1)} %reshape.48), channel_id=1, source_target_pairs={{0,192},{64,0},{128,64},{192,128},{1,193},{65,1},{129,65},{193,129... | collective-permute-start | bytes 2359304 | tf_op jit(solution)/shard_map/ppermute | solution.py:15
  62.7 7.0 %collective-permute-start.5 = (bf16[4,32,1536]{2,1,0:T(8,128)(2,1)S(1)}, bf16[4,32,1536]{2,1,0:T(8,128)(2,1)S(1)}, u32[]{:S(2)}, u32[]{:S(2)}) collective-permute-start(bf16[4,32,1536]{2,1,0:T(8,128)(2,1)S(1)} %slice.9), channel_id=1, source_target_pairs={{0,192},{64,0},{128,64},{192,128},{1,193},{65,1},{129,65},{193,129... | collective-permute-start | bytes 1179656 | tf_op jit(solution)/shard_map/ppermute | solution.py:15
  64.7 7.9 %collective-permute-start.4 = (bf16[4,32,1536]{2,1,0:T(8,128)(2,1)S(1)}, bf16[4,32,1536]{2,1,0:T(8,128)(2,1)S(1)}, u32[]{:S(2)}, u32[]{:S(2)}) collective-permute-start(bf16[4,32,1536]{2,1,0:T(8,128)(2,1)S(1)} %slice.8), channel_id=1, source_target_pairs={{0,64},{64,128},{128,192},{192,0},{1,65},{65,129},{129,193},{193,1... | collective-permute-start | bytes 1179656 | tf_op jit(solution)/shard_map/ppermute | solution.py:15
  73.8 6.5 %collective-permute-start.6 = (f32[64,256]{1,0:T(8,128)S(1)}, f32[64,256]{1,0:T(8,128)S(1)}, u32[]{:S(2)}, u32[]{:S(2)}) collective-permute-start(f32[64,256]{1,0:T(8,128)S(1)} %fusion), channel_id=1, source_target_pairs={{0,1},{1,0},{2,3},{3,2},{4,5},{5,4},{6,7},{7,6},{8,9},{9,8},{10,11... | collective-permute-start | bytes 196616 | tf_op jit(solution)/shard_map/ppermute | solution.py:15
  80.2 10.7 %collective-permute-start.7 = (f32[64,256]{1,0:T(8,128)S(1)}, f32[64,256]{1,0:T(8,128)S(1)}, u32[]{:S(2)}, u32[]{:S(2)}) collective-permute-start(f32[64,256]{1,0:T(8,128)S(1)} %add.60), channel_id=1, source_target_pairs={{0,2},{2,0},{1,3},{3,1},{4,6},{6,4},{5,7},{7,5},{8,10},{10,8},{9,1... | collective-permute-start | bytes 196616 | tf_op jit(solution)/shard_map/ppermute | solution.py:15

commit v8 on v3

--- a/solution.py
+++ b/solution.py
@@ -54,30 +54,34 @@
     moved = lax.ppermute(scaled, ("z", "xh", "core"), pairs)
     copies = jnp.broadcast_to(moved[None], (nx * nz,) + moved.shape)
     s2 = lax.all_to_all(copies, ("xl", "z"), 0, 0)
-    s2 = s2.reshape(nx, nz // nt, nt, n_loads, width)
-    own = jnp.transpose(s2, (0, 1, 3, 2, 4)).reshape(nx * nz // nt, n_loads, nt * width)
-    per_y = own.shape[0]
+    per_y = nx * nz // nt
     cov_local = cov[:, :, 0, :]
     ny = lax.axis_size("y")
     me = lax.axis_index("y")
+    offsets = (0, -1, 1, 2)
+    cov_parts = [
+        lax.dynamic_slice_in_dim(cov_local, ((me + k) % ny) * per_y, per_y, 1) for k in offsets
+    ]
+    s2, cov_parts = lax.optimization_barrier((s2, cov_parts))
+    s2 = s2.reshape(nx, nz // nt, nt, n_loads, width)
+    own = jnp.transpose(s2, (0, 1, 3, 2, 4)).reshape(per_y, n_loads, nt * width)
 
-    def term(block, y_from):
-        cov_part = lax.dynamic_slice_in_dim(cov_local, (y_from % ny) * per_y, per_y, 1)
-        block, cov_part = lax.optimization_barrier((block, cov_part))
+    def term(block, k):
+        block, cov_part = lax.optimization_barrier((block, cov_parts[offsets.index(k)]))
         return lax.dot_general(
             block, cov_part, (((0, 2), (1, 2)), ((), ())), preferred_element_type=jnp.float32
         )
 
     fwd = shifted(own, "y", 1)
     bwd = shifted(own, "y", -1)
-    part = term(own, me)
-    part = part + term(fwd, me - 1)
-    part = part + term(bwd, me + 1)
+    part = term(own, 0)
+    part = part + term(fwd, -1)
+    part = part + term(bwd, 1)
     half = n_loads // 2
     far_a = shifted(fwd[:, :half], "y", 1)
     far_b = shifted(bwd[:, half:], "y", -1)
     far = jnp.concatenate([far_a, far_b], axis=1)
-    part = part + term(far, me + 2)
+    part = part + term(far, 2)
     return team_sum(part)
 
 

time: 84 us -> 97.9 us (1.17)
  the two profiles are of different devices: /device:TPU:1 before, /device:TPU:94 now
where the time goes in v8:
time: 97.9 us; the launch traced here: 97.5 us
  waiting for transfers between devices  39.9 us (41%)
  local copies, waits for them, and re-layouts  32.9 us (34%)
  starting transfers between devices  17.6 us (18%)
  matrix products  5.41 us (6%)
  other arithmetic  1.52 us (2%)
    ppermute x6, waiting for transfers between devices, shifted(): return lax.ppermute(x, axis, [(i, (i + by) % n) for i in range(n)])  30.6 us
    dynamic_slice x3, local copies, waits for them, and re-layouts, per_device(): lax.dynamic_slice_in_dim(cov_local, (me + k) % ny * per_y, per_y, 1)  25.9 us
    all_to_all x1, starting transfers between devices, per_device(): s2 = lax.all_to_all(copies, ('xl', 'z'), 0, 0)  12.6 us
    all_to_all x1, waiting for transfers between devices, per_device(): s2 = lax.all_to_all(copies, ('xl', 'z'), 0, 0)  9.35 us
    dot_general x4, matrix products, term(): lax.dot_general(block, cov_part, (((0, 2), (1, 2)), ((), ())), preferred_...  5.41 us
    ppermute x6, starting transfers between devices, shifted(): return lax.ppermute(x, axis, [(i, (i + by) % n) for i in range(n)])  4.39 us
    transpose x1, local copies, waits for them, and re-layouts, per_device(): own = jnp.transpose(s2, (0, 1, 3, 2, 4)).reshape(per_y, n_loads, nt * width)  2.69 us
    reshape x1, local copies, waits for them, and re-layouts, per_device(): own = jnp.transpose(s2, (0, 1, 3, 2, 4)).reshape(per_y, n_loads, nt * width)  2.34 us
  transfers between devices with their start and end apart: 8, of which 6 were waited for; matrix products, arithmetic and copies ran while one was open for 31% of the time, Pallas kernels for 0%

profile of v8, /device:TPU:94, one launch (start us, length us, event | category | flops | bytes accessed | tf_op | source)
XLA Modules:
  0.0 97.5 jit_solution(10611582881809205584)
XLA Ops:
  0.0 0.8 copy.10
  0.9 0.8 fusion.3
  1.7 0.7 collective-permute-start
  2.5 15.1 %constant_dynamic-slice_fusion = (bf16[256,4,1,1536]{3,1,2,0:T(4,128)(2,1)}, bf16[256,4,1,1536]{3,1,2,0:T(4,128)(2,1)}, bf16[256,4,1,1536]{3,1,2,0:T(4,128)(2,1)S(1)}, bf16[256,4,1,1536]{3,1,2,0:T(4,128)(2,1)}) fusion(bf16[256,16,1,1536]{3,1,2,0:T(8,128)(2,1)} %param.5, s32[]{:T(128)S(6)} %select_n.38, s32[]{:T(128)S(6)} %select_n.36, s32[]{:T(128)S(6)} %select_n.34, ...), kind=kLoop, calls=%fused_computation.14 | loop fusion | bytes 25165840 | tf_op jit(solution)/shard_map/dynamic_slice | solution.py:63
  17.6 1.0 %broadcast_in_dim.2 = bf16[16,64,384]{2,1,0:T(8,128)(2,1)} broadcast(bf16[64,384]{1,0:T(8,128)(2,1)S(1)} %collective-permute-done), dimensions={1,2} | broadcast | bytes 835584 | tf_op jit(solution)/shard_map/broadcast_in_dim | solution.py:55
  18.6 12.6 %all-to-all-start = ((bf16[16,64,384]{2,1,0:T(8,128)(2,1)}), bf16[16,64,384]{2,1,0:T(8,128)(2,1)}, u32[]{:S(2)}, u32[]{:S(2)}) async-start(bf16[16,64,384]{2,1,0:T(8,128)(2,1)} %broadcast_in_dim.2), calls=%async_computation | async-start | bytes 1572864 | tf_op jit(solution)/shard_map/all_to_all | solution.py:56
  31.2 6.9 %copy_bitcast_fusion = (bf16[256,4,1536]{2,0,1:T(8,128)(2,1)}, bf16[256,4,1536]{2,0,1:T(8,128)(2,1)}) fusion(bf16[256,4,1,1536]{3,1,2,0:T(4,128)(2,1)} %get-tuple-element.31, bf16[256,4,1,1536]{3,1,2,0:T(4,128)(2,1)} %get-tuple-element.32), kind=kLoop, calls=%fused_computation | loop fusion | bytes 12582912 | tf_op jit(solution)/shard_map/dynamic_slice | solution.py:63
  38.1 3.9 %copy_bitcast_fusion.2 = (bf16[256,4,1536]{2,0,1:T(8,128)(2,1)}, bf16[256,4,1536]{2,0,1:T(8,128)(2,1)}) fusion(bf16[256,4,1,1536]{3,1,2,0:T(4,128)(2,1)S(1)} %get-tuple-element.33, bf16[256,4,1,1536]{3,1,2,0:T(4,128)(2,1)S(1)} %copy-done), kind=kLoop, calls=%fused_computation.2 | loop fusion | bytes 12582912 | tf_op jit(solution)/shard_map/dynamic_slice | solution.py:63
  41.9 9.4 %all-to-all-done = bf16[16,64,384]{2,1,0:T(8,128)(2,1)} async-done(((bf16[16,64,384]{2,1,0:T(8,128)(2,1)}), bf16[16,64,384]{2,1,0:T(8,128)(2,1)}, u32[]{:S(2)}, u32[]{:S(2)}) %all-to-all-start) | async-done | bytes 786464 | tf_op jit(solution)/shard_map/all_to_all | solution.py:56
  51.3 2.7 %copy.15 = bf16[2,2,64,4,384]{4,3,2,1,0:T(4,128)(2,1)} copy(bf16[2,2,64,4,384]{4,2,3,1,0:T(8,128)(2,1)} %bitcast.5) | data formatting | bytes 1572864 | tf_op jit(solution)/shard_map/transpose | solution.py:67
  54.0 2.3 %reshape.16 = bf16[4,64,1536]{2,1,0:T(8,128)(2,1)} reshape(bf16[2,2,64,4,384]{4,3,2,1,0:T(4,128)(2,1)} %copy.15) | data formatting | bytes 1572864 | tf_op jit(solution)/shard_map/reshape | solution.py:67
  56.5 1.8 %collective-permute-start.2 = (bf16[4,64,1536]{2,1,0:T(8,128)(2,1)}, bf16[4,64,1536]{2,1,0:T(8,128)(2,1)S(1)}, u32[]{:S(2)}, u32[]{:S(2)}) collective-permute-start(bf16[4,64,1536]{2,1,0:T(8,128)(2,1)} %reshape.16), channel_id=1, source_target_pairs={{0,192},{64,0},{128,64},{192,128},{1,193},{65,1},{129,65},{193,129... | collective-permute-start | bytes 2359304 | tf_op jit(solution)/shard_map/ppermute | solution.py:15
  58.3 2.2 %convolution_bitcast_fusion.3 = f32[64,256]{1,0:T(8,128)S(1)} fusion(bf16[4,64,1536]{2,1,0:T(8,128)(2,1)} %reshape.16, bf16[256,4,1536]{2,0,1:T(8,128)(2,1)S(1)} %copy-done.4), kind=kOutput, calls=%fused_computation.10 | convolution fusion | flops 201326592 | bytes 3997696 | tf_op jit(solution)/shard_map/dot_general | solution.py:71
  60.6 15.3 %collective-permute-done.1 = bf16[4,64,1536]{2,1,0:T(8,128)(2,1)S(1)} collective-permute-done((bf16[4,64,1536]{2,1,0:T(8,128)(2,1)}, bf16[4,64,1536]{2,1,0:T(8,128)(2,1)S(1)}, u32[]{:S(2)}, u32[]{:S(2)}) %collective-permute-start.1) | collective-permute-done | bytes 786464 | tf_op jit(solution)/shard_map/ppermute | solution.py:15
  75.9 1.6 %collective-permute-start.3 = (bf16[4,32,1536]{2,1,0:T(8,128)(2,1)S(1)}, bf16[4,32,1536]{2,1,0:T(8,128)(2,1)S(1)}, u32[]{:S(2)}, u32[]{:S(2)}) collective-permute-start(bf16[4,32,1536]{2,1,0:T(8,128)(2,1)S(1)} %slice.8), channel_id=1, source_target_pairs={{0,64},{64,128},{128,192},{192,0},{1,65},{65,129},{129,193},{193,1... | collective-permute-start | bytes 1179656 | tf_op jit(solution)/shard_map/ppermute | solution.py:15
  77.5 0.6 collective-permute-start.4
  78.1 1.1 %fusion.2 = f32[64,256]{1,0:T(8,128)S(1)} fusion(f32[64,256]{1,0:T(8,128)S(1)} %convolution_bitcast_fusion.3, bf16[4,64,1536]{2,1,0:T(8,128)(2,1)S(1)} %collective-permute-done.1, bf16[256,4,1536]{2,0,1:T(8,128)(2,1)S(1)} %copy-done.3), kind=kOutput, calls=%fused_computation.9 | convolution fusion | flops 201342976 | bytes 4063232 | tf_op jit(solution)/shard_map/dot_general | solution.py:71
  79.2 1.1 %fusion.1 = f32[64,256]{1,0:T(8,128)S(1)} fusion(f32[64,256]{1,0:T(8,128)S(1)} %fusion.2, bf16[4,64,1536]{2,1,0:T(8,128)(2,1)S(1)} %collective-permute-done.2, bf16[256,4,1536]{2,0,1:T(8,128)(2,1)S(1)} %copy-done.2), kind=kOutput, calls=%fused_computation.7 | convolution fusion | flops 201342976 | bytes 4063232 | tf_op jit(solution)/shard_map/dot_general | solution.py:71
  80.2 5.7 %collective-permute-done.3 = bf16[4,32,1536]{2,1,0:T(8,128)(2,1)S(1)} collective-permute-done((bf16[4,32,1536]{2,1,0:T(8,128)(2,1)S(1)}, bf16[4,32,1536]{2,1,0:T(8,128)(2,1)S(1)}, u32[]{:S(2)}, u32[]{:S(2)}) %collective-permute-start.3) | collective-permute-done | bytes 393248 | tf_op jit(solution)/shard_map/ppermute | solution.py:15
  85.9 2.6 %collective-permute-done.4 = bf16[4,32,1536]{2,1,0:T(8,128)(2,1)S(1)} collective-permute-done((bf16[4,32,1536]{2,1,0:T(8,128)(2,1)S(1)}, bf16[4,32,1536]{2,1,0:T(8,128)(2,1)S(1)}, u32[]{:S(2)}, u32[]{:S(2)}) %collective-permute-start.4) | collective-permute-done | bytes 393248 | tf_op jit(solution)/shard_map/ppermute | solution.py:15
  88.6 1.1 %fusion = f32[64,256]{1,0:T(8,128)S(1)} fusion(f32[64,256]{1,0:T(8,128)S(1)} %fusion.1, bf16[4,64,1536]{2,1,0:T(8,128)(2,1)S(1)} %pad_maximum_fusion, bf16[256,4,1536]{2,0,1:T(8,128)(2,1)S(1)} %copy-done.1), kind=kOutput, calls=%fused_computation.5 | convolution fusion | flops 201342976 | bytes 4063232 | tf_op jit(solution)/shard_map/dot_general | solution.py:71
  89.8 1.2 %collective-permute-done.5 = f32[64,256]{1,0:T(8,128)S(1)} collective-permute-done((f32[64,256]{1,0:T(8,128)S(1)}, f32[64,256]{1,0:T(8,128)S(1)}, u32[]{:S(2)}, u32[]{:S(2)}) %collective-permute-start.5) | collective-permute-done | bytes 65568 | tf_op jit(solution)/shard_map/ppermute | solution.py:15
  91.1 5.8 %collective-permute-done.6 = f32[64,256]{1,0:T(8,128)S(1)} collective-permute-done((f32[64,256]{1,0:T(8,128)S(1)}, f32[64,256]{1,0:T(8,128)S(1)}, u32[]{:S(2)}, u32[]{:S(2)}) %collective-permute-start.6) | collective-permute-done | bytes 65568 | tf_op jit(solution)/shard_map/ppermute | solution.py:15
  96.9 0.6 add.64
  (20 shorter events, 0.7 us)
Async XLA Ops:
  1.7 15.8 %collective-permute-start = (bf16[64,384]{1,0:T(8,128)(2,1)S(1)}, bf16[64,384]{1,0:T(8,128)(2,1)S(1)}, u32[]{:S(2)}, u32[]{:S(2)}) collective-permute-start(bf16[64,384]{1,0:T(8,128)(2,1)S(1)} %fusion.3), channel_id=1, source_target_pairs={{0,0},{1,4},{2,8},{3,12},{4,1},{5,5},{6,9},{7,13},{8,2},{9,6},{10,... | collective-permute-start | bytes 147464 | tf_op jit(solution)/shard_map/ppermute | solution.py:54
  18.6 32.7 %all-to-all-start = ((bf16[16,64,384]{2,1,0:T(8,128)(2,1)}), bf16[16,64,384]{2,1,0:T(8,128)(2,1)}, u32[]{:S(2)}, u32[]{:S(2)}) async-start(bf16[16,64,384]{2,1,0:T(8,128)(2,1)} %broadcast_in_dim.2), calls=%async_computation | async-start | bytes 1572864 | tf_op jit(solution)/shard_map/all_to_all | solution.py:56
  31.2 6.9 %copy-start = (bf16[256,4,1,1536]{3,1,2,0:T(4,128)(2,1)S(1)}, bf16[256,4,1,1536]{3,1,2,0:T(4,128)(2,1)}, u32[]{:S(2)}) copy-start(bf16[256,4,1,1536]{3,1,2,0:T(4,128)(2,1)} %get-tuple-element.34) | copy-start | bytes 9437188
  41.9 16.4 %copy-start.4 = (bf16[256,4,1536]{2,0,1:T(8,128)(2,1)S(1)}, bf16[256,4,1536]{2,0,1:T(8,128)(2,1)}, u32[]{:S(2)}) copy-start(bf16[256,4,1536]{2,0,1:T(8,128)(2,1)} %get-tuple-element.21) | copy-start | bytes 9437188
  56.3 21.8 %copy-start.3 = (bf16[256,4,1536]{2,0,1:T(8,128)(2,1)S(1)}, bf16[256,4,1536]{2,0,1:T(8,128)(2,1)}, u32[]{:S(2)}) copy-start(bf16[256,4,1536]{2,0,1:T(8,128)(2,1)} %get-tuple-element.24) | copy-start | bytes 9437188
  56.3 19.5 %collective-permute-start.1 = (bf16[4,64,1536]{2,1,0:T(8,128)(2,1)}, bf16[4,64,1536]{2,1,0:T(8,128)(2,1)S(1)}, u32[]{:S(2)}, u32[]{:S(2)}) collective-permute-start(bf16[4,64,1536]{2,1,0:T(8,128)(2,1)} %reshape.16), channel_id=1, source_target_pairs={{0,64},{64,128},{128,192},{192,0},{1,65},{65,129},{129,193},{193,1... | collective-permute-start | bytes 2359304 | tf_op jit(solution)/shard_map/ppermute | solution.py:15
  56.5 20.9 %collective-permute-start.2 = (bf16[4,64,1536]{2,1,0:T(8,128)(2,1)}, bf16[4,64,1536]{2,1,0:T(8,128)(2,1)S(1)}, u32[]{:S(2)}, u32[]{:S(2)}) collective-permute-start(bf16[4,64,1536]{2,1,0:T(8,128)(2,1)} %reshape.16), channel_id=1, source_target_pairs={{0,192},{64,0},{128,64},{192,128},{1,193},{65,1},{129,65},{193,129... | collective-permute-start | bytes 2359304 | tf_op jit(solution)/shard_map/ppermute | solution.py:15
  60.6 18.6 %copy-start.2 = (bf16[256,4,1536]{2,0,1:T(8,128)(2,1)S(1)}, bf16[256,4,1536]{2,0,1:T(8,128)(2,1)}, u32[]{:S(2)}) copy-start(bf16[256,4,1536]{2,0,1:T(8,128)(2,1)} %get-tuple-element.27) | copy-start | bytes 9437188
  75.9 10.1 %collective-permute-start.3 = (bf16[4,32,1536]{2,1,0:T(8,128)(2,1)S(1)}, bf16[4,32,1536]{2,1,0:T(8,128)(2,1)S(1)}, u32[]{:S(2)}, u32[]{:S(2)}) collective-permute-start(bf16[4,32,1536]{2,1,0:T(8,128)(2,1)S(1)} %slice.8), channel_id=1, source_target_pairs={{0,64},{64,128},{128,192},{192,0},{1,65},{65,129},{129,193},{193,1... | collective-permute-start | bytes 1179656 | tf_op jit(solution)/shard_map/ppermute | solution.py:15
  77.5 11.1 %collective-permute-start.4 = (bf16[4,32,1536]{2,1,0:T(8,128)(2,1)S(1)}, bf16[4,32,1536]{2,1,0:T(8,128)(2,1)S(1)}, u32[]{:S(2)}, u32[]{:S(2)}) collective-permute-start(bf16[4,32,1536]{2,1,0:T(8,128)(2,1)S(1)} %slice.9), channel_id=1, source_target_pairs={{0,192},{64,0},{128,64},{192,128},{1,193},{65,1},{129,65},{193,129... | collective-permute-start | bytes 1179656 | tf_op jit(solution)/shard_map/ppermute | solution.py:15
  79.1 9.5 %copy-start.1 = (bf16[256,4,1536]{2,0,1:T(8,128)(2,1)S(1)}, bf16[256,4,1536]{2,0,1:T(8,128)(2,1)}, u32[]{:S(2)}) copy-start(bf16[256,4,1536]{2,0,1:T(8,128)(2,1)} %get-tuple-element.30) | copy-start | bytes 9437188
  89.7 1.3 %collective-permute-start.5 = (f32[64,256]{1,0:T(8,128)S(1)}, f32[64,256]{1,0:T(8,128)S(1)}, u32[]{:S(2)}, u32[]{:S(2)}) collective-permute-start(f32[64,256]{1,0:T(8,128)S(1)} %fusion), channel_id=1, source_target_pairs={{0,1},{1,0},{2,3},{3,2},{4,5},{5,4},{6,7},{7,6},{8,9},{9,8},{10,11... | collective-permute-start | bytes 196616 | tf_op jit(solution)/shard_map/ppermute | solution.py:15
  91.0 5.9 %collective-permute-start.6 = (f32[64,256]{1,0:T(8,128)S(1)}, f32[64,256]{1,0:T(8,128)S(1)}, u32[]{:S(2)}, u32[]{:S(2)}) collective-permute-start(f32[64,256]{1,0:T(8,128)S(1)} %add.63), channel_id=1, source_target_pairs={{0,2},{2,0},{1,3},{3,1},{4,6},{6,4},{5,7},{7,5},{8,10},{10,8},{9,1... | collective-permute-start | bytes 196616 | tf_op jit(solution)/shard_map/ppermute | solution.py:15

commit v9 on v3

--- a/solution.py
+++ b/solution.py
@@ -77,8 +77,7 @@
     far_a = shifted(fwd[:, :half], "y", 1)
     far_b = shifted(bwd[:, half:], "y", -1)
     far = jnp.concatenate([far_a, far_b], axis=1)
-    part = part + term(far, me + 2)
-    return team_sum(part)
+    return team_sum(part) + team_sum(term(far, me + 2))
 
 
 def solution(mesh):

time: 84 us -> 82.9 us (0.987)
  waiting for transfers between devices: 27.8 us -> 22.9 us
  starting transfers between devices: 33 us -> 37 us
    ppermute x6 -> x8, waiting for transfers between devices: 8.7 us -> 3.84 us  [shifted(): return lax.ppermute(x, axis, [(i, (i + by) % n) for i in range(n)])]
    ppermute x6 -> x8, starting transfers between devices: 17.4 us -> 21.3 us  [shifted(): return lax.ppermute(x, axis, [(i, (i + by) % n) for i in range(n)])]
  transfers between devices with their start and end apart: 8 -> 10, of which waited for: 6 -> 4; matrix products, arithmetic and copies ran while one was open for 21% -> 22% of each run, Pallas kernels for 0% -> 0%
where the time goes in v9:
time: 82.9 us; the launch traced here: 82.6 us
  starting transfers between devices  37 us (45%)
  waiting for transfers between devices  22.9 us (28%)
  local copies, waits for them, and re-layouts  16.7 us (20%)
  matrix products  4.26 us (5%)
  other arithmetic  1.54 us (2%)
    ppermute x8, starting transfers between devices, shifted(): return lax.ppermute(x, axis, [(i, (i + by) % n) for i in range(n)])  21.3 us
    all_to_all x1, waiting for transfers between devices, per_device(): s2 = lax.all_to_all(copies, ('xl', 'z'), 0, 0)  17.3 us
    dynamic_slice x1, local copies, waits for them, and re-layouts, term(): lax.dynamic_slice_in_dim(cov_local, y_from % ny * per_y, per_y, 1)  11.6 us
    all_to_all x1, starting transfers between devices, per_device(): s2 = lax.all_to_all(copies, ('xl', 'z'), 0, 0)  10.7 us
    ppermute x1, starting transfers between devices, per_device(): moved = lax.ppermute(scaled, ('z', 'xh', 'core'), pairs)  4.94 us
    dot_general x4, matrix products, term(): lax.dot_general(block, cov_part, (((0, 2), (1, 2)), ((), ())), preferred_...  4.26 us
    ppermute x8, waiting for transfers between devices, shifted(): return lax.ppermute(x, axis, [(i, (i + by) % n) for i in range(n)])  3.84 us
    unnamed x4, local copies, waits for them, and re-layouts  2.28 us
  transfers between devices with their start and end apart: 10, of which 4 were waited for; matrix products, arithmetic and copies ran while one was open for 22% of the time, Pallas kernels for 0%

profile of v9, /device:TPU:1, one launch (start us, length us, event | category | flops | bytes accessed | tf_op | source)
XLA Modules:
  0.0 82.6 jit_solution(9601923378706380881)
XLA Ops:
  0.0 0.8 copy.10
  0.9 0.8 fusion.2
  1.7 4.9 %collective-permute-start = (bf16[64,384]{1,0:T(8,128)(2,1)S(1)}, bf16[64,384]{1,0:T(8,128)(2,1)S(1)}, u32[]{:S(2)}, u32[]{:S(2)}) collective-permute-start(bf16[64,384]{1,0:T(8,128)(2,1)S(1)} %fusion.2), channel_id=1, source_target_pairs={{0,0},{1,4},{2,8},{3,12},{4,1},{5,5},{6,9},{7,13},{8,2},{9,6},{10,... | collective-permute-start | bytes 147464 | tf_op jit(solution)/shard_map/ppermute | solution.py:54
  6.7 1.8 %collective-permute-done = bf16[64,384]{1,0:T(8,128)(2,1)S(1)} collective-permute-done((bf16[64,384]{1,0:T(8,128)(2,1)S(1)}, bf16[64,384]{1,0:T(8,128)(2,1)S(1)}, u32[]{:S(2)}, u32[]{:S(2)}) %collective-permute-start) | collective-permute-done | bytes 49184 | tf_op jit(solution)/shard_map/ppermute | solution.py:54
  8.4 1.0 %broadcast_in_dim.2 = bf16[16,64,384]{2,1,0:T(8,128)(2,1)} broadcast(bf16[64,384]{1,0:T(8,128)(2,1)S(1)} %collective-permute-done), dimensions={1,2} | broadcast | bytes 835584 | tf_op jit(solution)/shard_map/broadcast_in_dim | solution.py:55
  9.4 10.7 %all-to-all-start = ((bf16[16,64,384]{2,1,0:T(8,128)(2,1)}), bf16[16,64,384]{2,1,0:T(8,128)(2,1)S(1)}, u32[]{:S(2)}, u32[]{:S(2)}) async-start(bf16[16,64,384]{2,1,0:T(8,128)(2,1)} %broadcast_in_dim.2), calls=%async_computation | async-start | bytes 1572864 | tf_op jit(solution)/shard_map/all_to_all | solution.py:56
  20.2 17.3 %all-to-all-done = bf16[16,64,384]{2,1,0:T(8,128)(2,1)S(1)} async-done(((bf16[16,64,384]{2,1,0:T(8,128)(2,1)}), bf16[16,64,384]{2,1,0:T(8,128)(2,1)S(1)}, u32[]{:S(2)}, u32[]{:S(2)}) %all-to-all-start) | async-done | bytes 786464 | tf_op jit(solution)/shard_map/all_to_all | solution.py:56
  37.5 0.6 copy.11
  38.4 1.4 %collective-permute-start.1 = (bf16[4,64,1536]{2,1,0:T(8,128)(2,1)S(1)}, bf16[4,64,1536]{2,1,0:T(8,128)(2,1)S(1)}, u32[]{:S(2)}, u32[]{:S(2)}) collective-permute-start(bf16[4,64,1536]{2,1,0:T(8,128)(2,1)S(1)} %reshape.16), channel_id=1, source_target_pairs={{0,64},{64,128},{128,192},{192,0},{1,65},{65,129},{129,193},{193,1... | collective-permute-start | bytes 2359304 | tf_op jit(solution)/shard_map/ppermute | solution.py:15
  39.8 1.5 %collective-permute-start.2 = (bf16[4,64,1536]{2,1,0:T(8,128)(2,1)S(1)}, bf16[4,64,1536]{2,1,0:T(8,128)(2,1)S(1)}, u32[]{:S(2)}, u32[]{:S(2)}) collective-permute-start(bf16[4,64,1536]{2,1,0:T(8,128)(2,1)S(1)} %reshape.16), channel_id=1, source_target_pairs={{0,192},{64,0},{128,64},{192,128},{1,193},{65,1},{129,65},{193,129... | collective-permute-start | bytes 2359304 | tf_op jit(solution)/shard_map/ppermute | solution.py:15
  41.3 11.6 %constant_dynamic-slice_fusion.1 = (bf16[256,4,1,1536]{3,1,2,0:T(4,128)(2,1)S(1)}, bf16[256,4,1,1536]{3,1,2,0:T(4,128)(2,1)S(1)}, bf16[256,4,1,1536]{3,1,2,0:T(4,128)(2,1)S(1)}, bf16[256,4,1,1536]{3,1,2,0:T(4,128)(2,1)S(1)}) fusion(bf16[256,16,1,1536]{3,1,2,0:T(8,128)(2,1)} %param.5, s32[]{:T(128)S(6)} %select_n.36, s32[]{:T(128)S(6)} %select_n.34, ...), kind=kLoop, calls=%fused_computation.15 | loop fusion | bytes 25165840 | tf_op jit(solution)/shard_map/dynamic_slice | solution.py:65
  52.9 0.6 copy.29
  55.2 1.1 %convolution_bitcast_fusion.3 = f32[64,256]{1,0:T(8,128)S(1)} fusion(bf16[4,64,1536]{2,1,0:T(8,128)(2,1)S(1)} %reshape.16, bf16[256,4,1536]{2,0,1:T(8,128)(2,1)S(1)} %bitcast.41), kind=kOutput, calls=%fused_computation.9 | convolution fusion | flops 201326592 | bytes 3997696 | tf_op jit(solution)/shard_map/dot_general | solution.py:67
  56.5 2.7 %collective-permute-start.6 = (bf16[4,32,1536]{2,1,0:T(8,128)(2,1)S(1)}, bf16[4,32,1536]{2,1,0:T(8,128)(2,1)S(1)}, u32[]{:S(2)}, u32[]{:S(2)}) collective-permute-start(bf16[4,32,1536]{2,1,0:T(8,128)(2,1)S(1)} %slice.9), channel_id=1, source_target_pairs={{0,192},{64,0},{128,64},{192,128},{1,193},{65,1},{129,65},{193,129... | collective-permute-start | bytes 1179656 | tf_op jit(solution)/shard_map/ppermute | solution.py:15
  59.2 1.1 %fusion.1 = f32[64,256]{1,0:T(8,128)S(1)} fusion(f32[64,256]{1,0:T(8,128)S(1)} %convolution_bitcast_fusion.3, bf16[4,64,1536]{2,1,0:T(8,128)(2,1)S(1)} %collective-permute-done.1, bf16[256,4,1536]{2,0,1:T(8,128)(2,1)S(1)} %bitcast.43), kind=kOutput, calls=%fused_computation.8 | convolution fusion | flops 201342976 | bytes 4063232 | tf_op jit(solution)/shard_map/dot_general | solution.py:67
  60.3 1.1 %fusion = f32[64,256]{1,0:T(8,128)S(1)} fusion(f32[64,256]{1,0:T(8,128)S(1)} %fusion.1, bf16[4,64,1536]{2,1,0:T(8,128)(2,1)S(1)} %collective-permute-done.2, bf16[256,4,1536]{2,0,1:T(8,128)(2,1)S(1)} %bitcast.42), kind=kOutput, calls=%fused_computation.6 | convolution fusion | flops 201342976 | bytes 4063232 | tf_op jit(solution)/shard_map/dot_general | solution.py:67
  61.3 5.7 %collective-permute-start.3 = (f32[64,256]{1,0:T(8,128)S(1)}, f32[64,256]{1,0:T(8,128)S(1)}, u32[]{:S(2)}, u32[]{:S(2)}) collective-permute-start(f32[64,256]{1,0:T(8,128)S(1)} %fusion), channel_id=1, source_target_pairs={{0,1},{1,0},{2,3},{3,2},{4,5},{5,4},{6,7},{7,6},{8,9},{9,8},{10,11... | collective-permute-start | bytes 196616 | tf_op jit(solution)/shard_map/ppermute | solution.py:15
  67.1 1.1 %convolution_bitcast_fusion = f32[64,256]{1,0:T(8,128)S(1)} fusion(bf16[4,64,1536]{2,1,0:T(8,128)(2,1)S(1)} %pad_maximum_fusion, bf16[256,4,1536]{2,0,1:T(8,128)(2,1)S(1)} %bitcast.40), kind=kOutput, calls=%fused_computation.4 | convolution fusion | flops 201326592 | bytes 3997696 | tf_op jit(solution)/shard_map/dot_general | solution.py:67
  68.2 3.5 %collective-permute-start.7 = (f32[64,256]{1,0:T(8,128)S(1)}, f32[64,256]{1,0:T(8,128)S(1)}, u32[]{:S(2)}, u32[]{:S(2)}) collective-permute-start(f32[64,256]{1,0:T(8,128)S(1)} %convolution_bitcast_fusion), channel_id=1, source_target_pairs={{0,1},{1,0},{2,3},{3,2},{4,5},{5,4},{6,7},{7,6},{8,9},{9,8},{10,11... | collective-permute-start | bytes 196616 | tf_op jit(solution)/shard_map/ppermute | solution.py:15
  71.7 5.5 %collective-permute-start.4 = (f32[64,256]{1,0:T(8,128)S(1)}, f32[64,256]{1,0:T(8,128)S(1)}, u32[]{:S(2)}, u32[]{:S(2)}) collective-permute-start(f32[64,256]{1,0:T(8,128)S(1)} %add.62), channel_id=1, source_target_pairs={{0,2},{2,0},{1,3},{3,1},{4,6},{6,4},{5,7},{7,5},{8,10},{10,8},{9,1... | collective-permute-start | bytes 196616 | tf_op jit(solution)/shard_map/ppermute | solution.py:15
  77.2 0.9 %collective-permute-start.8 = (f32[64,256]{1,0:T(8,128)S(1)}, f32[64,256]{1,0:T(8,128)S(1)}, u32[]{:S(2)}, u32[]{:S(2)}) collective-permute-start(f32[64,256]{1,0:T(8,128)S(1)} %add.67), channel_id=1, source_target_pairs={{0,2},{2,0},{1,3},{3,1},{4,6},{6,4},{5,7},{7,5},{8,10},{10,8},{9,1... | collective-permute-start | bytes 196616 | tf_op jit(solution)/shard_map/ppermute | solution.py:15
  78.1 1.5 %collective-permute-done.4 = f32[64,256]{1,0:T(8,128)S(1)} collective-permute-done((f32[64,256]{1,0:T(8,128)S(1)}, f32[64,256]{1,0:T(8,128)S(1)}, u32[]{:S(2)}, u32[]{:S(2)}) %collective-permute-start.4) | collective-permute-done | bytes 65568 | tf_op jit(solution)/shard_map/ppermute | solution.py:15
  79.7 2.3 %collective-permute-done.8 = f32[64,256]{1,0:T(8,128)S(1)} collective-permute-done((f32[64,256]{1,0:T(8,128)S(1)}, f32[64,256]{1,0:T(8,128)S(1)}, u32[]{:S(2)}, u32[]{:S(2)}) %collective-permute-start.8) | collective-permute-done | bytes 65568 | tf_op jit(solution)/shard_map/ppermute | solution.py:15
  82.0 0.6 add_add_fusion
  (17 shorter events, 2.4 us)
Async XLA Ops:
  1.7 6.7 %collective-permute-start = (bf16[64,384]{1,0:T(8,128)(2,1)S(1)}, bf16[64,384]{1,0:T(8,128)(2,1)S(1)}, u32[]{:S(2)}, u32[]{:S(2)}) collective-permute-start(bf16[64,384]{1,0:T(8,128)(2,1)S(1)} %fusion.2), channel_id=1, source_target_pairs={{0,0},{1,4},{2,8},{3,12},{4,1},{5,5},{6,9},{7,13},{8,2},{9,6},{10,... | collective-permute-start | bytes 147464 | tf_op jit(solution)/shard_map/ppermute | solution.py:54
  9.4 28.1 %all-to-all-start = ((bf16[16,64,384]{2,1,0:T(8,128)(2,1)}), bf16[16,64,384]{2,1,0:T(8,128)(2,1)S(1)}, u32[]{:S(2)}, u32[]{:S(2)}) async-start(bf16[16,64,384]{2,1,0:T(8,128)(2,1)} %broadcast_in_dim.2), calls=%async_computation | async-start | bytes 1572864 | tf_op jit(solution)/shard_map/all_to_all | solution.py:56
  38.4 17.9 %collective-permute-start.1 = (bf16[4,64,1536]{2,1,0:T(8,128)(2,1)S(1)}, bf16[4,64,1536]{2,1,0:T(8,128)(2,1)S(1)}, u32[]{:S(2)}, u32[]{:S(2)}) collective-permute-start(bf16[4,64,1536]{2,1,0:T(8,128)(2,1)S(1)} %reshape.16), channel_id=1, source_target_pairs={{0,64},{64,128},{128,192},{192,0},{1,65},{65,129},{129,193},{193,1... | collective-permute-start | bytes 2359304 | tf_op jit(solution)/shard_map/ppermute | solution.py:15
  39.8 16.6 %collective-permute-start.2 = (bf16[4,64,1536]{2,1,0:T(8,128)(2,1)S(1)}, bf16[4,64,1536]{2,1,0:T(8,128)(2,1)S(1)}, u32[]{:S(2)}, u32[]{:S(2)}) collective-permute-start(bf16[4,64,1536]{2,1,0:T(8,128)(2,1)S(1)} %reshape.16), channel_id=1, source_target_pairs={{0,192},{64,0},{128,64},{192,128},{1,193},{65,1},{129,65},{193,129... | collective-permute-start | bytes 2359304 | tf_op jit(solution)/shard_map/ppermute | solution.py:15
  56.3 10.7 %collective-permute-start.5 = (bf16[4,32,1536]{2,1,0:T(8,128)(2,1)S(1)}, bf16[4,32,1536]{2,1,0:T(8,128)(2,1)S(1)}, u32[]{:S(2)}, u32[]{:S(2)}) collective-permute-start(bf16[4,32,1536]{2,1,0:T(8,128)(2,1)S(1)} %slice.8), channel_id=1, source_target_pairs={{0,64},{64,128},{128,192},{192,0},{1,65},{65,129},{129,193},{193,1... | collective-permute-start | bytes 1179656 | tf_op jit(solution)/shard_map/ppermute | solution.py:15
  56.5 10.6 %collective-permute-start.6 = (bf16[4,32,1536]{2,1,0:T(8,128)(2,1)S(1)}, bf16[4,32,1536]{2,1,0:T(8,128)(2,1)S(1)}, u32[]{:S(2)}, u32[]{:S(2)}) collective-permute-start(bf16[4,32,1536]{2,1,0:T(8,128)(2,1)S(1)} %slice.9), channel_id=1, source_target_pairs={{0,192},{64,0},{128,64},{192,128},{1,193},{65,1},{129,65},{193,129... | collective-permute-start | bytes 1179656 | tf_op jit(solution)/shard_map/ppermute | solution.py:15
  61.3 10.4 %collective-permute-start.3 = (f32[64,256]{1,0:T(8,128)S(1)}, f32[64,256]{1,0:T(8,128)S(1)}, u32[]{:S(2)}, u32[]{:S(2)}) collective-permute-start(f32[64,256]{1,0:T(8,128)S(1)} %fusion), channel_id=1, source_target_pairs={{0,1},{1,0},{2,3},{3,2},{4,5},{5,4},{6,7},{7,6},{8,9},{9,8},{10,11... | collective-permute-start | bytes 196616 | tf_op jit(solution)/shard_map/ppermute | solution.py:15
  68.2 9.0 %collective-permute-start.7 = (f32[64,256]{1,0:T(8,128)S(1)}, f32[64,256]{1,0:T(8,128)S(1)}, u32[]{:S(2)}, u32[]{:S(2)}) collective-permute-start(f32[64,256]{1,0:T(8,128)S(1)} %convolution_bitcast_fusion), channel_id=1, source_target_pairs={{0,1},{1,0},{2,3},{3,2},{4,5},{5,4},{6,7},{7,6},{8,9},{9,8},{10,11... | collective-permute-start | bytes 196616 | tf_op jit(solution)/shard_map/ppermute | solution.py:15
  71.7 8.0 %collective-permute-start.4 = (f32[64,256]{1,0:T(8,128)S(1)}, f32[64,256]{1,0:T(8,128)S(1)}, u32[]{:S(2)}, u32[]{:S(2)}) collective-permute-start(f32[64,256]{1,0:T(8,128)S(1)} %add.62), channel_id=1, source_target_pairs={{0,2},{2,0},{1,3},{3,1},{4,6},{6,4},{5,7},{7,5},{8,10},{10,8},{9,1... | collective-permute-start | bytes 196616 | tf_op jit(solution)/shard_map/ppermute | solution.py:15
  77.2 4.7 %collective-permute-start.8 = (f32[64,256]{1,0:T(8,128)S(1)}, f32[64,256]{1,0:T(8,128)S(1)}, u32[]{:S(2)}, u32[]{:S(2)}) collective-permute-start(f32[64,256]{1,0:T(8,128)S(1)} %add.67), channel_id=1, source_target_pairs={{0,2},{2,0},{1,3},{3,1},{4,6},{6,4},{5,7},{7,5},{8,10},{10,8},{9,1... | collective-permute-start | bytes 196616 | tf_op jit(solution)/shard_map/ppermute | solution.py:15

commit v10 on v9

--- a/solution.py
+++ b/solution.py
@@ -77,7 +77,8 @@
     far_a = shifted(fwd[:, :half], "y", 1)
     far_b = shifted(bwd[:, half:], "y", -1)
     far = jnp.concatenate([far_a, far_b], axis=1)
-    return team_sum(part) + team_sum(term(far, me + 2))
+    early, far = lax.optimization_barrier((team_sum(part), far))
+    return early + team_sum(term(far, me + 2))
 
 
 def solution(mesh):

time: 82.9 us -> 88.7 us (1.070)
  local copies, waits for them, and re-layouts: 16.7 us -> 28.1 us
  waiting for transfers between devices: 22.9 us -> 16.9 us
    all_to_all x1, waiting for transfers between devices: 17.3 us -> 0.01 us  [per_device(): s2 = lax.all_to_all(copies, ('xl', 'z'), 0, 0)]
    ppermute x8, waiting for transfers between devices: 3.84 us -> 15.1 us  [shifted(): return lax.ppermute(x, axis, [(i, (i + by) % n) for i in range(n)])]
    dynamic_slice x1 -> x2, local copies, waits for them, and re-layouts: 11.6 us -> 16.7 us  [term(): lax.dynamic_slice_in_dim(cov_local, y_from % ny * per_y, per_y, 1)]
    unnamed x4 -> x8, local copies, waits for them, and re-layouts: 2.28 us -> 4.47 us
    reshape x1, local copies, waits for them, and re-layouts: 0.3 us -> 2.36 us  [per_device(): jnp.transpose(s2, (0, 1, 3, 2, 4))]
    transpose x1, local copies, waits for them, and re-layouts: 0.61 us -> 2.63 us  [per_device(): jnp.transpose(s2, (0, 1, 3, 2, 4))]
  transfers between devices with their start and end apart: 10 -> 10, of which waited for: 4 -> 6; matrix products, arithmetic and copies ran while one was open for 22% -> 28% of each run, Pallas kernels for 0% -> 0%
where the time goes in v10:
time: 88.7 us; the launch traced here: 88.1 us
  starting transfers between devices  37.1 us (42%)
  local copies, waits for them, and re-layouts  28.1 us (32%)
  waiting for transfers between devices  16.9 us (19%)
  matrix products  4.25 us (5%)
  other arithmetic  1.55 us (2%)
    ppermute x8, starting transfers between devices, shifted(): return lax.ppermute(x, axis, [(i, (i + by) % n) for i in range(n)])  21.5 us
    dynamic_slice x2, local copies, waits for them, and re-layouts, term(): lax.dynamic_slice_in_dim(cov_local, y_from % ny * per_y, per_y, 1)  16.7 us
    ppermute x8, waiting for transfers between devices, shifted(): return lax.ppermute(x, axis, [(i, (i + by) % n) for i in range(n)])  15.1 us
    all_to_all x1, starting transfers between devices, per_device(): s2 = lax.all_to_all(copies, ('xl', 'z'), 0, 0)  10.7 us
    ppermute x1, starting transfers between devices, per_device(): moved = lax.ppermute(scaled, ('z', 'xh', 'core'), pairs)  4.94 us
    unnamed x8, local copies, waits for them, and re-layouts  4.47 us
    dot_general x4, matrix products, term(): lax.dot_general(block, cov_part, (((0, 2), (1, 2)), ((), ())), preferred_...  4.25 us
    transpose x1, local copies, waits for them, and re-layouts, per_device(): jnp.transpose(s2, (0, 1, 3, 2, 4))  2.63 us
  transfers between devices with their start and end apart: 10, of which 6 were waited for; matrix products, arithmetic and copies ran while one was open for 28% of the time, Pallas kernels for 0%

profile of v10, /device:TPU:1, one launch (start us, length us, event | category | flops | bytes accessed | tf_op | source)
XLA Modules:
  0.0 88.1 jit_solution(7802990402748301537)
XLA Ops:
  1.7 4.9 %collective-permute-start = (bf16[64,384]{1,0:T(8,128)(2,1)S(1)}, bf16[64,384]{1,0:T(8,128)(2,1)S(1)}, u32[]{:S(2)}, u32[]{:S(2)}) collective-permute-start(bf16[64,384]{1,0:T(8,128)(2,1)S(1)} %fusion.2), channel_id=1, source_target_pairs={{0,0},{1,4},{2,8},{3,12},{4,1},{5,5},{6,9},{7,13},{8,2},{9,6},{10,... | collective-permute-start | bytes 147464 | tf_op jit(solution)/shard_map/ppermute | solution.py:54
  6.7 1.8 %collective-permute-done = bf16[64,384]{1,0:T(8,128)(2,1)S(1)} collective-permute-done((bf16[64,384]{1,0:T(8,128)(2,1)S(1)}, bf16[64,384]{1,0:T(8,128)(2,1)S(1)}, u32[]{:S(2)}, u32[]{:S(2)}) %collective-permute-start) | collective-permute-done | bytes 49184 | tf_op jit(solution)/shard_map/ppermute | solution.py:54
  8.4 1.0 %broadcast_in_dim.2 = bf16[16,64,384]{2,1,0:T(8,128)(2,1)} broadcast(bf16[64,384]{1,0:T(8,128)(2,1)S(1)} %collective-permute-done), dimensions={1,2} | broadcast | bytes 835584 | tf_op jit(solution)/shard_map/broadcast_in_dim | solution.py:55
  9.4 10.7 %all-to-all-start = ((bf16[16,64,384]{2,1,0:T(8,128)(2,1)}), bf16[16,64,384]{2,1,0:T(8,128)(2,1)}, u32[]{:S(2)}, u32[]{:S(2)}) async-start(bf16[16,64,384]{2,1,0:T(8,128)(2,1)} %broadcast_in_dim.2), calls=%async_computation | async-start | bytes 1572864 | tf_op jit(solution)/shard_map/all_to_all | solution.py:56
  20.2 13.5 %constant_dynamic-slice_fusion = (bf16[256,4,1,1536]{3,1,2,0:T(4,128)(2,1)S(1)}, bf16[256,4,1,1536]{3,1,2,0:T(4,128)(2,1)S(1)}, bf16[256,4,1,1536]{3,1,2,0:T(4,128)(2,1)S(1)}, bf16[256,4,1,1536]{3,1,2,0:T(4,128)(2,1)}) fusion(bf16[256,16,1,1536]{3,1,2,0:T(8,128)(2,1)} %param.5, s32[]{:T(128)S(6)} %select_n.38, s32[]{:T(128)S(6)} %select_n.36, ...), kind=kLoop, calls=%fused_computation.14 | loop fusion | bytes 25165840 | tf_op jit(solution)/shard_map/dynamic_slice | solution.py:65
  33.7 2.2 %copy.27 = bf16[256,4,1,1536]{3,0,2,1:T(8,128)(2,1)} copy(bf16[256,4,1,1536]{3,1,2,0:T(4,128)(2,1)S(1)} %get-tuple-element.27) | data formatting | bytes 6291456
  36.0 2.2 %copy.26 = bf16[256,4,1,1536]{3,0,2,1:T(8,128)(2,1)} copy(bf16[256,4,1,1536]{3,1,2,0:T(4,128)(2,1)S(1)} %get-tuple-element.26) | data formatting | bytes 6291456
  38.2 2.6 %copy.11 = bf16[2,2,64,4,384]{4,3,2,1,0:T(4,128)(2,1)} copy(bf16[2,2,64,4,384]{4,2,3,1,0:T(8,128)(2,1)} %bitcast.1) | data formatting | bytes 1572864 | tf_op jit(solution)/shard_map/transpose | solution.py:58
  40.8 2.4 %reshape.16 = bf16[4,64,1536]{2,1,0:T(8,128)(2,1)} reshape(bf16[2,2,64,4,384]{4,3,2,1,0:T(4,128)(2,1)} %copy.11) | data formatting | bytes 1572864 | tf_op jit(solution)/shard_map/reshape | solution.py:58
  43.2 1.3 %collective-permute-start.1 = (bf16[4,64,1536]{2,1,0:T(8,128)(2,1)}, bf16[4,64,1536]{2,1,0:T(8,128)(2,1)S(1)}, u32[]{:S(2)}, u32[]{:S(2)}) collective-permute-start(bf16[4,64,1536]{2,1,0:T(8,128)(2,1)} %reshape.16), channel_id=1, source_target_pairs={{0,64},{64,128},{128,192},{192,0},{1,65},{65,129},{129,193},{193,1... | collective-permute-start | bytes 2359304 | tf_op jit(solution)/shard_map/ppermute | solution.py:15
  44.5 1.4 %collective-permute-start.2 = (bf16[4,64,1536]{2,1,0:T(8,128)(2,1)}, bf16[4,64,1536]{2,1,0:T(8,128)(2,1)S(1)}, u32[]{:S(2)}, u32[]{:S(2)}) collective-permute-start(bf16[4,64,1536]{2,1,0:T(8,128)(2,1)} %reshape.16), channel_id=1, source_target_pairs={{0,192},{64,0},{128,64},{192,128},{1,193},{65,1},{129,65},{193,129... | collective-permute-start | bytes 2359304 | tf_op jit(solution)/shard_map/ppermute | solution.py:15
  45.9 3.2 %copy_bitcast_fusion = (bf16[256,4,1536]{2,0,1:T(8,128)(2,1)S(1)}, bf16[256,4,1536]{2,0,1:T(8,128)(2,1)S(1)}) fusion(bf16[256,4,1,1536]{3,1,2,0:T(4,128)(2,1)S(1)} %get-tuple-element.25, bf16[256,4,1,1536]{3,1,2,0:T(4,128)(2,1)} %get-tuple-element.28), kind=kLoop, calls=%fused_computation | loop fusion | bytes 12582912 | tf_op jit(solution)/shard_map/dynamic_slice | solution.py:65
  49.2 1.1 %convolution_bitcast_fusion.3 = f32[64,256]{1,0:T(8,128)S(1)} fusion(bf16[4,64,1536]{2,1,0:T(8,128)(2,1)S(1)} %copy-done.2, bf16[256,4,1536]{2,0,1:T(8,128)(2,1)S(1)} %get-tuple-element.16), kind=kOutput, calls=%fused_computation.9 | convolution fusion | flops 201326592 | bytes 3997696 | tf_op jit(solution)/shard_map/dot_general | solution.py:67
  50.2 9.5 %collective-permute-done.1 = bf16[4,64,1536]{2,1,0:T(8,128)(2,1)S(1)} collective-permute-done((bf16[4,64,1536]{2,1,0:T(8,128)(2,1)}, bf16[4,64,1536]{2,1,0:T(8,128)(2,1)S(1)}, u32[]{:S(2)}, u32[]{:S(2)}) %collective-permute-start.1) | collective-permute-done | bytes 786464 | tf_op jit(solution)/shard_map/ppermute | solution.py:15
  60.6 2.0 %collective-permute-start.6 = (bf16[4,32,1536]{2,1,0:T(8,128)(2,1)S(1)}, bf16[4,32,1536]{2,1,0:T(8,128)(2,1)S(1)}, u32[]{:S(2)}, u32[]{:S(2)}) collective-permute-start(bf16[4,32,1536]{2,1,0:T(8,128)(2,1)S(1)} %slice.9), channel_id=1, source_target_pairs={{0,192},{64,0},{128,64},{192,128},{1,193},{65,1},{129,65},{193,129... | collective-permute-start | bytes 1179656 | tf_op jit(solution)/shard_map/ppermute | solution.py:15
  62.6 1.1 %fusion.1 = f32[64,256]{1,0:T(8,128)S(1)} fusion(f32[64,256]{1,0:T(8,128)S(1)} %convolution_bitcast_fusion.3, bf16[4,64,1536]{2,1,0:T(8,128)(2,1)S(1)} %collective-permute-done.1, bf16[256,4,1536]{2,0,1:T(8,128)(2,1)S(1)} %bitcast.39), kind=kOutput, calls=%fused_computation.8 | convolution fusion | flops 201342976 | bytes 4063232 | tf_op jit(solution)/shard_map/dot_general | solution.py:67
  63.7 1.1 %fusion = f32[64,256]{1,0:T(8,128)S(1)} fusion(f32[64,256]{1,0:T(8,128)S(1)} %fusion.1, bf16[4,64,1536]{2,1,0:T(8,128)(2,1)S(1)} %collective-permute-done.2, bf16[256,4,1536]{2,0,1:T(8,128)(2,1)S(1)} %bitcast.38), kind=kOutput, calls=%fused_computation.6 | convolution fusion | flops 201342976 | bytes 4063232 | tf_op jit(solution)/shard_map/dot_general | solution.py:67
  64.8 6.4 %collective-permute-start.3 = (f32[64,256]{1,0:T(8,128)S(1)}, f32[64,256]{1,0:T(8,128)S(1)}, u32[]{:S(2)}, u32[]{:S(2)}) collective-permute-start(f32[64,256]{1,0:T(8,128)S(1)} %fusion), channel_id=1, source_target_pairs={{0,1},{1,0},{2,3},{3,2},{4,5},{5,4},{6,7},{7,6},{8,9},{9,8},{10,11... | collective-permute-start | bytes 196616 | tf_op jit(solution)/shard_map/ppermute | solution.py:15
  72.1 5.4 %collective-permute-start.4 = (f32[64,256]{1,0:T(8,128)S(1)}, f32[64,256]{1,0:T(8,128)S(1)}, u32[]{:S(2)}, u32[]{:S(2)}) collective-permute-start(f32[64,256]{1,0:T(8,128)S(1)} %add.62), channel_id=1, source_target_pairs={{0,2},{2,0},{1,3},{3,1},{4,6},{6,4},{5,7},{7,5},{8,10},{10,8},{9,1... | collective-permute-start | bytes 196616 | tf_op jit(solution)/shard_map/ppermute | solution.py:15
  77.5 2.2 %collective-permute-done.4 = f32[64,256]{1,0:T(8,128)S(1)} collective-permute-done((f32[64,256]{1,0:T(8,128)S(1)}, f32[64,256]{1,0:T(8,128)S(1)}, u32[]{:S(2)}, u32[]{:S(2)}) %collective-permute-start.4) | collective-permute-done | bytes 65568 | tf_op jit(solution)/shard_map/ppermute | solution.py:15
  79.7 1.1 %convolution_bitcast_fusion = f32[64,256]{1,0:T(8,128)S(1)} fusion(bf16[4,64,1536]{2,1,0:T(8,128)(2,1)S(1)} %pad_maximum_fusion, bf16[256,4,1536]{2,0,1:T(8,128)(2,1)S(1)} %get-tuple-element.24), kind=kOutput, calls=%fused_computation.4 | convolution fusion | flops 201326592 | bytes 3997696 | tf_op jit(solution)/shard_map/dot_general | solution.py:67
  80.8 1.0 %collective-permute-start.7 = (f32[64,256]{1,0:T(8,128)S(1)}, f32[64,256]{1,0:T(8,128)S(1)}, u32[]{:S(2)}, u32[]{:S(2)}) collective-permute-start(f32[64,256]{1,0:T(8,128)S(1)} %convolution_bitcast_fusion), channel_id=1, source_target_pairs={{0,1},{1,0},{2,3},{3,2},{4,5},{5,4},{6,7},{7,6},{8,9},{9,8},{10,11... | collective-permute-start | bytes 196616 | tf_op jit(solution)/shard_map/ppermute | solution.py:15
  82.7 3.2 %collective-permute-start.8 = (f32[64,256]{1,0:T(8,128)S(1)}, f32[64,256]{1,0:T(8,128)S(1)}, u32[]{:S(2)}, u32[]{:S(2)}) collective-permute-start(f32[64,256]{1,0:T(8,128)S(1)} %add.67), channel_id=1, source_target_pairs={{0,2},{2,0},{1,3},{3,1},{4,6},{6,4},{5,7},{7,5},{8,10},{10,8},{9,1... | collective-permute-start | bytes 196616 | tf_op jit(solution)/shard_map/ppermute | solution.py:15
  85.8 1.7 %collective-permute-done.8 = f32[64,256]{1,0:T(8,128)S(1)} collective-permute-done((f32[64,256]{1,0:T(8,128)S(1)}, f32[64,256]{1,0:T(8,128)S(1)}, u32[]{:S(2)}, u32[]{:S(2)}) %collective-permute-start.8) | collective-permute-done | bytes 65568 | tf_op jit(solution)/shard_map/ppermute | solution.py:15
  (23 shorter events, 5.1 us)
Async XLA Ops:
  1.7 6.7 %collective-permute-start = (bf16[64,384]{1,0:T(8,128)(2,1)S(1)}, bf16[64,384]{1,0:T(8,128)(2,1)S(1)}, u32[]{:S(2)}, u32[]{:S(2)}) collective-permute-start(bf16[64,384]{1,0:T(8,128)(2,1)S(1)} %fusion.2), channel_id=1, source_target_pairs={{0,0},{1,4},{2,8},{3,12},{4,1},{5,5},{6,9},{7,13},{8,2},{9,6},{10,... | collective-permute-start | bytes 147464 | tf_op jit(solution)/shard_map/ppermute | solution.py:54
  9.4 28.8 %all-to-all-start = ((bf16[16,64,384]{2,1,0:T(8,128)(2,1)}), bf16[16,64,384]{2,1,0:T(8,128)(2,1)}, u32[]{:S(2)}, u32[]{:S(2)}) async-start(bf16[16,64,384]{2,1,0:T(8,128)(2,1)} %broadcast_in_dim.2), calls=%async_computation | async-start | bytes 1572864 | tf_op jit(solution)/shard_map/all_to_all | solution.py:56
  43.2 16.5 %collective-permute-start.1 = (bf16[4,64,1536]{2,1,0:T(8,128)(2,1)}, bf16[4,64,1536]{2,1,0:T(8,128)(2,1)S(1)}, u32[]{:S(2)}, u32[]{:S(2)}) collective-permute-start(bf16[4,64,1536]{2,1,0:T(8,128)(2,1)} %reshape.16), channel_id=1, source_target_pairs={{0,64},{64,128},{128,192},{192,0},{1,65},{65,129},{129,193},{193,1... | collective-permute-start | bytes 2359304 | tf_op jit(solution)/shard_map/ppermute | solution.py:15
  44.5 15.2 %collective-permute-start.2 = (bf16[4,64,1536]{2,1,0:T(8,128)(2,1)}, bf16[4,64,1536]{2,1,0:T(8,128)(2,1)S(1)}, u32[]{:S(2)}, u32[]{:S(2)}) collective-permute-start(bf16[4,64,1536]{2,1,0:T(8,128)(2,1)} %reshape.16), channel_id=1, source_target_pairs={{0,192},{64,0},{128,64},{192,128},{1,193},{65,1},{129,65},{193,129... | collective-permute-start | bytes 2359304 | tf_op jit(solution)/shard_map/ppermute | solution.py:15
  45.9 3.2 %copy-start.2 = (bf16[4,64,1536]{2,1,0:T(8,128)(2,1)S(1)}, bf16[4,64,1536]{2,1,0:T(8,128)(2,1)}, u32[]{:S(2)}) copy-start(bf16[4,64,1536]{2,1,0:T(8,128)(2,1)} %reshape.16) | copy-start | bytes 2359300
  49.1 13.5 %copy-start.1 = (bf16[256,4,1,1536]{3,0,2,1:T(8,128)(2,1)S(1)}, bf16[256,4,1,1536]{3,0,2,1:T(8,128)(2,1)}, u32[]{:S(2)}) copy-start(bf16[256,4,1,1536]{3,0,2,1:T(8,128)(2,1)} %copy.27) | copy-start | bytes 9437188
  50.2 13.5 %copy-start = (bf16[256,4,1,1536]{3,0,2,1:T(8,128)(2,1)S(1)}, bf16[256,4,1,1536]{3,0,2,1:T(8,128)(2,1)}, u32[]{:S(2)}) copy-start(bf16[256,4,1,1536]{3,0,2,1:T(8,128)(2,1)} %copy.26) | copy-start | bytes 9437188
  59.8 19.9 %collective-permute-start.5 = (bf16[4,32,1536]{2,1,0:T(8,128)(2,1)S(1)}, bf16[4,32,1536]{2,1,0:T(8,128)(2,1)S(1)}, u32[]{:S(2)}, u32[]{:S(2)}) collective-permute-start(bf16[4,32,1536]{2,1,0:T(8,128)(2,1)S(1)} %slice.8), channel_id=1, source_target_pairs={{0,64},{64,128},{128,192},{192,0},{1,65},{65,129},{129,193},{193,1... | collective-permute-start | bytes 1179656 | tf_op jit(solution)/shard_map/ppermute | solution.py:15
  60.6 19.1 %collective-permute-start.6 = (bf16[4,32,1536]{2,1,0:T(8,128)(2,1)S(1)}, bf16[4,32,1536]{2,1,0:T(8,128)(2,1)S(1)}, u32[]{:S(2)}, u32[]{:S(2)}) collective-permute-start(bf16[4,32,1536]{2,1,0:T(8,128)(2,1)S(1)} %slice.9), channel_id=1, source_target_pairs={{0,192},{64,0},{128,64},{192,128},{1,193},{65,1},{129,65},{193,129... | collective-permute-start | bytes 1179656 | tf_op jit(solution)/shard_map/ppermute | solution.py:15
  64.8 7.3 %collective-permute-start.3 = (f32[64,256]{1,0:T(8,128)S(1)}, f32[64,256]{1,0:T(8,128)S(1)}, u32[]{:S(2)}, u32[]{:S(2)}) collective-permute-start(f32[64,256]{1,0:T(8,128)S(1)} %fusion), channel_id=1, source_target_pairs={{0,1},{1,0},{2,3},{3,2},{4,5},{5,4},{6,7},{7,6},{8,9},{9,8},{10,11... | collective-permute-start | bytes 196616 | tf_op jit(solution)/shard_map/ppermute | solution.py:15
  72.1 7.6 %collective-permute-start.4 = (f32[64,256]{1,0:T(8,128)S(1)}, f32[64,256]{1,0:T(8,128)S(1)}, u32[]{:S(2)}, u32[]{:S(2)}) collective-permute-start(f32[64,256]{1,0:T(8,128)S(1)} %add.62), channel_id=1, source_target_pairs={{0,2},{2,0},{1,3},{3,1},{4,6},{6,4},{5,7},{7,5},{8,10},{10,8},{9,1... | collective-permute-start | bytes 196616 | tf_op jit(solution)/shard_map/ppermute | solution.py:15
  80.8 1.9 %collective-permute-start.7 = (f32[64,256]{1,0:T(8,128)S(1)}, f32[64,256]{1,0:T(8,128)S(1)}, u32[]{:S(2)}, u32[]{:S(2)}) collective-permute-start(f32[64,256]{1,0:T(8,128)S(1)} %convolution_bitcast_fusion), channel_id=1, source_target_pairs={{0,1},{1,0},{2,3},{3,2},{4,5},{5,4},{6,7},{7,6},{8,9},{9,8},{10,11... | collective-permute-start | bytes 196616 | tf_op jit(solution)/shard_map/ppermute | solution.py:15
  82.7 4.8 %collective-permute-start.8 = (f32[64,256]{1,0:T(8,128)S(1)}, f32[64,256]{1,0:T(8,128)S(1)}, u32[]{:S(2)}, u32[]{:S(2)}) collective-permute-start(f32[64,256]{1,0:T(8,128)S(1)} %add.67), channel_id=1, source_target_pairs={{0,2},{2,0},{1,3},{3,1},{4,6},{6,4},{5,7},{7,5},{8,10},{10,8},{9,1... | collective-permute-start | bytes 196616 | tf_op jit(solution)/shard_map/ppermute | solution.py:15

commit v11 on v9

--- a/solution.py
+++ b/solution.py
@@ -77,7 +77,10 @@
     far_a = shifted(fwd[:, :half], "y", 1)
     far_b = shifted(bwd[:, half:], "y", -1)
     far = jnp.concatenate([far_a, far_b], axis=1)
-    return team_sum(part) + team_sum(term(far, me + 2))
+    pair = part + shifted(part, "core", 1)
+    far_term = term(far, me + 2)
+    pair = pair + (far_term + shifted(far_term, "core", 1))
+    return pair + shifted(pair, "xh", 1)
 
 
 def solution(mesh):

time: 82.9 us -> 81.2 us (0.979)
  starting transfers between devices: 37 us -> 36.1 us
    ppermute x8 -> x7, starting transfers between devices: 21.3 us -> 20.5 us  [shifted(): return lax.ppermute(x, axis, [(i, (i + by) % n) for i in range(n)])]
    ppermute x8 -> x7, waiting for transfers between devices: 3.84 us -> 3.09 us  [shifted(): return lax.ppermute(x, axis, [(i, (i + by) % n) for i in range(n)])]
  transfers between devices with their start and end apart: 10 -> 9, of which waited for: 4 -> 4; matrix products, arithmetic and copies ran while one was open for 22% -> 23% of each run, Pallas kernels for 0% -> 0%
where the time goes in v11:
time: 81.2 us; the launch traced here: 80.9 us
  starting transfers between devices  36.1 us (44%)
  waiting for transfers between devices  22.2 us (27%)
  local copies, waits for them, and re-layouts  16.7 us (21%)
  matrix products  4.26 us (5%)
  other arithmetic  1.53 us (2%)
    ppermute x7, starting transfers between devices, shifted(): return lax.ppermute(x, axis, [(i, (i + by) % n) for i in range(n)])  20.5 us
    all_to_all x1, waiting for transfers between devices, per_device(): s2 = lax.all_to_all(copies, ('xl', 'z'), 0, 0)  17.3 us
    dynamic_slice x1, local copies, waits for them, and re-layouts, term(): lax.dynamic_slice_in_dim(cov_local, y_from % ny * per_y, per_y, 1)  11.6 us
    all_to_all x1, starting transfers between devices, per_device(): s2 = lax.all_to_all(copies, ('xl', 'z'), 0, 0)  10.7 us
    ppermute x1, starting transfers between devices, per_device(): moved = lax.ppermute(scaled, ('z', 'xh', 'core'), pairs)  4.94 us
    dot_general x4, matrix products, term(): lax.dot_general(block, cov_part, (((0, 2), (1, 2)), ((), ())), preferred_...  4.26 us
    ppermute x7, waiting for transfers between devices, shifted(): return lax.ppermute(x, axis, [(i, (i + by) % n) for i in range(n)])  3.09 us
    unnamed x4, local copies, waits for them, and re-layouts  2.28 us
  transfers between devices with their start and end apart: 9, of which 4 were waited for; matrix products, arithmetic and copies ran while one was open for 23% of the time, Pallas kernels for 0%

profile of v11, /device:TPU:1, one launch (start us, length us, event | category | flops | bytes accessed | tf_op | source)
XLA Modules:
  0.0 80.9 jit_solution(964967772513240394)
XLA Ops:
  0.0 0.8 copy.10
  0.9 0.8 %fusion.2 = bf16[64,384]{1,0:T(8,128)(2,1)S(1)} fusion(f32[8,8,3,128]{3,2,1,0:T(4,128)S(1)} %bitcast.45, bf16[64,384]{1,0:T(8,128)(2,1)} %param.3), kind=kLoop, calls=%fused_computation.12 | loop fusion | flops 73728 | bytes 196608 | tf_op jit(solution)/shard_map/convert_element_type | solution.py:45
  1.7 4.9 %collective-permute-start = (bf16[64,384]{1,0:T(8,128)(2,1)S(1)}, bf16[64,384]{1,0:T(8,128)(2,1)S(1)}, u32[]{:S(2)}, u32[]{:S(2)}) collective-permute-start(bf16[64,384]{1,0:T(8,128)(2,1)S(1)} %fusion.2), channel_id=1, source_target_pairs={{0,0},{1,4},{2,8},{3,12},{4,1},{5,5},{6,9},{7,13},{8,2},{9,6},{10,... | collective-permute-start | bytes 147464 | tf_op jit(solution)/shard_map/ppermute | solution.py:54
  6.7 1.8 %collective-permute-done = bf16[64,384]{1,0:T(8,128)(2,1)S(1)} collective-permute-done((bf16[64,384]{1,0:T(8,128)(2,1)S(1)}, bf16[64,384]{1,0:T(8,128)(2,1)S(1)}, u32[]{:S(2)}, u32[]{:S(2)}) %collective-permute-start) | collective-permute-done | bytes 49184 | tf_op jit(solution)/shard_map/ppermute | solution.py:54
  8.4 1.0 %broadcast_in_dim.2 = bf16[16,64,384]{2,1,0:T(8,128)(2,1)} broadcast(bf16[64,384]{1,0:T(8,128)(2,1)S(1)} %collective-permute-done), dimensions={1,2} | broadcast | bytes 835584 | tf_op jit(solution)/shard_map/broadcast_in_dim | solution.py:55
  9.4 10.7 %all-to-all-start = ((bf16[16,64,384]{2,1,0:T(8,128)(2,1)}), bf16[16,64,384]{2,1,0:T(8,128)(2,1)S(1)}, u32[]{:S(2)}, u32[]{:S(2)}) async-start(bf16[16,64,384]{2,1,0:T(8,128)(2,1)} %broadcast_in_dim.2), calls=%async_computation | async-start | bytes 1572864 | tf_op jit(solution)/shard_map/all_to_all | solution.py:56
  20.2 17.3 %all-to-all-done = bf16[16,64,384]{2,1,0:T(8,128)(2,1)S(1)} async-done(((bf16[16,64,384]{2,1,0:T(8,128)(2,1)}), bf16[16,64,384]{2,1,0:T(8,128)(2,1)S(1)}, u32[]{:S(2)}, u32[]{:S(2)}) %all-to-all-start) | async-done | bytes 786464 | tf_op jit(solution)/shard_map/all_to_all | solution.py:56
  37.5 0.6 copy.11
  38.4 1.4 %collective-permute-start.1 = (bf16[4,64,1536]{2,1,0:T(8,128)(2,1)S(1)}, bf16[4,64,1536]{2,1,0:T(8,128)(2,1)S(1)}, u32[]{:S(2)}, u32[]{:S(2)}) collective-permute-start(bf16[4,64,1536]{2,1,0:T(8,128)(2,1)S(1)} %reshape.16), channel_id=1, source_target_pairs={{0,64},{64,128},{128,192},{192,0},{1,65},{65,129},{129,193},{193,1... | collective-permute-start | bytes 2359304 | tf_op jit(solution)/shard_map/ppermute | solution.py:15
  39.8 1.5 %collective-permute-start.2 = (bf16[4,64,1536]{2,1,0:T(8,128)(2,1)S(1)}, bf16[4,64,1536]{2,1,0:T(8,128)(2,1)S(1)}, u32[]{:S(2)}, u32[]{:S(2)}) collective-permute-start(bf16[4,64,1536]{2,1,0:T(8,128)(2,1)S(1)} %reshape.16), channel_id=1, source_target_pairs={{0,192},{64,0},{128,64},{192,128},{1,193},{65,1},{129,65},{193,129... | collective-permute-start | bytes 2359304 | tf_op jit(solution)/shard_map/ppermute | solution.py:15
  41.3 11.6 %constant_dynamic-slice_fusion.1 = (bf16[256,4,1,1536]{3,1,2,0:T(4,128)(2,1)S(1)}, bf16[256,4,1,1536]{3,1,2,0:T(4,128)(2,1)S(1)}, bf16[256,4,1,1536]{3,1,2,0:T(4,128)(2,1)S(1)}, bf16[256,4,1,1536]{3,1,2,0:T(4,128)(2,1)S(1)}) fusion(bf16[256,16,1,1536]{3,1,2,0:T(8,128)(2,1)} %param.5, s32[]{:T(128)S(6)} %select_n.36, s32[]{:T(128)S(6)} %select_n.34, ...), kind=kLoop, calls=%fused_computation.15 | loop fusion | bytes 25165840 | tf_op jit(solution)/shard_map/dynamic_slice | solution.py:65
  52.9 0.6 copy.29
  53.5 0.6 copy.28
  55.2 1.1 %convolution_bitcast_fusion.3 = f32[64,256]{1,0:T(8,128)S(1)} fusion(bf16[4,64,1536]{2,1,0:T(8,128)(2,1)S(1)} %reshape.16, bf16[256,4,1536]{2,0,1:T(8,128)(2,1)S(1)} %bitcast.41), kind=kOutput, calls=%fused_computation.9 | convolution fusion | flops 201326592 | bytes 3997696 | tf_op jit(solution)/shard_map/dot_general | solution.py:67
  56.5 2.7 %collective-permute-start.5 = (bf16[4,32,1536]{2,1,0:T(8,128)(2,1)S(1)}, bf16[4,32,1536]{2,1,0:T(8,128)(2,1)S(1)}, u32[]{:S(2)}, u32[]{:S(2)}) collective-permute-start(bf16[4,32,1536]{2,1,0:T(8,128)(2,1)S(1)} %slice.9), channel_id=1, source_target_pairs={{0,192},{64,0},{128,64},{192,128},{1,193},{65,1},{129,65},{193,129... | collective-permute-start | bytes 1179656 | tf_op jit(solution)/shard_map/ppermute | solution.py:15
  59.2 1.1 %fusion.1 = f32[64,256]{1,0:T(8,128)S(1)} fusion(f32[64,256]{1,0:T(8,128)S(1)} %convolution_bitcast_fusion.3, bf16[4,64,1536]{2,1,0:T(8,128)(2,1)S(1)} %collective-permute-done.1, bf16[256,4,1536]{2,0,1:T(8,128)(2,1)S(1)} %bitcast.43), kind=kOutput, calls=%fused_computation.8 | convolution fusion | flops 201342976 | bytes 4063232 | tf_op jit(solution)/shard_map/dot_general | solution.py:67
  60.2 1.1 %fusion = f32[64,256]{1,0:T(8,128)S(1)} fusion(f32[64,256]{1,0:T(8,128)S(1)} %fusion.1, bf16[4,64,1536]{2,1,0:T(8,128)(2,1)S(1)} %collective-permute-done.2, bf16[256,4,1536]{2,0,1:T(8,128)(2,1)S(1)} %bitcast.42), kind=kOutput, calls=%fused_computation.6 | convolution fusion | flops 201342976 | bytes 4063232 | tf_op jit(solution)/shard_map/dot_general | solution.py:67
  61.3 5.7 %collective-permute-start.3 = (f32[64,256]{1,0:T(8,128)S(1)}, f32[64,256]{1,0:T(8,128)S(1)}, u32[]{:S(2)}, u32[]{:S(2)}) collective-permute-start(f32[64,256]{1,0:T(8,128)S(1)} %fusion), channel_id=1, source_target_pairs={{0,1},{1,0},{2,3},{3,2},{4,5},{5,4},{6,7},{7,6},{8,9},{9,8},{10,11... | collective-permute-start | bytes 196616 | tf_op jit(solution)/shard_map/ppermute | solution.py:15
  67.1 1.1 %convolution_bitcast_fusion = f32[64,256]{1,0:T(8,128)S(1)} fusion(bf16[4,64,1536]{2,1,0:T(8,128)(2,1)S(1)} %pad_maximum_fusion, bf16[256,4,1536]{2,0,1:T(8,128)(2,1)S(1)} %bitcast.40), kind=kOutput, calls=%fused_computation.4 | convolution fusion | flops 201326592 | bytes 3997696 | tf_op jit(solution)/shard_map/dot_general | solution.py:67
  68.2 3.5 %collective-permute-start.6 = (f32[64,256]{1,0:T(8,128)S(1)}, f32[64,256]{1,0:T(8,128)S(1)}, u32[]{:S(2)}, u32[]{:S(2)}) collective-permute-start(f32[64,256]{1,0:T(8,128)S(1)} %convolution_bitcast_fusion), channel_id=1, source_target_pairs={{0,1},{1,0},{2,3},{3,2},{4,5},{5,4},{6,7},{7,6},{8,9},{9,8},{10,11... | collective-permute-start | bytes 196616 | tf_op jit(solution)/shard_map/ppermute | solution.py:15
  71.7 0.9 %collective-permute-done.6 = f32[64,256]{1,0:T(8,128)S(1)} collective-permute-done((f32[64,256]{1,0:T(8,128)S(1)}, f32[64,256]{1,0:T(8,128)S(1)}, u32[]{:S(2)}, u32[]{:S(2)}) %collective-permute-start.6) | collective-permute-done | bytes 65568 | tf_op jit(solution)/shard_map/ppermute | solution.py:15
  72.6 5.5 %collective-permute-start.7 = (f32[64,256]{1,0:T(8,128)S(1)}, f32[64,256]{1,0:T(8,128)S(1)}, u32[]{:S(2)}, u32[]{:S(2)}) collective-permute-start(f32[64,256]{1,0:T(8,128)S(1)} %add_add_fusion), channel_id=1, source_target_pairs={{0,2},{2,0},{1,3},{3,1},{4,6},{6,4},{5,7},{7,5},{8,10},{10,8},{9,1... | collective-permute-start | bytes 196616 | tf_op jit(solution)/shard_map/ppermute | solution.py:15
  78.1 2.2 %collective-permute-done.7 = f32[64,256]{1,0:T(8,128)S(1)} collective-permute-done((f32[64,256]{1,0:T(8,128)S(1)}, f32[64,256]{1,0:T(8,128)S(1)}, u32[]{:S(2)}, u32[]{:S(2)}) %collective-permute-start.7) | collective-permute-done | bytes 65568 | tf_op jit(solution)/shard_map/ppermute | solution.py:15
  80.3 0.6 add.65
  (14 shorter events, 1.8 us)
Async XLA Ops:
  1.7 6.7 %collective-permute-start = (bf16[64,384]{1,0:T(8,128)(2,1)S(1)}, bf16[64,384]{1,0:T(8,128)(2,1)S(1)}, u32[]{:S(2)}, u32[]{:S(2)}) collective-permute-start(bf16[64,384]{1,0:T(8,128)(2,1)S(1)} %fusion.2), channel_id=1, source_target_pairs={{0,0},{1,4},{2,8},{3,12},{4,1},{5,5},{6,9},{7,13},{8,2},{9,6},{10,... | collective-permute-start | bytes 147464 | tf_op jit(solution)/shard_map/ppermute | solution.py:54
  9.4 28.1 %all-to-all-start = ((bf16[16,64,384]{2,1,0:T(8,128)(2,1)}), bf16[16,64,384]{2,1,0:T(8,128)(2,1)S(1)}, u32[]{:S(2)}, u32[]{:S(2)}) async-start(bf16[16,64,384]{2,1,0:T(8,128)(2,1)} %broadcast_in_dim.2), calls=%async_computation | async-start | bytes 1572864 | tf_op jit(solution)/shard_map/all_to_all | solution.py:56
  38.4 17.9 %collective-permute-start.1 = (bf16[4,64,1536]{2,1,0:T(8,128)(2,1)S(1)}, bf16[4,64,1536]{2,1,0:T(8,128)(2,1)S(1)}, u32[]{:S(2)}, u32[]{:S(2)}) collective-permute-start(bf16[4,64,1536]{2,1,0:T(8,128)(2,1)S(1)} %reshape.16), channel_id=1, source_target_pairs={{0,64},{64,128},{128,192},{192,0},{1,65},{65,129},{129,193},{193,1... | collective-permute-start | bytes 2359304 | tf_op jit(solution)/shard_map/ppermute | solution.py:15
  39.8 16.6 %collective-permute-start.2 = (bf16[4,64,1536]{2,1,0:T(8,128)(2,1)S(1)}, bf16[4,64,1536]{2,1,0:T(8,128)(2,1)S(1)}, u32[]{:S(2)}, u32[]{:S(2)}) collective-permute-start(bf16[4,64,1536]{2,1,0:T(8,128)(2,1)S(1)} %reshape.16), channel_id=1, source_target_pairs={{0,192},{64,0},{128,64},{192,128},{1,193},{65,1},{129,65},{193,129... | collective-permute-start | bytes 2359304 | tf_op jit(solution)/shard_map/ppermute | solution.py:15
  56.3 10.7 %collective-permute-start.4 = (bf16[4,32,1536]{2,1,0:T(8,128)(2,1)S(1)}, bf16[4,32,1536]{2,1,0:T(8,128)(2,1)S(1)}, u32[]{:S(2)}, u32[]{:S(2)}) collective-permute-start(bf16[4,32,1536]{2,1,0:T(8,128)(2,1)S(1)} %slice.8), channel_id=1, source_target_pairs={{0,64},{64,128},{128,192},{192,0},{1,65},{65,129},{129,193},{193,1... | collective-permute-start | bytes 1179656 | tf_op jit(solution)/shard_map/ppermute | solution.py:15
  56.5 10.6 %collective-permute-start.5 = (bf16[4,32,1536]{2,1,0:T(8,128)(2,1)S(1)}, bf16[4,32,1536]{2,1,0:T(8,128)(2,1)S(1)}, u32[]{:S(2)}, u32[]{:S(2)}) collective-permute-start(bf16[4,32,1536]{2,1,0:T(8,128)(2,1)S(1)} %slice.9), channel_id=1, source_target_pairs={{0,192},{64,0},{128,64},{192,128},{1,193},{65,1},{129,65},{193,129... | collective-permute-start | bytes 1179656 | tf_op jit(solution)/shard_map/ppermute | solution.py:15
  61.3 10.4 %collective-permute-start.3 = (f32[64,256]{1,0:T(8,128)S(1)}, f32[64,256]{1,0:T(8,128)S(1)}, u32[]{:S(2)}, u32[]{:S(2)}) collective-permute-start(f32[64,256]{1,0:T(8,128)S(1)} %fusion), channel_id=1, source_target_pairs={{0,1},{1,0},{2,3},{3,2},{4,5},{5,4},{6,7},{7,6},{8,9},{9,8},{10,11... | collective-permute-start | bytes 196616 | tf_op jit(solution)/shard_map/ppermute | solution.py:15
  68.2 4.4 %collective-permute-start.6 = (f32[64,256]{1,0:T(8,128)S(1)}, f32[64,256]{1,0:T(8,128)S(1)}, u32[]{:S(2)}, u32[]{:S(2)}) collective-permute-start(f32[64,256]{1,0:T(8,128)S(1)} %convolution_bitcast_fusion), channel_id=1, source_target_pairs={{0,1},{1,0},{2,3},{3,2},{4,5},{5,4},{6,7},{7,6},{8,9},{9,8},{10,11... | collective-permute-start | bytes 196616 | tf_op jit(solution)/shard_map/ppermute | solution.py:15
  72.6 7.7 %collective-permute-start.7 = (f32[64,256]{1,0:T(8,128)S(1)}, f32[64,256]{1,0:T(8,128)S(1)}, u32[]{:S(2)}, u32[]{:S(2)}) collective-permute-start(f32[64,256]{1,0:T(8,128)S(1)} %add_add_fusion), channel_id=1, source_target_pairs={{0,2},{2,0},{1,3},{3,1},{4,6},{6,4},{5,7},{7,5},{8,10},{10,8},{9,1... | collective-permute-start | bytes 196616 | tf_op jit(solution)/shard_map/ppermute | solution.py:15

commit v12 on v11

--- a/solution.py
+++ b/solution.py
@@ -79,8 +79,12 @@
     far = jnp.concatenate([far_a, far_b], axis=1)
     pair = part + shifted(part, "core", 1)
     far_term = term(far, me + 2)
-    pair = pair + (far_term + shifted(far_term, "core", 1))
-    return pair + shifted(pair, "xh", 1)
+    f_core = shifted(far_term, "core", 1)
+    f_diag = lax.ppermute(far_term, ("xh", "core"), [(0, 3), (3, 0), (1, 2), (2, 1)])
+    other = shifted(jnp.stack([pair, far_term]), "xh", 1)
+    mine = pair + (far_term + f_core)
+    theirs = other[0] + (other[1] + f_diag)
+    return mine + theirs
 
 
 def solution(mesh):

time: 81.2 us -> 83.7 us (1.031)
  waiting for transfers between devices: 22.2 us -> 24.7 us
    ppermute x0 -> x1, waiting for transfers between devices: none -> 4.31 us  [per_device(): lax.ppermute(far_term, ('xh', 'core'), [(0, 3), (3, 0), (1, 2), (2, 1)])]
    ppermute x7, waiting for transfers between devices: 3.09 us -> 1.24 us  [shifted(): return lax.ppermute(x, axis, [(i, (i + by) % n) for i in range(n)])]
  transfers between devices with their start and end apart: 9 -> 10, of which waited for: 4 -> 5; matrix products, arithmetic and copies ran while one was open for 23% -> 20% of each run, Pallas kernels for 0% -> 0%
where the time goes in v12:
time: 83.7 us; the launch traced here: 83.4 us
  starting transfers between devices  36.1 us (43%)
  waiting for transfers between devices  24.7 us (30%)
  local copies, waits for them, and re-layouts  16.7 us (20%)
  matrix products  4.26 us (5%)
  other arithmetic  1.55 us (2%)
    ppermute x7, starting transfers between devices, shifted(): return lax.ppermute(x, axis, [(i, (i + by) % n) for i in range(n)])  20.5 us
    all_to_all x1, waiting for transfers between devices, per_device(): s2 = lax.all_to_all(copies, ('xl', 'z'), 0, 0)  17.3 us
    dynamic_slice x1, local copies, waits for them, and re-layouts, term(): lax.dynamic_slice_in_dim(cov_local, y_from % ny * per_y, per_y, 1)  11.6 us
    all_to_all x1, starting transfers between devices, per_device(): s2 = lax.all_to_all(copies, ('xl', 'z'), 0, 0)  10.7 us
    ppermute x1, starting transfers between devices, per_device(): moved = lax.ppermute(scaled, ('z', 'xh', 'core'), pairs)  4.94 us
    ppermute x1, waiting for transfers between devices, per_device(): lax.ppermute(far_term, ('xh', 'core'), [(0, 3), (3, 0), (1, 2), (2, 1)])  4.31 us
    dot_general x4, matrix products, term(): lax.dot_general(block, cov_part, (((0, 2), (1, 2)), ((), ())), preferred_...  4.26 us
    unnamed x4, local copies, waits for them, and re-layouts  2.28 us
  transfers between devices with their start and end apart: 10, of which 5 were waited for; matrix products, arithmetic and copies ran while one was open for 20% of the time, Pallas kernels for 0%

profile of v12, /device:TPU:1, one launch (start us, length us, event | category | flops | bytes accessed | tf_op | source)
XLA Modules:
  0.0 83.4 jit_solution(7841448570617471724)
XLA Ops:
  0.0 0.8 copy.10
  0.9 0.8 fusion.2
  1.7 4.9 %collective-permute-start = (bf16[64,384]{1,0:T(8,128)(2,1)S(1)}, bf16[64,384]{1,0:T(8,128)(2,1)S(1)}, u32[]{:S(2)}, u32[]{:S(2)}) collective-permute-start(bf16[64,384]{1,0:T(8,128)(2,1)S(1)} %fusion.2), channel_id=1, source_target_pairs={{0,0},{1,4},{2,8},{3,12},{4,1},{5,5},{6,9},{7,13},{8,2},{9,6},{10,... | collective-permute-start | bytes 147464 | tf_op jit(solution)/shard_map/ppermute | solution.py:54
  6.7 1.8 %collective-permute-done = bf16[64,384]{1,0:T(8,128)(2,1)S(1)} collective-permute-done((bf16[64,384]{1,0:T(8,128)(2,1)S(1)}, bf16[64,384]{1,0:T(8,128)(2,1)S(1)}, u32[]{:S(2)}, u32[]{:S(2)}) %collective-permute-start) | collective-permute-done | bytes 49184 | tf_op jit(solution)/shard_map/ppermute | solution.py:54
  8.4 1.0 %broadcast_in_dim.2 = bf16[16,64,384]{2,1,0:T(8,128)(2,1)} broadcast(bf16[64,384]{1,0:T(8,128)(2,1)S(1)} %collective-permute-done), dimensions={1,2} | broadcast | bytes 835584 | tf_op jit(solution)/shard_map/broadcast_in_dim | solution.py:55
  9.4 10.7 %all-to-all-start = ((bf16[16,64,384]{2,1,0:T(8,128)(2,1)}), bf16[16,64,384]{2,1,0:T(8,128)(2,1)S(1)}, u32[]{:S(2)}, u32[]{:S(2)}) async-start(bf16[16,64,384]{2,1,0:T(8,128)(2,1)} %broadcast_in_dim.2), calls=%async_computation | async-start | bytes 1572864 | tf_op jit(solution)/shard_map/all_to_all | solution.py:56
  20.2 17.3 %all-to-all-done = bf16[16,64,384]{2,1,0:T(8,128)(2,1)S(1)} async-done(((bf16[16,64,384]{2,1,0:T(8,128)(2,1)}), bf16[16,64,384]{2,1,0:T(8,128)(2,1)S(1)}, u32[]{:S(2)}, u32[]{:S(2)}) %all-to-all-start) | async-done | bytes 786464 | tf_op jit(solution)/shard_map/all_to_all | solution.py:56
  37.5 0.6 copy.11
  38.4 1.4 %collective-permute-start.1 = (bf16[4,64,1536]{2,1,0:T(8,128)(2,1)S(1)}, bf16[4,64,1536]{2,1,0:T(8,128)(2,1)S(1)}, u32[]{:S(2)}, u32[]{:S(2)}) collective-permute-start(bf16[4,64,1536]{2,1,0:T(8,128)(2,1)S(1)} %reshape.16), channel_id=1, source_target_pairs={{0,64},{64,128},{128,192},{192,0},{1,65},{65,129},{129,193},{193,1... | collective-permute-start | bytes 2359304 | tf_op jit(solution)/shard_map/ppermute | solution.py:15
  39.8 1.5 %collective-permute-start.2 = (bf16[4,64,1536]{2,1,0:T(8,128)(2,1)S(1)}, bf16[4,64,1536]{2,1,0:T(8,128)(2,1)S(1)}, u32[]{:S(2)}, u32[]{:S(2)}) collective-permute-start(bf16[4,64,1536]{2,1,0:T(8,128)(2,1)S(1)} %reshape.16), channel_id=1, source_target_pairs={{0,192},{64,0},{128,64},{192,128},{1,193},{65,1},{129,65},{193,129... | collective-permute-start | bytes 2359304 | tf_op jit(solution)/shard_map/ppermute | solution.py:15
  41.3 11.6 %constant_dynamic-slice_fusion.1 = (bf16[256,4,1,1536]{3,1,2,0:T(4,128)(2,1)S(1)}, bf16[256,4,1,1536]{3,1,2,0:T(4,128)(2,1)S(1)}, bf16[256,4,1,1536]{3,1,2,0:T(4,128)(2,1)S(1)}, bf16[256,4,1,1536]{3,1,2,0:T(4,128)(2,1)S(1)}) fusion(bf16[256,16,1,1536]{3,1,2,0:T(8,128)(2,1)} %param.5, s32[]{:T(128)S(6)} %select_n.36, s32[]{:T(128)S(6)} %select_n.34, ...), kind=kLoop, calls=%fused_computation.20 | loop fusion | bytes 25165840 | tf_op jit(solution)/shard_map/dynamic_slice | solution.py:65
  52.9 0.6 copy.29
  53.5 0.6 copy.28
  54.6 1.1 %convolution_bitcast_fusion.2 = f32[64,256]{1,0:T(8,128)S(1)} fusion(bf16[4,64,1536]{2,1,0:T(8,128)(2,1)S(1)} %reshape.16, bf16[256,4,1536]{2,0,1:T(8,128)(2,1)S(1)} %bitcast.56), kind=kOutput, calls=%fused_computation.8 | convolution fusion | flops 201326592 | bytes 3997696 | tf_op jit(solution)/shard_map/dot_general | solution.py:67
  55.9 2.7 %collective-permute-start.5 = (bf16[4,32,1536]{2,1,0:T(8,128)(2,1)S(1)}, bf16[4,32,1536]{2,1,0:T(8,128)(2,1)S(1)}, u32[]{:S(2)}, u32[]{:S(2)}) collective-permute-start(bf16[4,32,1536]{2,1,0:T(8,128)(2,1)S(1)} %slice.17), channel_id=1, source_target_pairs={{0,192},{64,0},{128,64},{192,128},{1,193},{65,1},{129,65},{193,129... | collective-permute-start | bytes 1179656 | tf_op jit(solution)/shard_map/ppermute | solution.py:15
  58.6 1.1 %fusion.1 = f32[64,256]{1,0:T(8,128)S(1)} fusion(f32[64,256]{1,0:T(8,128)S(1)} %convolution_bitcast_fusion.2, bf16[4,64,1536]{2,1,0:T(8,128)(2,1)S(1)} %collective-permute-done.1, bf16[256,4,1536]{2,0,1:T(8,128)(2,1)S(1)} %bitcast.58), kind=kOutput, calls=%fused_computation.7 | convolution fusion | flops 201342976 | bytes 4063232 | tf_op jit(solution)/shard_map/dot_general | solution.py:67
  59.7 1.1 %fusion = f32[64,256]{1,0:T(8,128)S(1)} fusion(f32[64,256]{1,0:T(8,128)S(1)} %fusion.1, bf16[4,64,1536]{2,1,0:T(8,128)(2,1)S(1)} %collective-permute-done.2, bf16[256,4,1536]{2,0,1:T(8,128)(2,1)S(1)} %bitcast.57), kind=kOutput, calls=%fused_computation.5 | convolution fusion | flops 201342976 | bytes 4063232 | tf_op jit(solution)/shard_map/dot_general | solution.py:67
  60.8 5.7 %collective-permute-start.3 = (f32[64,256]{1,0:T(8,128)S(1)}, f32[64,256]{1,0:T(8,128)S(1)}, u32[]{:S(2)}, u32[]{:S(2)}) collective-permute-start(f32[64,256]{1,0:T(8,128)S(1)} %fusion), channel_id=1, source_target_pairs={{0,1},{1,0},{2,3},{3,2},{4,5},{5,4},{6,7},{7,6},{8,9},{9,8},{10,11... | collective-permute-start | bytes 196616 | tf_op jit(solution)/shard_map/ppermute | solution.py:15
  67.5 1.1 %fusion.6 = f32[64,256,1]{1,0,2:T(8,128)S(1)} fusion(bf16[4,64,1536]{2,1,0:T(8,128)(2,1)S(1)} %pad_maximum_fusion, bf16[256,4,1536]{2,0,1:T(8,128)(2,1)S(1)} %bitcast.55), kind=kOutput, calls=%fused_computation.23 | convolution fusion | flops 201326592 | bytes 3997696 | tf_op jit(solution)/shard_map/dot_general | solution.py:67
  68.6 5.8 %collective-permute-start.7 = (f32[2,64,256]{2,1,0:T(8,128)S(1)}, f32[2,64,256]{2,1,0:T(8,128)S(1)}, u32[]{:S(2)}, u32[]{:S(2)}) collective-permute-start(f32[2,64,256]{2,1,0:T(8,128)S(1)} %pad_maximum_fusion.1), channel_id=1, source_target_pairs={{0,2},{2,0},{1,3},{3,1},{4,6},{6,4},{5,7},{7,5},{8,10},{10,8},{9,1... | collective-permute-start | bytes 393224 | tf_op jit(solution)/shard_map/ppermute | solution.py:15
  74.3 3.2 %collective-permute-start.6 = (f32[64,256]{1,0:T(8,128)S(1)}, f32[64,256]{1,0:T(8,128)S(1)}, u32[]{:S(2)}, u32[]{:S(2)}) collective-permute-start(f32[64,256]{1,0:T(8,128)S(1)} %bitcast.61), channel_id=1, source_target_pairs={{0,1},{1,0},{2,3},{3,2},{4,5},{5,4},{6,7},{7,6},{8,9},{9,8},{10,11... | collective-permute-start | bytes 196616 | tf_op jit(solution)/shard_map/ppermute | solution.py:15
  77.6 0.9 %collective-permute-done.6 = f32[64,256]{1,0:T(8,128)S(1)} collective-permute-done((f32[64,256]{1,0:T(8,128)S(1)}, f32[64,256]{1,0:T(8,128)S(1)}, u32[]{:S(2)}, u32[]{:S(2)}) %collective-permute-start.6) | collective-permute-done | bytes 65568 | tf_op jit(solution)/shard_map/ppermute | solution.py:15
  78.5 4.3 %collective-permute-done.8 = f32[64,256]{1,0:T(8,128)S(1)} collective-permute-done((f32[64,256]{1,0:T(8,128)S(1)}, f32[64,256]{1,0:T(8,128)S(1)}, u32[]{:S(2)}, u32[]{:S(2)}) %collective-permute-start.8) | collective-permute-done | bytes 65568 | tf_op jit(solution)/shard_map/ppermute | solution.py:83
  82.8 0.7 fusion.5
  (17 shorter events, 2.1 us)
Async XLA Ops:
  1.7 6.7 %collective-permute-start = (bf16[64,384]{1,0:T(8,128)(2,1)S(1)}, bf16[64,384]{1,0:T(8,128)(2,1)S(1)}, u32[]{:S(2)}, u32[]{:S(2)}) collective-permute-start(bf16[64,384]{1,0:T(8,128)(2,1)S(1)} %fusion.2), channel_id=1, source_target_pairs={{0,0},{1,4},{2,8},{3,12},{4,1},{5,5},{6,9},{7,13},{8,2},{9,6},{10,... | collective-permute-start | bytes 147464 | tf_op jit(solution)/shard_map/ppermute | solution.py:54
  9.4 28.1 %all-to-all-start = ((bf16[16,64,384]{2,1,0:T(8,128)(2,1)}), bf16[16,64,384]{2,1,0:T(8,128)(2,1)S(1)}, u32[]{:S(2)}, u32[]{:S(2)}) async-start(bf16[16,64,384]{2,1,0:T(8,128)(2,1)} %broadcast_in_dim.2), calls=%async_computation | async-start | bytes 1572864 | tf_op jit(solution)/shard_map/all_to_all | solution.py:56
  38.4 17.3 %collective-permute-start.1 = (bf16[4,64,1536]{2,1,0:T(8,128)(2,1)S(1)}, bf16[4,64,1536]{2,1,0:T(8,128)(2,1)S(1)}, u32[]{:S(2)}, u32[]{:S(2)}) collective-permute-start(bf16[4,64,1536]{2,1,0:T(8,128)(2,1)S(1)} %reshape.16), channel_id=1, source_target_pairs={{0,64},{64,128},{128,192},{192,0},{1,65},{65,129},{129,193},{193,1... | collective-permute-start | bytes 2359304 | tf_op jit(solution)/shard_map/ppermute | solution.py:15
  39.8 15.9 %collective-permute-start.2 = (bf16[4,64,1536]{2,1,0:T(8,128)(2,1)S(1)}, bf16[4,64,1536]{2,1,0:T(8,128)(2,1)S(1)}, u32[]{:S(2)}, u32[]{:S(2)}) collective-permute-start(bf16[4,64,1536]{2,1,0:T(8,128)(2,1)S(1)} %reshape.16), channel_id=1, source_target_pairs={{0,192},{64,0},{128,64},{192,128},{1,193},{65,1},{129,65},{193,129... | collective-permute-start | bytes 2359304 | tf_op jit(solution)/shard_map/ppermute | solution.py:15
  55.8 11.6 %collective-permute-start.4 = (bf16[4,32,1536]{2,1,0:T(8,128)(2,1)S(1)}, bf16[4,32,1536]{2,1,0:T(8,128)(2,1)S(1)}, u32[]{:S(2)}, u32[]{:S(2)}) collective-permute-start(bf16[4,32,1536]{2,1,0:T(8,128)(2,1)S(1)} %slice.16), channel_id=1, source_target_pairs={{0,64},{64,128},{128,192},{192,0},{1,65},{65,129},{129,193},{193,1... | collective-permute-start | bytes 1179656 | tf_op jit(solution)/shard_map/ppermute | solution.py:15
  55.9 11.5 %collective-permute-start.5 = (bf16[4,32,1536]{2,1,0:T(8,128)(2,1)S(1)}, bf16[4,32,1536]{2,1,0:T(8,128)(2,1)S(1)}, u32[]{:S(2)}, u32[]{:S(2)}) collective-permute-start(bf16[4,32,1536]{2,1,0:T(8,128)(2,1)S(1)} %slice.17), channel_id=1, source_target_pairs={{0,192},{64,0},{128,64},{192,128},{1,193},{65,1},{129,65},{193,129... | collective-permute-start | bytes 1179656 | tf_op jit(solution)/shard_map/ppermute | solution.py:15
  60.8 6.6 %collective-permute-start.3 = (f32[64,256]{1,0:T(8,128)S(1)}, f32[64,256]{1,0:T(8,128)S(1)}, u32[]{:S(2)}, u32[]{:S(2)}) collective-permute-start(f32[64,256]{1,0:T(8,128)S(1)} %fusion), channel_id=1, source_target_pairs={{0,1},{1,0},{2,3},{3,2},{4,5},{5,4},{6,7},{7,6},{8,9},{9,8},{10,11... | collective-permute-start | bytes 196616 | tf_op jit(solution)/shard_map/ppermute | solution.py:15
  68.6 14.2 %collective-permute-start.7 = (f32[2,64,256]{2,1,0:T(8,128)S(1)}, f32[2,64,256]{2,1,0:T(8,128)S(1)}, u32[]{:S(2)}, u32[]{:S(2)}) collective-permute-start(f32[2,64,256]{2,1,0:T(8,128)S(1)} %pad_maximum_fusion.1), channel_id=1, source_target_pairs={{0,2},{2,0},{1,3},{3,1},{4,6},{6,4},{5,7},{7,5},{8,10},{10,8},{9,1... | collective-permute-start | bytes 393224 | tf_op jit(solution)/shard_map/ppermute | solution.py:15
  74.3 4.1 %collective-permute-start.6 = (f32[64,256]{1,0:T(8,128)S(1)}, f32[64,256]{1,0:T(8,128)S(1)}, u32[]{:S(2)}, u32[]{:S(2)}) collective-permute-start(f32[64,256]{1,0:T(8,128)S(1)} %bitcast.61), channel_id=1, source_target_pairs={{0,1},{1,0},{2,3},{3,2},{4,5},{5,4},{6,7},{7,6},{8,9},{9,8},{10,11... | collective-permute-start | bytes 196616 | tf_op jit(solution)/shard_map/ppermute | solution.py:15
  77.6 5.2 %collective-permute-start.8 = (f32[64,256]{1,0:T(8,128)S(1)}, f32[64,256]{1,0:T(8,128)S(1)}, u32[]{:S(2)}, u32[]{:S(2)}) collective-permute-start(f32[64,256]{1,0:T(8,128)S(1)} %bitcast.62), channel_id=1, source_target_pairs={{0,3},{3,0},{1,2},{2,1},{4,7},{7,4},{5,6},{6,5},{8,11},{11,8},{9,1... | collective-permute-start | bytes 196616 | tf_op jit(solution)/shard_map/ppermute | solution.py:83

commit v13 on v11

--- a/solution.py
+++ b/solution.py
@@ -54,18 +54,19 @@
     moved = lax.ppermute(scaled, ("z", "xh", "core"), pairs)
     copies = jnp.broadcast_to(moved[None], (nx * nz,) + moved.shape)
     s2 = lax.all_to_all(copies, ("xl", "z"), 0, 0)
-    s2 = s2.reshape(nx, nz // nt, nt, n_loads, width)
-    own = jnp.transpose(s2, (0, 1, 3, 2, 4)).reshape(nx * nz // nt, n_loads, nt * width)
-    per_y = own.shape[0]
+    own = s2
+    per_y = nx * nz // nt
     cov_local = cov[:, :, 0, :]
     ny = lax.axis_size("y")
     me = lax.axis_index("y")
 
     def term(block, y_from):
         cov_part = lax.dynamic_slice_in_dim(cov_local, (y_from % ny) * per_y, per_y, 1)
+        cov_part = cov_part.reshape(cov_part.shape[0], nx, nz // nt, nt, width)
+        block = block.reshape(nx, nz // nt, nt, block.shape[1], width)
         block, cov_part = lax.optimization_barrier((block, cov_part))
         return lax.dot_general(
-            block, cov_part, (((0, 2), (1, 2)), ((), ())), preferred_element_type=jnp.float32
+            block, cov_part, (((0, 1, 2, 4), (1, 2, 3, 4)), ((), ())), preferred_element_type=jnp.float32
         )
 
     fwd = shifted(own, "y", 1)

time: 81.2 us -> 107 us (1.32)
  local copies, waits for them, and re-layouts: 16.7 us -> 40.9 us
  matrix products: 4.26 us -> 7.32 us
  starting transfers between devices: 36.1 us -> 33.7 us
    unnamed x4 -> x10, local copies, waits for them, and re-layouts: 2.28 us -> 21.8 us
    dynamic_slice x1, local copies, waits for them, and re-layouts: 11.6 us -> 15 us  [term(): lax.dynamic_slice_in_dim(cov_local, y_from % ny * per_y, per_y, 1)]
    dot_general x4, matrix products: 4.26 us -> 7.32 us  [term(): lax.dot_general(block, cov_part, (((0, 1, 2, 4), (1, 2, 3, 4)), ((), ()))...]
    ppermute x7, starting transfers between devices: 20.5 us -> 18 us  [shifted(): return lax.ppermute(x, axis, [(i, (i + by) % n) for i in range(n)])]
    slice x1, local copies, waits for them, and re-layouts: 0.03 us -> 1.19 us  [per_device(): far_a = shifted(fwd[:, :half], 'y', 1)]
  transfers between devices with their start and end apart: 9 -> 9, of which waited for: 4 -> 4; matrix products, arithmetic and copies ran while one was open for 23% -> 44% of each run, Pallas kernels for 0% -> 0%
where the time goes in v13:
time: 107 us; the launch traced here: 106 us
  local copies, waits for them, and re-layouts  40.9 us (38%)
  starting transfers between devices  33.7 us (31%)
  waiting for transfers between devices  22.3 us (21%)
  matrix products  7.32 us (7%)
  other arithmetic  1.59 us (1%)
    unnamed x10, local copies, waits for them, and re-layouts  21.8 us
    ppermute x7, starting transfers between devices, shifted(): return lax.ppermute(x, axis, [(i, (i + by) % n) for i in range(n)])  18 us
    all_to_all x1, waiting for transfers between devices, per_device(): s2 = lax.all_to_all(copies, ('xl', 'z'), 0, 0)  17.4 us
    dynamic_slice x1, local copies, waits for them, and re-layouts, term(): lax.dynamic_slice_in_dim(cov_local, y_from % ny * per_y, per_y, 1)  15 us
    all_to_all x1, starting transfers between devices, per_device(): s2 = lax.all_to_all(copies, ('xl', 'z'), 0, 0)  10.7 us
    dot_general x4, matrix products, term(): lax.dot_general(block, cov_part, (((0, 1, 2, 4), (1, 2, 3, 4)), ((), ()))...  7.32 us
    ppermute x1, starting transfers between devices, per_device(): moved = lax.ppermute(scaled, ('z', 'xh', 'core'), pairs)  4.94 us
    ppermute x7, waiting for transfers between devices, shifted(): return lax.ppermute(x, axis, [(i, (i + by) % n) for i in range(n)])  3.09 us
  transfers between devices with their start and end apart: 9, of which 4 were waited for; matrix products, arithmetic and copies ran while one was open for 44% of the time, Pallas kernels for 0%

profile of v13, /device:TPU:1, one launch (start us, length us, event | category | flops | bytes accessed | tf_op | source)
XLA Modules:
  0.0 106.0 jit_solution(205312218682078471)
XLA Ops:
  0.9 0.8 fusion.2
  1.7 4.9 %collective-permute-start = (bf16[64,384]{1,0:T(8,128)(2,1)S(1)}, bf16[64,384]{1,0:T(8,128)(2,1)S(1)}, u32[]{:S(2)}, u32[]{:S(2)}) collective-permute-start(bf16[64,384]{1,0:T(8,128)(2,1)S(1)} %fusion.2), channel_id=1, source_target_pairs={{0,0},{1,4},{2,8},{3,12},{4,1},{5,5},{6,9},{7,13},{8,2},{9,6},{10,... | collective-permute-start | bytes 147464 | tf_op jit(solution)/shard_map/ppermute | solution.py:54
  6.7 1.8 %collective-permute-done = bf16[64,384]{1,0:T(8,128)(2,1)S(1)} collective-permute-done((bf16[64,384]{1,0:T(8,128)(2,1)S(1)}, bf16[64,384]{1,0:T(8,128)(2,1)S(1)}, u32[]{:S(2)}, u32[]{:S(2)}) %collective-permute-start) | collective-permute-done | bytes 49184 | tf_op jit(solution)/shard_map/ppermute | solution.py:54
  8.4 1.0 broadcast_in_dim.2
  9.4 10.7 %all-to-all-start = ((bf16[16,64,384]{2,1,0:T(8,128)(2,1)}), bf16[16,64,384]{2,1,0:T(8,128)(2,1)}, u32[]{:S(2)}, u32[]{:S(2)}) async-start(bf16[16,64,384]{2,1,0:T(8,128)(2,1)} %broadcast_in_dim.2), calls=%async_computation | async-start | bytes 1572864 | tf_op jit(solution)/shard_map/all_to_all | solution.py:56
  20.2 17.4 %all-to-all-done = bf16[16,64,384]{2,1,0:T(8,128)(2,1)} async-done(((bf16[16,64,384]{2,1,0:T(8,128)(2,1)}), bf16[16,64,384]{2,1,0:T(8,128)(2,1)}, u32[]{:S(2)}, u32[]{:S(2)}) %all-to-all-start) | async-done | bytes 786464 | tf_op jit(solution)/shard_map/all_to_all | solution.py:56
  37.6 1.3 %collective-permute-start.1 = (bf16[16,64,384]{2,1,0:T(8,128)(2,1)}, bf16[16,64,384]{2,1,0:T(8,128)(2,1)}, u32[]{:S(2)}, u32[]{:S(2)}) collective-permute-start(bf16[16,64,384]{2,1,0:T(8,128)(2,1)} %all-to-all-done), channel_id=1, source_target_pairs={{0,64},{64,128},{128,192},{192,0},{1,65},{65,129},{129,193},{193,1... | collective-permute-start | bytes 2359304 | tf_op jit(solution)/shard_map/ppermute | solution.py:15
  38.9 1.4 %collective-permute-start.2 = (bf16[16,64,384]{2,1,0:T(8,128)(2,1)}, bf16[16,64,384]{2,1,0:T(8,128)(2,1)}, u32[]{:S(2)}, u32[]{:S(2)}) collective-permute-start(bf16[16,64,384]{2,1,0:T(8,128)(2,1)} %all-to-all-done), channel_id=1, source_target_pairs={{0,192},{64,0},{128,64},{192,128},{1,193},{65,1},{129,65},{193,129... | collective-permute-start | bytes 2359304 | tf_op jit(solution)/shard_map/ppermute | solution.py:15
  40.4 15.0 %constant_dynamic-slice_fusion.1 = (bf16[256,4,1,1536]{3,1,2,0:T(4,128)(2,1)}, bf16[256,4,1,1536]{3,1,2,0:T(4,128)(2,1)}, bf16[256,4,1,1536]{3,1,2,0:T(4,128)(2,1)}, bf16[256,4,1,1536]{3,1,2,0:T(4,128)(2,1)S(1)}) fusion(bf16[256,16,1,1536]{3,1,2,0:T(8,128)(2,1)} %param.5, s32[]{:T(128)S(6)} %select_n.36, s32[]{:T(128)S(6)} %select_n.34, s32[]{:T(128)S(6)} %select_n.32, ...), kind=kLoop, calls=%fused_computation.11 | loop fusion | bytes 25165840 | tf_op jit(solution)/shard_map/dynamic_slice | solution.py:64
  55.4 5.9 %copy.22 = bf16[256,4,1,1536]{0,3,1,2:T(8,128)(2,1)} copy(bf16[256,4,1,1536]{3,1,2,0:T(4,128)(2,1)} %get-tuple-element.23) | data formatting | bytes 6291456
  61.3 6.0 %copy.23 = bf16[256,4,1,1536]{0,3,1,2:T(8,128)(2,1)} copy(bf16[256,4,1,1536]{3,1,2,0:T(4,128)(2,1)} %get-tuple-element.22) | data formatting | bytes 6291456
  67.3 5.9 %copy.24 = bf16[256,4,1,1536]{0,3,1,2:T(8,128)(2,1)} copy(bf16[256,4,1,1536]{3,1,2,0:T(4,128)(2,1)} %get-tuple-element.21) | data formatting | bytes 6291456
  73.2 3.9 %copy.25 = bf16[256,4,1,1536]{0,3,1,2:T(8,128)(2,1)} copy(bf16[256,4,1,1536]{3,1,2,0:T(4,128)(2,1)S(1)} %get-tuple-element.24) | data formatting | bytes 6291456
  77.2 2.9 %convolution_bitcast_fusion.3 = f32[64,256]{1,0:T(8,128)S(1)} fusion(bf16[2,2,4,64,384]{4,3,2,1,0:T(8,128)(2,1)} %bitcast, bf16[256,2,2,4,384]{0,4,3,2,1:T(8,128)(2,1)} %bitcast.42), kind=kOutput, calls=%fused_computation.5 | convolution fusion | flops 201326592 | bytes 3997696 | tf_op jit(solution)/shard_map/dot_general | solution.py:68
  80.1 1.2 %slice.8 = bf16[16,32,384]{2,1,0:T(8,128)(2,1)S(1)} slice(bf16[16,64,384]{2,1,0:T(8,128)(2,1)} %collective-permute-done.1), slice={[0:16], [0:32], [0:384]} | slice | bytes 786432 | tf_op jit(solution)/shard_map/slice | solution.py:78
  81.4 1.0 slice.9
  82.5 2.7 %collective-permute-start.5 = (bf16[16,32,384]{2,1,0:T(8,128)(2,1)S(1)}, bf16[16,32,384]{2,1,0:T(8,128)(2,1)S(1)}, u32[]{:S(2)}, u32[]{:S(2)}) collective-permute-start(bf16[16,32,384]{2,1,0:T(8,128)(2,1)S(1)} %slice.9), channel_id=1, source_target_pairs={{0,192},{64,0},{128,64},{192,128},{1,193},{65,1},{129,65},{193,129... | collective-permute-start | bytes 1179656 | tf_op jit(solution)/shard_map/ppermute | solution.py:15
  85.2 1.8 %fusion.1 = f32[64,256]{1,0:T(8,128)S(1)} fusion(f32[64,256]{1,0:T(8,128)S(1)} %convolution_bitcast_fusion.3, bf16[2,2,4,64,384]{4,3,2,1,0:T(8,128)(2,1)} %bitcast.4, bf16[256,2,2,4,384]{0,4,3,2,1:T(8,128)(2,1)S(1)} %bitcast.44), kind=kOutput, calls=%fused_computation.4 | convolution fusion | flops 201342976 | bytes 4063232 | tf_op jit(solution)/shard_map/dot_general | solution.py:68
  87.0 1.9 %fusion = f32[64,256]{1,0:T(8,128)S(1)} fusion(f32[64,256]{1,0:T(8,128)S(1)} %fusion.1, bf16[2,2,4,64,384]{4,3,2,1,0:T(8,128)(2,1)} %bitcast.8, bf16[256,2,2,4,384]{0,4,3,2,1:T(8,128)(2,1)S(1)} %bitcast.43), kind=kOutput, calls=%fused_computation.2 | convolution fusion | flops 201342976 | bytes 4063232 | tf_op jit(solution)/shard_map/dot_general | solution.py:68
  89.0 5.8 %collective-permute-start.3 = (f32[64,256]{1,0:T(8,128)S(1)}, f32[64,256]{1,0:T(8,128)S(1)}, u32[]{:S(2)}, u32[]{:S(2)}) collective-permute-start(f32[64,256]{1,0:T(8,128)S(1)} %fusion), channel_id=1, source_target_pairs={{0,1},{1,0},{2,3},{3,2},{4,5},{5,4},{6,7},{7,6},{8,9},{9,8},{10,11... | collective-permute-start | bytes 196616 | tf_op jit(solution)/shard_map/ppermute | solution.py:15
  95.6 1.5 %collective-permute-start.6 = (f32[64,256]{1,0:T(8,128)S(1)}, f32[64,256]{1,0:T(8,128)S(1)}, u32[]{:S(2)}, u32[]{:S(2)}) collective-permute-start(f32[64,256]{1,0:T(8,128)S(1)} %convolution_bitcast_fusion), channel_id=1, source_target_pairs={{0,1},{1,0},{2,3},{3,2},{4,5},{5,4},{6,7},{7,6},{8,9},{9,8},{10,11... | collective-permute-start | bytes 196616 | tf_op jit(solution)/shard_map/ppermute | solution.py:15
  97.1 0.9 collective-permute-done.6
  98.0 5.1 %collective-permute-start.7 = (f32[64,256]{1,0:T(8,128)S(1)}, f32[64,256]{1,0:T(8,128)S(1)}, u32[]{:S(2)}, u32[]{:S(2)}) collective-permute-start(f32[64,256]{1,0:T(8,128)S(1)} %add_add_fusion), channel_id=1, source_target_pairs={{0,2},{2,0},{1,3},{3,1},{4,6},{6,4},{5,7},{7,5},{8,10},{10,8},{9,1... | collective-permute-start | bytes 196616 | tf_op jit(solution)/shard_map/ppermute | solution.py:15
  103.1 2.2 %collective-permute-done.7 = f32[64,256]{1,0:T(8,128)S(1)} collective-permute-done((f32[64,256]{1,0:T(8,128)S(1)}, f32[64,256]{1,0:T(8,128)S(1)}, u32[]{:S(2)}, u32[]{:S(2)}) %collective-permute-start.7) | collective-permute-done | bytes 65568 | tf_op jit(solution)/shard_map/ppermute | solution.py:15
  (18 shorter events, 2.4 us)
Async XLA Ops:
  1.7 6.7 %collective-permute-start = (bf16[64,384]{1,0:T(8,128)(2,1)S(1)}, bf16[64,384]{1,0:T(8,128)(2,1)S(1)}, u32[]{:S(2)}, u32[]{:S(2)}) collective-permute-start(bf16[64,384]{1,0:T(8,128)(2,1)S(1)} %fusion.2), channel_id=1, source_target_pairs={{0,0},{1,4},{2,8},{3,12},{4,1},{5,5},{6,9},{7,13},{8,2},{9,6},{10,... | collective-permute-start | bytes 147464 | tf_op jit(solution)/shard_map/ppermute | solution.py:54
  9.4 28.2 %all-to-all-start = ((bf16[16,64,384]{2,1,0:T(8,128)(2,1)}), bf16[16,64,384]{2,1,0:T(8,128)(2,1)}, u32[]{:S(2)}, u32[]{:S(2)}) async-start(bf16[16,64,384]{2,1,0:T(8,128)(2,1)} %broadcast_in_dim.2), calls=%async_computation | async-start | bytes 1572864 | tf_op jit(solution)/shard_map/all_to_all | solution.py:56
  37.6 42.5 %collective-permute-start.1 = (bf16[16,64,384]{2,1,0:T(8,128)(2,1)}, bf16[16,64,384]{2,1,0:T(8,128)(2,1)}, u32[]{:S(2)}, u32[]{:S(2)}) collective-permute-start(bf16[16,64,384]{2,1,0:T(8,128)(2,1)} %all-to-all-done), channel_id=1, source_target_pairs={{0,64},{64,128},{128,192},{192,0},{1,65},{65,129},{129,193},{193,1... | collective-permute-start | bytes 2359304 | tf_op jit(solution)/shard_map/ppermute | solution.py:15
  38.9 42.5 %collective-permute-start.2 = (bf16[16,64,384]{2,1,0:T(8,128)(2,1)}, bf16[16,64,384]{2,1,0:T(8,128)(2,1)}, u32[]{:S(2)}, u32[]{:S(2)}) collective-permute-start(bf16[16,64,384]{2,1,0:T(8,128)(2,1)} %all-to-all-done), channel_id=1, source_target_pairs={{0,192},{64,0},{128,64},{192,128},{1,193},{65,1},{129,65},{193,129... | collective-permute-start | bytes 2359304 | tf_op jit(solution)/shard_map/ppermute | solution.py:15
  77.2 8.0 %copy-start.2 = (bf16[256,4,1,1536]{0,3,1,2:T(8,128)(2,1)S(1)}, bf16[256,4,1,1536]{0,3,1,2:T(8,128)(2,1)}, u32[]{:S(2)}) copy-start(bf16[256,4,1,1536]{0,3,1,2:T(8,128)(2,1)} %copy.23) | copy-start | bytes 9437188
  80.1 6.9 %copy-start.1 = (bf16[256,4,1,1536]{0,3,1,2:T(8,128)(2,1)S(1)}, bf16[256,4,1,1536]{0,3,1,2:T(8,128)(2,1)}, u32[]{:S(2)}) copy-start(bf16[256,4,1,1536]{0,3,1,2:T(8,128)(2,1)} %copy.24) | copy-start | bytes 9437188
  81.3 13.5 %collective-permute-start.4 = (bf16[16,32,384]{2,1,0:T(8,128)(2,1)S(1)}, bf16[16,32,384]{2,1,0:T(8,128)(2,1)S(1)}, u32[]{:S(2)}, u32[]{:S(2)}) collective-permute-start(bf16[16,32,384]{2,1,0:T(8,128)(2,1)S(1)} %slice.8), channel_id=1, source_target_pairs={{0,64},{64,128},{128,192},{192,0},{1,65},{65,129},{129,193},{193,1... | collective-permute-start | bytes 1179656 | tf_op jit(solution)/shard_map/ppermute | solution.py:15
  82.5 12.3 %collective-permute-start.5 = (bf16[16,32,384]{2,1,0:T(8,128)(2,1)S(1)}, bf16[16,32,384]{2,1,0:T(8,128)(2,1)S(1)}, u32[]{:S(2)}, u32[]{:S(2)}) collective-permute-start(bf16[16,32,384]{2,1,0:T(8,128)(2,1)S(1)} %slice.9), channel_id=1, source_target_pairs={{0,192},{64,0},{128,64},{192,128},{1,193},{65,1},{129,65},{193,129... | collective-permute-start | bytes 1179656 | tf_op jit(solution)/shard_map/ppermute | solution.py:15
  87.0 7.9 %copy-start = (bf16[256,4,1,1536]{0,3,1,2:T(8,128)(2,1)S(1)}, bf16[256,4,1,1536]{0,3,1,2:T(8,128)(2,1)}, u32[]{:S(2)}) copy-start(bf16[256,4,1,1536]{0,3,1,2:T(8,128)(2,1)} %copy.25) | copy-start | bytes 9437188
  89.0 8.1 %collective-permute-start.3 = (f32[64,256]{1,0:T(8,128)S(1)}, f32[64,256]{1,0:T(8,128)S(1)}, u32[]{:S(2)}, u32[]{:S(2)}) collective-permute-start(f32[64,256]{1,0:T(8,128)S(1)} %fusion), channel_id=1, source_target_pairs={{0,1},{1,0},{2,3},{3,2},{4,5},{5,4},{6,7},{7,6},{8,9},{9,8},{10,11... | collective-permute-start | bytes 196616 | tf_op jit(solution)/shard_map/ppermute | solution.py:15
  95.6 2.4 %collective-permute-start.6 = (f32[64,256]{1,0:T(8,128)S(1)}, f32[64,256]{1,0:T(8,128)S(1)}, u32[]{:S(2)}, u32[]{:S(2)}) collective-permute-start(f32[64,256]{1,0:T(8,128)S(1)} %convolution_bitcast_fusion), channel_id=1, source_target_pairs={{0,1},{1,0},{2,3},{3,2},{4,5},{5,4},{6,7},{7,6},{8,9},{9,8},{10,11... | collective-permute-start | bytes 196616 | tf_op jit(solution)/shard_map/ppermute | solution.py:15
  98.0 7.3 %collective-permute-start.7 = (f32[64,256]{1,0:T(8,128)S(1)}, f32[64,256]{1,0:T(8,128)S(1)}, u32[]{:S(2)}, u32[]{:S(2)}) collective-permute-start(f32[64,256]{1,0:T(8,128)S(1)} %add_add_fusion), channel_id=1, source_target_pairs={{0,2},{2,0},{1,3},{3,1},{4,6},{6,4},{5,7},{7,5},{8,10},{10,8},{9,1... | collective-permute-start | bytes 196616 | tf_op jit(solution)/shard_map/ppermute | solution.py:15
